TPU v7x, 128 devices: a whole 4x4x4 slice. The times are simulated.
128 devices in a mesh: scen: 8 (over y, x_lo), gx: 4 (over x_hi, core), gy: 4 (over z).
Axes of the slice: x: 4 (x_hi: 2, x_lo: 2; x = x_hi * 2 + x_lo), y: 4, z: 4, core: 2. Of those that a mesh axis runs over, the one named last changes fastest.
Arguments:
- source: float32 [8, 32, 1024, 1024], P('scen', None, 'gx', 'gy'), may hold values from 0.2 to 3
- obstacle: int32 [32, 1024, 1024], P(None, 'gx', 'gy'), may hold values 0 or 1
- sector: int32 [8], P('scen'), may hold values from 0 to 15
- freq_class: int32 [8], P('scen'), may hold values from 0 to 4
Outputs:
- risk: float32 [16, 1024, 1024], P('scen', 'gx', 'gy')
All inputs are finite; a program needn't handle non-finite values. No bound on the sum of `obstacle` on one device may be relied on, other than what follows from the above.
Results may differ from a plain program's by a relative error of at most 0.00002.
Values sent between devices are 32-bit elements; how exact they have to be, the bound alone decides.
No kernel may reach another device: no remote copies, remote signals or barrier semaphores. Data moves between devices by JAX's collectives and lax.ppermute only.
A program may use at most 256 MiB of HBM per device.

v0:
```python
import math

import jax
import jax.numpy as jnp
from jax import lax
from jax.sharding import PartitionSpec as P

STEPS = 4
RZ = 16


wind_speed = 0.4
diffusion = 0.05
settling = 0.1
probit_a = 3.0
probit_b = 1.0
load_eps = 0.01
freq_rate = 0.7


def with_halo(block, sides, width):
    for axis, dim in sides:
        count = lax.axis_size(axis)
        forward = [(i, i + 1) for i in range(count - 1)]
        backward = [(target, source) for source, target in forward]
        low = lax.ppermute(
            lax.slice_in_dim(block, block.shape[dim] - width, None, axis=dim), axis, forward
        )
        high = lax.ppermute(lax.slice_in_dim(block, 0, width, axis=dim), axis, backward)
        block = jnp.concatenate([low, block, high], axis=dim)
    return block


def wind_components(sector_id):
    heading = sector_id.astype(jnp.float32) * (2.0 * math.pi / 16.0)
    return (wind_speed * jnp.cos(heading), wind_speed * jnp.sin(heading))


def advance(padded, open_cells, courant_x, courant_y):
    centre = padded[:, 1:-1, 1:-1]
    west_side = padded[:, :-2, 1:-1]
    east_side = padded[:, 2:, 1:-1]
    south_side = padded[:, 1:-1, :-2]
    north_side = padded[:, 1:-1, 2:]
    zero_plane = jnp.zeros_like(centre[:1])
    upper_cell = jnp.concatenate([centre[1:], zero_plane], 0)
    lower_cell = jnp.concatenate([centre[:1], centre[:-1]], 0)
    falling = jnp.concatenate([zero_plane, centre[1:]], 0)
    advect = jnp.maximum(courant_x, 0.0) * (centre - west_side) + jnp.minimum(courant_x, 0.0) * (
        east_side - centre
    )
    advect = (
        advect
        + jnp.maximum(courant_y, 0.0) * (centre - south_side)
        + jnp.minimum(courant_y, 0.0) * (north_side - centre)
    )
    spread = (
        west_side + east_side + south_side + north_side + upper_cell + lower_cell - 6.0 * centre
    )
    return (centre - advect + diffusion * spread + settling * (upper_cell - falling)) * open_cells


def lethality(toxic_load):
    probit = probit_a + probit_b * jnp.log(toxic_load + load_eps)
    return 0.5 * (1.0 + lax.erf((probit - 5.0) / math.sqrt(2.0)))


def on_device(source, obstacle, sector, freq_class):
    open_cells = (1 - obstacle).astype(jnp.float32)
    courant_x, courant_y = wind_components(sector[0])
    weight = jnp.exp(-freq_rate * freq_class[0].astype(jnp.float32))
    current = source[0] * open_cells
    toxic_load = jnp.zeros_like(current)
    for step_index in range(STEPS):
        padded = with_halo(current, (("gx", 1), ("gy", 2)), 1)
        current = advance(padded, open_cells, courant_x, courant_y)
        toxic_load = toxic_load + current * current
    weighted = weight * lethality(toxic_load[:RZ])
    summed = lax.psum(weighted, "scen")
    share = RZ // lax.axis_size("scen")
    return lax.dynamic_slice_in_dim(summed, lax.axis_index("scen") * share, share, 0)


def solution(mesh):
    in_specs = (P("scen", None, "gx", "gy"), P(None, "gx", "gy"), P("scen"), P("scen"))
    out_specs = P("scen", "gx", "gy")
    return jax.shard_map(
        on_device, mesh=mesh, in_specs=in_specs, out_specs=out_specs, check_vma=False
    )
```

profile of v0, /device:TPU:1, one launch (start us, length us, event | category | flops | bytes accessed | tf_op | source)
XLA Modules:
  0.0 627.8 jit_solution(8884289977543023363)
XLA Ops:
  6.5 16.5 %bitcast_multiply_fusion = f32[32,256,256]{2,0,1:T(8,128)S(1)} fusion(f32[1,32,256,256]{3,2,1,0:T(8,128)} %param.4, s32[32,256,256]{2,1,0:T(8,128)} %param.5), kind=kLoop, calls=%fused_computation.103 | loop fusion | flops 6291456 | bytes 25165824 | tf_op jit(solution)/shard_map/mul | solution.py:72
  23.0 6.0 collective-permute-start
  31.0 4.8 collective-permute-done.1
  36.7 5.0 fusion.83
  54.2 13.4 %fusion.90 = (f32[31,256,256]{2,0,1:T(8,128)}, f32[31,256,256]{2,0,1:T(8,128)}) fusion(f32[32,256,256]{2,0,1:T(8,128)} %copy-done), kind=kLoop, calls=%fused_computation.136 | loop fusion | bytes 32505856 | tf_op jit(solution)/shard_map/slice | solution.py:46
  78.0 39.9 %fusion.59 = f32[32,256,256]{2,0,1:T(8,128)} fusion(f32[32,1,256]{2,0,1:T(8,128)S(1)} %collective-permute-done.1, f32[32,256,256]{2,0,1:T(8,128)} %copy-done, f32[32,1,256]{2,0,1:T(8,128)S(1)} %collective-permute-done, f32[31,256,256]{2,0,1:T(8,128)} %get-tuple-element.26, f32[1,256,256]{2,0,1:T(1,128)S(1)} %slice.205, ...), kind=kLoop, calls=%fused_computation.94 | loop fusion | flops 75497472 | bytes 41812496 | tf_op jit(solution)/shard_map/mul | solution.py:60
  123.0 4.6 collective-permute-done.5
  131.6 4.8 fusion.82
  140.2 4.7 collective-permute-start.6
  149.9 13.5 %fusion.88 = (f32[31,256,256]{2,0,1:T(8,128)}, f32[31,256,256]{2,0,1:T(8,128)}) fusion(f32[32,256,256]{2,0,1:T(8,128)} %fusion.59), kind=kLoop, calls=%fused_computation.134 | loop fusion | bytes 32505856 | tf_op jit(solution)/shard_map/slice | solution.py:46
  172.9 39.3 %fusion.41 = f32[32,256,256]{2,0,1:T(8,128)} fusion(f32[32,1,256]{2,0,1:T(8,128)S(1)} %collective-permute-done.5, f32[32,256,256]{2,0,1:T(8,128)} %fusion.59, f32[32,1,256]{2,0,1:T(8,128)S(1)} %collective-permute-done.4, f32[31,256,256]{2,0,1:T(8,128)} %get-tuple-element.22, f32[1,256,256]{2,0,1:T(1,128)S(1)} %slice.212, ...), kind=kLoop, calls=%fused_computation.68 | loop fusion | flops 75497472 | bytes 41812496 | tf_op jit(solution)/shard_map/mul | solution.py:60
  217.5 4.4 collective-permute-done.9
  225.9 4.8 fusion.81
  234.5 4.3 collective-permute-start.10
  243.8 13.4 %fusion.86 = (f32[31,256,256]{2,0,1:T(8,128)}, f32[31,256,256]{2,0,1:T(8,128)}) fusion(f32[32,256,256]{2,0,1:T(8,128)} %fusion.41), kind=kLoop, calls=%fused_computation.132 | loop fusion | bytes 32505856 | tf_op jit(solution)/shard_map/slice | solution.py:46
  266.6 40.3 %fusion.23 = f32[32,256,256]{2,0,1:T(8,128)} fusion(f32[32,1,256]{2,0,1:T(8,128)S(1)} %collective-permute-done.9, f32[32,256,256]{2,0,1:T(8,128)} %fusion.41, f32[32,1,256]{2,0,1:T(8,128)S(1)} %collective-permute-done.8, f32[31,256,256]{2,0,1:T(8,128)} %get-tuple-element.18, f32[1,256,256]{2,0,1:T(1,128)S(1)} %slice.219, ...), kind=kLoop, calls=%fused_computation.42 | loop fusion | flops 75497472 | bytes 41812496 | tf_op jit(solution)/shard_map/mul | solution.py:60
  312.6 11.7 %fusion.67 = f32[32,256,256]{2,0,1:T(8,128)} fusion(s32[32,256,256]{2,1,0:T(8,128)} %param.5), kind=kLoop, calls=%fused_computation.105 | loop fusion | flops 4194304 | bytes 16777216 | tf_op jit(solution)/shard_map/convert_element_type | solution.py:69
  326.9 4.9 fusion.80
  335.5 4.2 collective-permute-start.14
  345.0 13.4 %fusion.84 = (f32[31,256,256]{2,0,1:T(8,128)}, f32[31,256,256]{2,0,1:T(8,128)}) fusion(f32[32,256,256]{2,0,1:T(8,128)} %fusion.23), kind=kLoop, calls=%fused_computation.130 | loop fusion | bytes 32505856 | tf_op jit(solution)/shard_map/slice | solution.py:47
  367.9 23.8 %fusion.10 = f32[32,256,256]{2,0,1:T(8,128)} fusion(f32[32,256,256]{2,0,1:T(8,128)} %fusion.23, f32[32,1,256]{2,0,1:T(8,128)S(1)} %collective-permute-done.13, f32[32,1,256]{2,0,1:T(8,128)S(1)} %collective-permute-done.12, f32[32,258,1]{2,0,1:T(8,128)} %copy.23, f32[32,258,1]{2,0,1:T(8,128)} %copy.25, f32[]{:T(128)} %bitcast.4, f32[]{:T(128)} %bitcast.3, ...), kind=kLoop, calls=%fused_computation.21 | loop fusion | flops 39845888 | bytes 16908816 | tf_op jit(solution)/shard_map/add | solution.py:53
  391.8 27.2 %fusion.6 = f32[32,256,256]{2,0,1:T(8,128)} fusion(f32[32,1,256]{2,0,1:T(8,128)S(1)} %collective-permute-done.13, f32[32,256,256]{2,0,1:T(8,128)} %fusion.23, f32[32,1,256]{2,0,1:T(8,128)S(1)} %collective-permute-done.12, f32[31,256,256]{2,0,1:T(8,128)} %get-tuple-element.13, f32[1,256,256]{2,0,1:T(1,128)S(1)} %slice.226, ...), kind=kLoop, calls=%fused_computation.17 | loop fusion | flops 33554432 | bytes 33423872 | tf_op jit(solution)/shard_map/sub | solution.py:58
  419.1 13.3 %add_multiply_fusion = f32[16,256,256]{2,0,1:T(8,128)} fusion(f32[32,256,256]{2,0,1:T(8,128)} %fusion.67, f32[31,256,256]{2,0,1:T(8,128)} %get-tuple-element.14, f32[32,256,256]{2,0,1:T(8,128)} %fusion.6, f32[32,256,256]{2,0,1:T(8,128)} %fusion.10, f32[32,256,256]{2,0,1:T(8,128)S(1)} %bitcast.10, f32[32,256,256]{2,0,1:T(8,128)} %fusion.41, ...), kind=kLoop, calls=%fused_computation.124 | loop fusion | flops 19922944 | bytes 37486596 | tf_op jit(solution)/shard_map/mul | solution.py:78
  432.4 185.5 %all-reduce.10.cloned.1.call-done = f32[16,256,256]{2,0,1:T(8,128)} async-done(((f32[16,256,256]{2,0,1:T(8,128)}), f32[16,256,256]{2,0,1:T(8,128)}) %all-reduce.10.cloned.1.call-update) | async-done | bytes 4194320 | tf_op jit(solution)/shard_map/psum | solution.py:79
  (74 shorter events, 108.2 us)
Async XLA Ops:
  6.5 611.4 %all-reduce.10.cloned.1.call-start = ((), (), s32[]{:S(2)}) async-start(), calls=%async_computation | async-start | bytes 8388608 | tf_op jit(solution)/shard_map/psum | solution.py:79
  23.0 12.8 %copy-start = (f32[32,256,256]{2,0,1:T(8,128)}, f32[32,256,256]{2,0,1:T(8,128)S(1)}, u32[]{:S(2)}) copy-start(f32[32,256,256]{2,0,1:T(8,128)S(1)} %bitcast_multiply_fusion) | copy-start | bytes 25165828
  23.0 8.0 %collective-permute-start = (f32[32,1,256]{2,0,1:T(8,128)S(1)}, f32[32,1,256]{2,0,1:T(8,128)S(1)}, u32[]{:S(2)}, u32[]{:S(2)}) collective-permute-start(f32[32,1,256]{2,0,1:T(8,128)S(1)} %get-tuple-element.27), channel_id=1, source_target_pairs={{0,4},{4,8},{8,12},{1,5},{5,9},{9,13},{2,6},{6,10},{10,14},{3,7},{... | collective-permute-start | bytes 98312 | tf_op jit(solution)/shard_map/ppermute | solution.py:26
  29.1 6.7 %collective-permute-start.1 = (f32[32,1,256]{2,0,1:T(8,128)S(1)}, f32[32,1,256]{2,0,1:T(8,128)S(1)}, u32[]{:S(2)}, u32[]{:S(2)}) collective-permute-start(f32[32,1,256]{2,0,1:T(8,128)S(1)} %get-tuple-element.28), channel_id=1, source_target_pairs={{4,0},{8,4},{12,8},{5,1},{9,5},{13,9},{6,2},{10,6},{14,10},{7,3},{... | collective-permute-start | bytes 98312 | tf_op jit(solution)/shard_map/ppermute | solution.py:29
  45.4 24.7 %collective-permute-start.2 = (f32[32,258,1]{1,0,2:T(8,128)S(1)}, f32[32,258,1]{1,0,2:T(8,128)S(1)}, u32[]{:S(2)}, u32[]{:S(2)}) collective-permute-start(f32[32,258,1]{1,0,2:T(8,128)S(1)} %copy.10), channel_id=1, source_target_pairs={{0,1},{1,2},{2,3},{4,5},{5,6},{6,7},{8,9},{9,10},{10,11},{12,13},{... | collective-permute-start | bytes 99080 | tf_op jit(solution)/shard_map/ppermute | solution.py:26
  52.7 21.4 %collective-permute-start.3 = (f32[32,258,1]{1,0,2:T(8,128)S(1)}, f32[32,258,1]{1,0,2:T(8,128)S(1)}, u32[]{:S(2)}, u32[]{:S(2)}) collective-permute-start(f32[32,258,1]{1,0,2:T(8,128)S(1)} %copy.12), channel_id=1, source_target_pairs={{1,0},{2,1},{3,2},{5,4},{6,5},{7,6},{9,8},{10,9},{11,10},{13,12},{... | collective-permute-start | bytes 99080 | tf_op jit(solution)/shard_map/ppermute | solution.py:29
  118.7 4.3 collective-permute-start.4
  120.9 6.7 %collective-permute-start.5 = (f32[32,1,256]{2,0,1:T(8,128)S(1)}, f32[32,1,256]{2,0,1:T(8,128)S(1)}, u32[]{:S(2)}, u32[]{:S(2)}) collective-permute-start(f32[32,1,256]{2,0,1:T(8,128)S(1)} %get-tuple-element.24), channel_id=1, source_target_pairs={{4,0},{8,4},{12,8},{5,1},{9,5},{13,9},{6,2},{10,6},{14,10},{7,3},{... | collective-permute-start | bytes 98312 | tf_op jit(solution)/shard_map/ppermute | solution.py:29
  140.2 24.9 %collective-permute-start.6 = (f32[32,258,1]{1,0,2:T(8,128)S(1)}, f32[32,258,1]{1,0,2:T(8,128)S(1)}, u32[]{:S(2)}, u32[]{:S(2)}) collective-permute-start(f32[32,258,1]{1,0,2:T(8,128)S(1)} %copy.14), channel_id=1, source_target_pairs={{0,1},{1,2},{2,3},{4,5},{5,6},{6,7},{8,9},{9,10},{10,11},{12,13},{... | collective-permute-start | bytes 99080 | tf_op jit(solution)/shard_map/ppermute | solution.py:26
  148.6 20.4 %collective-permute-start.7 = (f32[32,258,1]{1,0,2:T(8,128)S(1)}, f32[32,258,1]{1,0,2:T(8,128)S(1)}, u32[]{:S(2)}, u32[]{:S(2)}) collective-permute-start(f32[32,258,1]{1,0,2:T(8,128)S(1)} %copy.16), channel_id=1, source_target_pairs={{1,0},{2,1},{3,2},{5,4},{6,5},{7,6},{9,8},{10,9},{11,10},{13,12},{... | collective-permute-start | bytes 99080 | tf_op jit(solution)/shard_map/ppermute | solution.py:29
  213.0 4.5 collective-permute-start.8
  215.2 6.7 %collective-permute-start.9 = (f32[32,1,256]{2,0,1:T(8,128)S(1)}, f32[32,1,256]{2,0,1:T(8,128)S(1)}, u32[]{:S(2)}, u32[]{:S(2)}) collective-permute-start(f32[32,1,256]{2,0,1:T(8,128)S(1)} %get-tuple-element.20), channel_id=1, source_target_pairs={{4,0},{8,4},{12,8},{5,1},{9,5},{13,9},{6,2},{10,6},{14,10},{7,3},{... | collective-permute-start | bytes 98312 | tf_op jit(solution)/shard_map/ppermute | solution.py:29
  234.5 24.4 %collective-permute-start.10 = (f32[32,258,1]{1,0,2:T(8,128)S(1)}, f32[32,258,1]{1,0,2:T(8,128)S(1)}, u32[]{:S(2)}, u32[]{:S(2)}) collective-permute-start(f32[32,258,1]{1,0,2:T(8,128)S(1)} %copy.18), channel_id=1, source_target_pairs={{0,1},{1,2},{2,3},{4,5},{5,6},{6,7},{8,9},{9,10},{10,11},{12,13},{... | collective-permute-start | bytes 99080 | tf_op jit(solution)/shard_map/ppermute | solution.py:26
  242.5 20.2 %collective-permute-start.11 = (f32[32,258,1]{1,0,2:T(8,128)S(1)}, f32[32,258,1]{1,0,2:T(8,128)S(1)}, u32[]{:S(2)}, u32[]{:S(2)}) collective-permute-start(f32[32,258,1]{1,0,2:T(8,128)S(1)} %copy.20), channel_id=1, source_target_pairs={{1,0},{2,1},{3,2},{5,4},{6,5},{7,6},{9,8},{10,9},{11,10},{13,12},{... | collective-permute-start | bytes 99080 | tf_op jit(solution)/shard_map/ppermute | solution.py:29
  307.7 17.4 %collective-permute-start.12 = (f32[32,1,256]{2,0,1:T(8,128)S(1)}, f32[32,1,256]{2,0,1:T(8,128)S(1)}, u32[]{:S(2)}, u32[]{:S(2)}) collective-permute-start(f32[32,1,256]{2,0,1:T(8,128)S(1)} %get-tuple-element.15), channel_id=1, source_target_pairs={{0,4},{4,8},{8,12},{1,5},{5,9},{9,13},{2,6},{6,10},{10,14},{3,7},{... | collective-permute-start | bytes 98312 | tf_op jit(solution)/shard_map/ppermute | solution.py:26
  309.9 15.2 %slice-start = ((s8[8388608]{0:T(1024)(128)(4,1)}), s8[4194304]{0:T(1024)(128)(4,1)S(1)}, s32[]{:S(2)}) async-start(s8[8388608]{0:T(1024)(128)(4,1)} %bitcast.7), calls=%async_computation.1 | async-start | bytes 8388608
  309.9 15.2 %slice-start.1 = ((s8[8388608]{0:T(1024)(128)(4,1)}), s8[4194304]{0:T(1024)(128)(4,1)S(1)}, s32[]{:S(2)}) async-start(s8[8388608]{0:T(1024)(128)(4,1)} %bitcast.7), calls=%async_computation.2 | async-start | bytes 8388608
  309.9 15.2 %collective-permute-start.13 = (f32[32,1,256]{2,0,1:T(8,128)S(1)}, f32[32,1,256]{2,0,1:T(8,128)S(1)}, u32[]{:S(2)}, u32[]{:S(2)}) collective-permute-start(f32[32,1,256]{2,0,1:T(8,128)S(1)} %get-tuple-element.16), channel_id=1, source_target_pairs={{4,0},{8,4},{12,8},{5,1},{9,5},{13,9},{6,2},{10,6},{14,10},{7,3},{... | collective-permute-start | bytes 98312 | tf_op jit(solution)/shard_map/ppermute | solution.py:29
  335.5 24.7 %collective-permute-start.14 = (f32[32,258,1]{1,0,2:T(8,128)S(1)}, f32[32,258,1]{1,0,2:T(8,128)S(1)}, u32[]{:S(2)}, u32[]{:S(2)}) collective-permute-start(f32[32,258,1]{1,0,2:T(8,128)S(1)} %copy.22), channel_id=1, source_target_pairs={{0,1},{1,2},{2,3},{4,5},{5,6},{6,7},{8,9},{9,10},{10,11},{12,13},{... | collective-permute-start | bytes 99080 | tf_op jit(solution)/shard_map/ppermute | solution.py:26
  343.5 20.5 %collective-permute-start.15 = (f32[32,258,1]{1,0,2:T(8,128)S(1)}, f32[32,258,1]{1,0,2:T(8,128)S(1)}, u32[]{:S(2)}, u32[]{:S(2)}) collective-permute-start(f32[32,258,1]{1,0,2:T(8,128)S(1)} %copy.24), channel_id=1, source_target_pairs={{1,0},{2,1},{3,2},{5,4},{6,5},{7,6},{9,8},{10,9},{11,10},{13,12},{... | collective-permute-start | bytes 99080 | tf_op jit(solution)/shard_map/ppermute | solution.py:29
  364.0 27.8 %slice-start.4 = ((s8[4227072]{0:T(1024)(128)(4,1)}), s8[32768]{0:T(1024)(128)(4,1)S(1)}, s32[]{:S(2)}) async-start(s8[4227072]{0:T(1024)(128)(4,1)} %bitcast.11), calls=%async_computation.5 | async-start | bytes 65536
  367.9 23.8 %slice-start.5 = ((s8[4227072]{0:T(1024)(128)(4,1)}), s8[4194304]{0:T(1024)(128)(4,1)S(1)}, s32[]{:S(2)}) async-start(s8[4227072]{0:T(1024)(128)(4,1)} %bitcast.11), calls=%async_computation.6 | async-start | bytes 8388608
  367.9 51.1 %slice-start.2 = ((s8[8388608]{0:T(1024)(128)(4,1)}), s8[4194304]{0:T(1024)(128)(4,1)S(1)}, s32[]{:S(2)}) async-start(s8[8388608]{0:T(1024)(128)(4,1)} %bitcast.9), calls=%async_computation.3 | async-start | bytes 8388608
  391.8 27.3 %slice-start.3 = ((s8[8388608]{0:T(1024)(128)(4,1)}), s8[4194304]{0:T(1024)(128)(4,1)S(1)}, s32[]{:S(2)}) async-start(s8[8388608]{0:T(1024)(128)(4,1)} %bitcast.9), calls=%async_computation.4 | async-start | bytes 8388608
Sparse Core Ops, SparseCore 0:
  432.5 185.3 all-reduce.9
where the time goes:
time: 637 us; the launch traced here: 628 us
  other arithmetic  223 us (35%)
  waiting for transfers between devices  199 us (31%)
  local copies, waits for them, and re-layouts  146 us (23%)
  starting transfers between devices  44 us (7%)
  between operations  15.8 us (2%)
    psum x1, waiting for transfers between devices, on_device(): summed = lax.psum(weighted, 'scen')  186 us
    mul x3, other arithmetic, advance(): (centre - advect + diffusion * spread + settling * (upper_cell - falling)...  120 us
    slice x3, local copies, waits for them, and re-layouts, advance(): upper_cell = jnp.concatenate([centre[1:], zero_plane], 0)  40.2 us
    slice x11, local copies, waits for them, and re-layouts, with_halo(): lax.slice_in_dim(block, block.shape[dim] - width, None, axis=dim)  31.9 us
    ppermute x8, starting transfers between devices, with_halo(): lax.ppermute(lax.slice_in_dim(block, block.shape[dim] - width, None, axis...  29.2 us
    sub x1, other arithmetic, advance(): west_side + east_side + south_side + north_side + upper_cell + lower_cell  27.2 us
    add x1, other arithmetic, advance(): advect + jnp.maximum(courant_y, 0.0) * (centre - south_side)  23.8 us
    slice x5, local copies, waits for them, and re-layouts, advance(): lower_cell = jnp.concatenate([centre[:1], centre[:-1]], 0)  20.3 us
  transfers between devices with their start and end apart: 17, of which 4 were waited for; matrix products, arithmetic and copies ran while one was open for 16% of the time, Pallas kernels for 0%

commit v1 on v0

--- a/solution.py
+++ b/solution.py
@@ -76,9 +76,7 @@
         current = advance(padded, open_cells, courant_x, courant_y)
         toxic_load = toxic_load + current * current
     weighted = weight * lethality(toxic_load[:RZ])
-    summed = lax.psum(weighted, "scen")
-    share = RZ // lax.axis_size("scen")
-    return lax.dynamic_slice_in_dim(summed, lax.axis_index("scen") * share, share, 0)
+    return lax.psum_scatter(weighted, "scen", scatter_dimension=0, tiled=True)
 
 
 def solution(mesh):

time: 637 us -> 545 us (0.86)
  waiting for transfers between devices: 199 us -> 108 us
    psum x1 -> x0, waiting for transfers between devices: 186 us -> none  [on_device(): summed = lax.psum(weighted, 'scen')]
    reduce_scatter x0 -> x1, waiting for transfers between devices: none -> 94.2 us  [on_device(): return lax.psum_scatter(weighted, 'scen', scatter_dimension=0, tiled=True)]
  transfers between devices with their start and end apart: 17 -> 17, of which waited for: 4 -> 4; matrix products, arithmetic and copies ran while one was open for 16% -> 19% of each run, Pallas kernels for 0% -> 0%
where the time goes in v1:
time: 545 us; the launch traced here: 536 us
  other arithmetic  221 us (41%)
  local copies, waits for them, and re-layouts  148 us (27%)
  waiting for transfers between devices  108 us (20%)
  starting transfers between devices  44 us (8%)
  between operations  15.8 us (3%)
    mul x3, other arithmetic, advance(): (centre - advect + diffusion * spread + settling * (upper_cell - falling)...  120 us
    reduce_scatter x1, waiting for transfers between devices, on_device(): return lax.psum_scatter(weighted, 'scen', scatter_dimension=0, tiled=True)  94.2 us
    slice x3, local copies, waits for them, and re-layouts, advance(): upper_cell = jnp.concatenate([centre[1:], zero_plane], 0)  40.2 us
    slice x11, local copies, waits for them, and re-layouts, with_halo(): lax.slice_in_dim(block, block.shape[dim] - width, None, axis=dim)  31.9 us
    ppermute x8, starting transfers between devices, with_halo(): lax.ppermute(lax.slice_in_dim(block, block.shape[dim] - width, None, axis...  29.2 us
    sub x1, other arithmetic, advance(): west_side + east_side + south_side + north_side + upper_cell + lower_cell  27.2 us
    add x1, other arithmetic, advance(): advect + jnp.maximum(courant_y, 0.0) * (centre - south_side)  23.8 us
    slice x5, local copies, waits for them, and re-layouts, advance(): lower_cell = jnp.concatenate([centre[:1], centre[:-1]], 0)  20.4 us
  transfers between devices with their start and end apart: 17, of which 4 were waited for; matrix products, arithmetic and copies ran while one was open for 19% of the time, Pallas kernels for 0%

profile of v1, /device:TPU:1, one launch (start us, length us, event | category | flops | bytes accessed | tf_op | source)
XLA Modules:
  0.0 536.5 jit_solution(6844728203244381851)
XLA Ops:
  6.5 16.5 %bitcast_multiply_fusion = f32[32,256,256]{2,0,1:T(8,128)S(1)} fusion(f32[1,32,256,256]{3,2,1,0:T(8,128)} %param.4, s32[32,256,256]{2,1,0:T(8,128)} %param.5), kind=kLoop, calls=%fused_computation.103 | loop fusion | flops 6291456 | bytes 25165824 | tf_op jit(solution)/shard_map/mul | solution.py:72
  23.0 6.0 %collective-permute-start = (f32[32,1,256]{2,0,1:T(8,128)S(1)}, f32[32,1,256]{2,0,1:T(8,128)S(1)}, u32[]{:S(2)}, u32[]{:S(2)}) collective-permute-start(f32[32,1,256]{2,0,1:T(8,128)S(1)} %get-tuple-element.27), channel_id=1, source_target_pairs={{0,4},{4,8},{8,12},{1,5},{5,9},{9,13},{2,6},{6,10},{10,14},{3,7},{... | collective-permute-start | bytes 98312 | tf_op jit(solution)/shard_map/ppermute | solution.py:26
  31.0 4.8 collective-permute-done.1
  36.7 5.0 fusion.83
  54.2 13.4 %fusion.90 = (f32[31,256,256]{2,0,1:T(8,128)}, f32[31,256,256]{2,0,1:T(8,128)}) fusion(f32[32,256,256]{2,0,1:T(8,128)} %copy-done), kind=kLoop, calls=%fused_computation.135 | loop fusion | bytes 32505856 | tf_op jit(solution)/shard_map/slice | solution.py:46
  78.0 39.9 %fusion.59 = f32[32,256,256]{2,0,1:T(8,128)} fusion(f32[32,1,256]{2,0,1:T(8,128)S(1)} %collective-permute-done.1, f32[32,256,256]{2,0,1:T(8,128)} %copy-done, f32[32,1,256]{2,0,1:T(8,128)S(1)} %collective-permute-done, f32[31,256,256]{2,0,1:T(8,128)} %get-tuple-element.26, f32[1,256,256]{2,0,1:T(1,128)S(1)} %slice.205, ...), kind=kLoop, calls=%fused_computation.94 | loop fusion | flops 75497472 | bytes 41812496 | tf_op jit(solution)/shard_map/mul | solution.py:60
  123.0 4.6 collective-permute-done.5
  131.6 4.8 fusion.82
  140.2 4.7 collective-permute-start.6
  149.9 13.5 %fusion.88 = (f32[31,256,256]{2,0,1:T(8,128)}, f32[31,256,256]{2,0,1:T(8,128)}) fusion(f32[32,256,256]{2,0,1:T(8,128)} %fusion.59), kind=kLoop, calls=%fused_computation.133 | loop fusion | bytes 32505856 | tf_op jit(solution)/shard_map/slice | solution.py:46
  172.9 39.3 %fusion.41 = f32[32,256,256]{2,0,1:T(8,128)} fusion(f32[32,1,256]{2,0,1:T(8,128)S(1)} %collective-permute-done.5, f32[32,256,256]{2,0,1:T(8,128)} %fusion.59, f32[32,1,256]{2,0,1:T(8,128)S(1)} %collective-permute-done.4, f32[31,256,256]{2,0,1:T(8,128)} %get-tuple-element.22, f32[1,256,256]{2,0,1:T(1,128)S(1)} %slice.212, ...), kind=kLoop, calls=%fused_computation.68 | loop fusion | flops 75497472 | bytes 41812496 | tf_op jit(solution)/shard_map/mul | solution.py:60
  217.5 4.4 collective-permute-done.9
  225.9 4.8 fusion.81
  234.5 4.3 collective-permute-start.10
  243.8 13.4 %fusion.86 = (f32[31,256,256]{2,0,1:T(8,128)}, f32[31,256,256]{2,0,1:T(8,128)}) fusion(f32[32,256,256]{2,0,1:T(8,128)} %fusion.41), kind=kLoop, calls=%fused_computation.131 | loop fusion | bytes 32505856 | tf_op jit(solution)/shard_map/slice | solution.py:46
  266.6 40.3 %fusion.23 = f32[32,256,256]{2,0,1:T(8,128)} fusion(f32[32,1,256]{2,0,1:T(8,128)S(1)} %collective-permute-done.9, f32[32,256,256]{2,0,1:T(8,128)} %fusion.41, f32[32,1,256]{2,0,1:T(8,128)S(1)} %collective-permute-done.8, f32[31,256,256]{2,0,1:T(8,128)} %get-tuple-element.18, f32[1,256,256]{2,0,1:T(1,128)S(1)} %slice.219, ...), kind=kLoop, calls=%fused_computation.42 | loop fusion | flops 75497472 | bytes 41812496 | tf_op jit(solution)/shard_map/mul | solution.py:60
  312.6 11.7 %fusion.67 = f32[32,256,256]{2,0,1:T(8,128)} fusion(s32[32,256,256]{2,1,0:T(8,128)} %param.5), kind=kLoop, calls=%fused_computation.105 | loop fusion | flops 4194304 | bytes 16777216 | tf_op jit(solution)/shard_map/convert_element_type | solution.py:69
  326.9 4.9 fusion.80
  345.0 13.5 %fusion.84 = (f32[31,256,256]{2,0,1:T(8,128)}, f32[31,256,256]{2,0,1:T(8,128)}) fusion(f32[32,256,256]{2,0,1:T(8,128)} %fusion.23), kind=kLoop, calls=%fused_computation.129 | loop fusion | bytes 32505856 | tf_op jit(solution)/shard_map/slice | solution.py:47
  368.0 23.8 %fusion.10 = f32[32,256,256]{2,0,1:T(8,128)} fusion(f32[32,256,256]{2,0,1:T(8,128)} %fusion.23, f32[32,1,256]{2,0,1:T(8,128)S(1)} %collective-permute-done.13, f32[32,1,256]{2,0,1:T(8,128)S(1)} %collective-permute-done.12, f32[32,258,1]{2,0,1:T(8,128)} %copy.23, f32[32,258,1]{2,0,1:T(8,128)} %copy.25, f32[]{:T(128)} %bitcast.4, f32[]{:T(128)} %bitcast.3, ...), kind=kLoop, calls=%fused_computation.21 | loop fusion | flops 39845888 | bytes 16908816 | tf_op jit(solution)/shard_map/add | solution.py:53
  391.8 27.2 %fusion.6 = f32[32,256,256]{2,0,1:T(8,128)} fusion(f32[32,1,256]{2,0,1:T(8,128)S(1)} %collective-permute-done.13, f32[32,256,256]{2,0,1:T(8,128)} %fusion.23, f32[32,1,256]{2,0,1:T(8,128)S(1)} %collective-permute-done.12, f32[31,256,256]{2,0,1:T(8,128)} %get-tuple-element.13, f32[1,256,256]{2,0,1:T(1,128)S(1)} %slice.226, ...), kind=kLoop, calls=%fused_computation.17 | loop fusion | flops 33554432 | bytes 33423872 | tf_op jit(solution)/shard_map/sub | solution.py:58
  419.0 11.5 %add_multiply_fusion = f32[16,256,256]{2,0,1:T(8,128)S(1)} fusion(f32[32,256,256]{2,0,1:T(8,128)} %fusion.67, f32[31,256,256]{2,0,1:T(8,128)} %get-tuple-element.14, f32[32,256,256]{2,0,1:T(8,128)} %fusion.6, f32[32,256,256]{2,0,1:T(8,128)} %fusion.10, f32[32,256,256]{2,0,1:T(8,128)S(1)} %bitcast.10, f32[32,256,256]{2,0,1:T(8,128)} %fusion.41, ...), kind=kLoop, calls=%fused_computation.124 | loop fusion | flops 19922944 | bytes 37486596 | tf_op jit(solution)/shard_map/mul | solution.py:78
  430.5 4.4 copy.26
  435.0 94.2 %reduce-scatter.2.cloned.1.call-done = f32[2,256,256]{2,1,0:T(8,128)} async-done(((f32[16,256,256]{2,1,0:T(8,128)}), f32[2,256,256]{2,1,0:T(8,128)}) %reduce-scatter.2.cloned.1.call-update) | async-done | bytes 524304 | tf_op jit(solution)/shard_map/reduce_scatter | solution.py:79
  (73 shorter events, 109.7 us)
Async XLA Ops:
  6.5 522.6 %reduce-scatter.2.cloned.1.call-start = ((), (), s32[]{:S(2)}) async-start(), calls=%async_computation.1 | async-start | bytes 4718592 | tf_op jit(solution)/shard_map/reduce_scatter | solution.py:79
  23.0 12.8 %copy-start = (f32[32,256,256]{2,0,1:T(8,128)}, f32[32,256,256]{2,0,1:T(8,128)S(1)}, u32[]{:S(2)}) copy-start(f32[32,256,256]{2,0,1:T(8,128)S(1)} %bitcast_multiply_fusion) | copy-start | bytes 25165828
  23.0 8.0 %collective-permute-start = (f32[32,1,256]{2,0,1:T(8,128)S(1)}, f32[32,1,256]{2,0,1:T(8,128)S(1)}, u32[]{:S(2)}, u32[]{:S(2)}) collective-permute-start(f32[32,1,256]{2,0,1:T(8,128)S(1)} %get-tuple-element.27), channel_id=1, source_target_pairs={{0,4},{4,8},{8,12},{1,5},{5,9},{9,13},{2,6},{6,10},{10,14},{3,7},{... | collective-permute-start | bytes 98312 | tf_op jit(solution)/shard_map/ppermute | solution.py:26
  29.1 6.7 %collective-permute-start.1 = (f32[32,1,256]{2,0,1:T(8,128)S(1)}, f32[32,1,256]{2,0,1:T(8,128)S(1)}, u32[]{:S(2)}, u32[]{:S(2)}) collective-permute-start(f32[32,1,256]{2,0,1:T(8,128)S(1)} %get-tuple-element.28), channel_id=1, source_target_pairs={{4,0},{8,4},{12,8},{5,1},{9,5},{13,9},{6,2},{10,6},{14,10},{7,3},{... | collective-permute-start | bytes 98312 | tf_op jit(solution)/shard_map/ppermute | solution.py:29
  45.4 24.7 %collective-permute-start.2 = (f32[32,258,1]{1,0,2:T(8,128)S(1)}, f32[32,258,1]{1,0,2:T(8,128)S(1)}, u32[]{:S(2)}, u32[]{:S(2)}) collective-permute-start(f32[32,258,1]{1,0,2:T(8,128)S(1)} %copy.10), channel_id=1, source_target_pairs={{0,1},{1,2},{2,3},{4,5},{5,6},{6,7},{8,9},{9,10},{10,11},{12,13},{... | collective-permute-start | bytes 99080 | tf_op jit(solution)/shard_map/ppermute | solution.py:26
  52.7 21.4 %collective-permute-start.3 = (f32[32,258,1]{1,0,2:T(8,128)S(1)}, f32[32,258,1]{1,0,2:T(8,128)S(1)}, u32[]{:S(2)}, u32[]{:S(2)}) collective-permute-start(f32[32,258,1]{1,0,2:T(8,128)S(1)} %copy.12), channel_id=1, source_target_pairs={{1,0},{2,1},{3,2},{5,4},{6,5},{7,6},{9,8},{10,9},{11,10},{13,12},{... | collective-permute-start | bytes 99080 | tf_op jit(solution)/shard_map/ppermute | solution.py:29
  118.7 4.3 collective-permute-start.4
  120.9 6.7 %collective-permute-start.5 = (f32[32,1,256]{2,0,1:T(8,128)S(1)}, f32[32,1,256]{2,0,1:T(8,128)S(1)}, u32[]{:S(2)}, u32[]{:S(2)}) collective-permute-start(f32[32,1,256]{2,0,1:T(8,128)S(1)} %get-tuple-element.24), channel_id=1, source_target_pairs={{4,0},{8,4},{12,8},{5,1},{9,5},{13,9},{6,2},{10,6},{14,10},{7,3},{... | collective-permute-start | bytes 98312 | tf_op jit(solution)/shard_map/ppermute | solution.py:29
  140.2 24.9 %collective-permute-start.6 = (f32[32,258,1]{1,0,2:T(8,128)S(1)}, f32[32,258,1]{1,0,2:T(8,128)S(1)}, u32[]{:S(2)}, u32[]{:S(2)}) collective-permute-start(f32[32,258,1]{1,0,2:T(8,128)S(1)} %copy.14), channel_id=1, source_target_pairs={{0,1},{1,2},{2,3},{4,5},{5,6},{6,7},{8,9},{9,10},{10,11},{12,13},{... | collective-permute-start | bytes 99080 | tf_op jit(solution)/shard_map/ppermute | solution.py:26
  148.6 20.4 %collective-permute-start.7 = (f32[32,258,1]{1,0,2:T(8,128)S(1)}, f32[32,258,1]{1,0,2:T(8,128)S(1)}, u32[]{:S(2)}, u32[]{:S(2)}) collective-permute-start(f32[32,258,1]{1,0,2:T(8,128)S(1)} %copy.16), channel_id=1, source_target_pairs={{1,0},{2,1},{3,2},{5,4},{6,5},{7,6},{9,8},{10,9},{11,10},{13,12},{... | collective-permute-start | bytes 99080 | tf_op jit(solution)/shard_map/ppermute | solution.py:29
  213.0 4.5 collective-permute-start.8
  215.2 6.7 %collective-permute-start.9 = (f32[32,1,256]{2,0,1:T(8,128)S(1)}, f32[32,1,256]{2,0,1:T(8,128)S(1)}, u32[]{:S(2)}, u32[]{:S(2)}) collective-permute-start(f32[32,1,256]{2,0,1:T(8,128)S(1)} %get-tuple-element.20), channel_id=1, source_target_pairs={{4,0},{8,4},{12,8},{5,1},{9,5},{13,9},{6,2},{10,6},{14,10},{7,3},{... | collective-permute-start | bytes 98312 | tf_op jit(solution)/shard_map/ppermute | solution.py:29
  234.5 24.4 %collective-permute-start.10 = (f32[32,258,1]{1,0,2:T(8,128)S(1)}, f32[32,258,1]{1,0,2:T(8,128)S(1)}, u32[]{:S(2)}, u32[]{:S(2)}) collective-permute-start(f32[32,258,1]{1,0,2:T(8,128)S(1)} %copy.18), channel_id=1, source_target_pairs={{0,1},{1,2},{2,3},{4,5},{5,6},{6,7},{8,9},{9,10},{10,11},{12,13},{... | collective-permute-start | bytes 99080 | tf_op jit(solution)/shard_map/ppermute | solution.py:26
  242.5 20.2 %collective-permute-start.11 = (f32[32,258,1]{1,0,2:T(8,128)S(1)}, f32[32,258,1]{1,0,2:T(8,128)S(1)}, u32[]{:S(2)}, u32[]{:S(2)}) collective-permute-start(f32[32,258,1]{1,0,2:T(8,128)S(1)} %copy.20), channel_id=1, source_target_pairs={{1,0},{2,1},{3,2},{5,4},{6,5},{7,6},{9,8},{10,9},{11,10},{13,12},{... | collective-permute-start | bytes 99080 | tf_op jit(solution)/shard_map/ppermute | solution.py:29
  307.7 17.4 %collective-permute-start.12 = (f32[32,1,256]{2,0,1:T(8,128)S(1)}, f32[32,1,256]{2,0,1:T(8,128)S(1)}, u32[]{:S(2)}, u32[]{:S(2)}) collective-permute-start(f32[32,1,256]{2,0,1:T(8,128)S(1)} %get-tuple-element.15), channel_id=1, source_target_pairs={{0,4},{4,8},{8,12},{1,5},{5,9},{9,13},{2,6},{6,10},{10,14},{3,7},{... | collective-permute-start | bytes 98312 | tf_op jit(solution)/shard_map/ppermute | solution.py:26
  309.9 15.2 %slice-start = ((s8[8388608]{0:T(1024)(128)(4,1)}), s8[4194304]{0:T(1024)(128)(4,1)S(1)}, s32[]{:S(2)}) async-start(s8[8388608]{0:T(1024)(128)(4,1)} %bitcast.7), calls=%async_computation.2 | async-start | bytes 8388608
  309.9 15.2 %slice-start.1 = ((s8[8388608]{0:T(1024)(128)(4,1)}), s8[4194304]{0:T(1024)(128)(4,1)S(1)}, s32[]{:S(2)}) async-start(s8[8388608]{0:T(1024)(128)(4,1)} %bitcast.7), calls=%async_computation.3 | async-start | bytes 8388608
  309.9 15.2 %collective-permute-start.13 = (f32[32,1,256]{2,0,1:T(8,128)S(1)}, f32[32,1,256]{2,0,1:T(8,128)S(1)}, u32[]{:S(2)}, u32[]{:S(2)}) collective-permute-start(f32[32,1,256]{2,0,1:T(8,128)S(1)} %get-tuple-element.16), channel_id=1, source_target_pairs={{4,0},{8,4},{12,8},{5,1},{9,5},{13,9},{6,2},{10,6},{14,10},{7,3},{... | collective-permute-start | bytes 98312 | tf_op jit(solution)/shard_map/ppermute | solution.py:29
  335.5 24.7 %collective-permute-start.14 = (f32[32,258,1]{1,0,2:T(8,128)S(1)}, f32[32,258,1]{1,0,2:T(8,128)S(1)}, u32[]{:S(2)}, u32[]{:S(2)}) collective-permute-start(f32[32,258,1]{1,0,2:T(8,128)S(1)} %copy.22), channel_id=1, source_target_pairs={{0,1},{1,2},{2,3},{4,5},{5,6},{6,7},{8,9},{9,10},{10,11},{12,13},{... | collective-permute-start | bytes 99080 | tf_op jit(solution)/shard_map/ppermute | solution.py:26
  343.5 20.6 %collective-permute-start.15 = (f32[32,258,1]{1,0,2:T(8,128)S(1)}, f32[32,258,1]{1,0,2:T(8,128)S(1)}, u32[]{:S(2)}, u32[]{:S(2)}) collective-permute-start(f32[32,258,1]{1,0,2:T(8,128)S(1)} %copy.24), channel_id=1, source_target_pairs={{1,0},{2,1},{3,2},{5,4},{6,5},{7,6},{9,8},{10,9},{11,10},{13,12},{... | collective-permute-start | bytes 99080 | tf_op jit(solution)/shard_map/ppermute | solution.py:29
  364.0 27.7 %slice-start.4 = ((s8[4227072]{0:T(1024)(128)(4,1)}), s8[32768]{0:T(1024)(128)(4,1)S(1)}, s32[]{:S(2)}) async-start(s8[4227072]{0:T(1024)(128)(4,1)} %bitcast.11), calls=%async_computation.6 | async-start | bytes 65536
  368.0 23.8 %slice-start.5 = ((s8[4227072]{0:T(1024)(128)(4,1)}), s8[4194304]{0:T(1024)(128)(4,1)S(1)}, s32[]{:S(2)}) async-start(s8[4227072]{0:T(1024)(128)(4,1)} %bitcast.11), calls=%async_computation.7 | async-start | bytes 8388608
  368.0 51.0 %slice-start.2 = ((s8[8388608]{0:T(1024)(128)(4,1)}), s8[4194304]{0:T(1024)(128)(4,1)S(1)}, s32[]{:S(2)}) async-start(s8[8388608]{0:T(1024)(128)(4,1)} %bitcast.9), calls=%async_computation.4 | async-start | bytes 8388608
  391.8 27.2 %slice-start.3 = ((s8[8388608]{0:T(1024)(128)(4,1)}), s8[4194304]{0:T(1024)(128)(4,1)S(1)}, s32[]{:S(2)}) async-start(s8[8388608]{0:T(1024)(128)(4,1)} %bitcast.9), calls=%async_computation.5 | async-start | bytes 8388608
Sparse Core Ops, SparseCore 0:
  435.1 94.0 reduce-scatter.1

commit v2 on v1

v2 whole, which is shorter than its diff:
```python
import math

import jax
import jax.numpy as jnp
from jax import lax
from jax.experimental import pallas as pl
from jax.experimental.pallas import tpu as pltpu
from jax.sharding import PartitionSpec as P

STEPS = 4
RZ = 16


wind_speed = 0.4
diffusion = 0.05
settling = 0.1
probit_a = 3.0
probit_b = 1.0
load_eps = 0.01
freq_rate = 0.7

H = STEPS
PAD = 16
EXTRA = 128
RB = 8


def wind_components(sector_id):
    heading = sector_id.astype(jnp.float32) * (2.0 * math.pi / 16.0)
    return (wind_speed * jnp.cos(heading), wind_speed * jnp.sin(heading))


def _open_and_c(src, obs):
    open_cells = (1 - obs).astype(jnp.float32)
    return jnp.stack([src * open_cells, open_cells])


def ghost_pieces(src, obs):
    nz, nx, ny = src.shape
    gxn = lax.axis_size("gx")
    gyn = lax.axis_size("gy")
    fx = [(i, i + 1) for i in range(gxn - 1)]
    bx = [(i + 1, i) for i in range(gxn - 1)]
    fy = [(i, i + 1) for i in range(gyn - 1)]
    by = [(i + 1, i) for i in range(gyn - 1)]
    last_rows = _open_and_c(src[:, nx - H:, :], obs[:, nx - H:, :])
    first_rows = _open_and_c(src[:, :H, :], obs[:, :H, :])
    xlo = lax.ppermute(last_rows, "gx", fx)
    xhi = lax.ppermute(first_rows, "gx", bx)
    last_cols = _open_and_c(src[:, :, ny - H:], obs[:, :, ny - H:])
    first_cols = _open_and_c(src[:, :, :H], obs[:, :, :H])
    ext_last = jnp.concatenate([xlo[..., ny - H:], last_cols, xhi[..., ny - H:]], axis=2)
    ext_first = jnp.concatenate([xlo[..., :H], first_cols, xhi[..., :H]], axis=2)
    yw = lax.ppermute(jnp.swapaxes(ext_last, -1, -2), "gy", fy)
    ye = lax.ppermute(jnp.swapaxes(ext_first, -1, -2), "gy", by)
    yw = jnp.swapaxes(yw, -1, -2)
    ye = jnp.swapaxes(ye, -1, -2)
    rows = nx + 2 * PAD
    mid = jnp.zeros(ye.shape[:-1] + (EXTRA - 2 * H,), jnp.float32)
    lanes = jnp.concatenate([ye, mid, yw], axis=-1)
    lanes = jnp.pad(lanes, ((0, 0), (0, 0), (PAD - H, rows - nx - PAD - H), (0, 0)))
    r_lo = jnp.pad(xlo, ((0, 0), (0, 0), (PAD - H, 0), (0, 0)))
    r_hi = jnp.pad(xhi, ((0, 0), (0, 0), (0, PAD - H), (0, 0)))
    return r_lo, r_hi, lanes


def make_kernel(nz, nx, ny, rz):
    rows = nx + 2 * PAD
    width = ny + EXTRA
    nblk = rows // RB
    b_first = 1
    b_last = nblk - 2
    acc_lo = PAD // RB
    acc_hi = (PAD + nx) // RB

    def kernel(coef, src_hbm, obs_hbm, rlo_hbm, rhi_hbm, lanes_hbm, out_ref,
               a_buf, b_buf, o_buf, obs_buf, sems):
        copies = [
            pltpu.make_async_copy(obs_hbm, obs_buf, sems.at[0]),
            pltpu.make_async_copy(rlo_hbm.at[1], o_buf.at[:, pl.ds(0, PAD), pl.ds(0, ny)], sems.at[1]),
            pltpu.make_async_copy(rhi_hbm.at[1], o_buf.at[:, pl.ds(PAD + nx, PAD), pl.ds(0, ny)], sems.at[2]),
            pltpu.make_async_copy(lanes_hbm.at[1], o_buf.at[:, :, pl.ds(ny, EXTRA)], sems.at[3]),
            pltpu.make_async_copy(src_hbm.at[0], a_buf.at[:, pl.ds(PAD, nx), pl.ds(0, ny)], sems.at[4]),
            pltpu.make_async_copy(rlo_hbm.at[0], a_buf.at[:, pl.ds(0, PAD), pl.ds(0, ny)], sems.at[5]),
            pltpu.make_async_copy(rhi_hbm.at[0], a_buf.at[:, pl.ds(PAD + nx, PAD), pl.ds(0, ny)], sems.at[6]),
            pltpu.make_async_copy(lanes_hbm.at[0], a_buf.at[:, :, pl.ds(ny, EXTRA)], sems.at[7]),
        ]
        for cp in copies:
            cp.start()

        zeros = jnp.zeros((RB, width), jnp.float32)

        def clear(z, c):
            b_buf[z, pl.ds(0, RB), :] = zeros
            b_buf[z, pl.ds(rows - RB, RB), :] = zeros
            return c

        lax.fori_loop(0, nz, clear, 0)

        copies[0].wait()

        def to_open(z, c):
            o_buf[z, pl.ds(PAD, nx), pl.ds(0, ny)] = (1 - obs_buf[z]).astype(jnp.float32)
            return c

        lax.fori_loop(0, nz, to_open, 0)
        copies[4].wait()

        def to_c0(z, c):
            a_buf[z, pl.ds(PAD, nx), pl.ds(0, ny)] = (
                a_buf[z, pl.ds(PAD, nx), pl.ds(0, ny)] * o_buf[z, pl.ds(PAD, nx), pl.ds(0, ny)]
            )
            return c

        lax.fori_loop(0, nz, to_c0, 0)
        for cp in copies[1:4] + copies[5:]:
            cp.wait()

        k_w = coef[0]
        k_e = coef[1]
        k_s = coef[2]
        k_n = coef[3]
        k0_first = coef[4]
        k0_rest = coef[5]
        weight = coef[6]
        row_id = lax.broadcasted_iota(jnp.int32, (RB, width), 0)
        first_row = row_id == 0
        last_row = row_id == RB - 1

        def step(src, dst, first):
            def level(z, accumulate):
                zu = jnp.minimum(z + 1, nz - 1)
                zl = jnp.maximum(z - 1, 0)
                k0 = jnp.where(z == 0, k0_first, k0_rest)
                ku = jnp.where(z == nz - 1, 0.0, diffusion + settling).astype(jnp.float32)

                def blk(b, carry, acc):
                    prev, cur = carry
                    r = pl.multiple_of(b * RB, RB)
                    nxt = src[z, pl.ds(r + RB, RB), :]
                    west = jnp.where(first_row, pltpu.roll(prev, 1, 0), pltpu.roll(cur, 1, 0))
                    east = jnp.where(last_row, pltpu.roll(nxt, RB - 1, 0), pltpu.roll(cur, RB - 1, 0))
                    south = pltpu.roll(cur, 1, 1)
                    north = pltpu.roll(cur, width - 1, 1)
                    up = src[zu, pl.ds(r, RB), :]
                    low = src[zl, pl.ds(r, RB), :]
                    o = o_buf[z, pl.ds(r, RB), :]
                    new = o * (
                        k0 * cur
                        + k_w * west
                        + k_e * east
                        + k_s * south
                        + k_n * north
                        + ku * up
                        + diffusion * low
                    )
                    dst[z, pl.ds(r, RB), :] = new
                    if acc:
                        inner = new[:, :ny]
                        ro = pl.multiple_of(r - PAD, RB)
                        if first:
                            out_ref[z, pl.ds(ro, RB), :] = inner * inner
                        else:
                            out_ref[z, pl.ds(ro, RB), :] = out_ref[z, pl.ds(ro, RB), :] + inner * inner
                    return (cur, nxt)

                carry = (src[z, pl.ds(0, RB), :], src[z, pl.ds(RB, RB), :])
                if accumulate:
                    carry = lax.fori_loop(b_first, acc_lo, lambda b, c: blk(b, c, False), carry)
                    carry = lax.fori_loop(acc_lo, acc_hi, lambda b, c: blk(b, c, True), carry, unroll=4)
                    carry = lax.fori_loop(acc_hi, b_last + 1, lambda b, c: blk(b, c, False), carry)
                else:
                    carry = lax.fori_loop(b_first, b_last + 1, lambda b, c: blk(b, c, False), carry, unroll=2)

            def lvl_acc(z, c):
                level(z, True)
                return c

            def lvl_plain(z, c):
                level(z, False)
                return c

            lax.fori_loop(0, rz, lvl_acc, 0)
            lax.fori_loop(rz, nz, lvl_plain, 0)

        bufs = (a_buf, b_buf)
        for n in range(STEPS):
            step(bufs[n % 2], bufs[(n + 1) % 2], n == 0)

        def leth(z, c):
            for q in range(nx // 32):
                load = out_ref[z, pl.ds(q * 32, 32), :]
                probit = probit_a + probit_b * jnp.log(load + load_eps)
                lethal = 0.5 * (1.0 + lax.erf((probit - 5.0) / math.sqrt(2.0)))
                out_ref[z, pl.ds(q * 32, 32), :] = weight * lethal
            return c

        lax.fori_loop(0, rz, leth, 0)

    return kernel


def on_device(source, obstacle, sector, freq_class):
    src = source[0]
    nz, nx, ny = src.shape
    courant_x, courant_y = wind_components(sector[0])
    weight = jnp.exp(-freq_rate * freq_class[0].astype(jnp.float32))
    px = jnp.maximum(courant_x, 0.0)
    mx = jnp.minimum(courant_x, 0.0)
    py = jnp.maximum(courant_y, 0.0)
    my = jnp.minimum(courant_y, 0.0)
    base = 1.0 - px + mx - py + my - 6.0 * diffusion
    coef = jnp.stack(
        [px + diffusion, diffusion - mx, py + diffusion, diffusion - my, base, base - settling,
         weight, jnp.float32(0.0)]
    ).astype(jnp.float32)
    r_lo, r_hi, lanes = ghost_pieces(src, obstacle)
    rows = nx + 2 * PAD
    width = ny + EXTRA
    any_spec = pl.BlockSpec(memory_space=pl.ANY)
    weighted = pl.pallas_call(
        make_kernel(nz, nx, ny, RZ),
        out_shape=jax.ShapeDtypeStruct((RZ, nx, ny), jnp.float32),
        in_specs=[pl.BlockSpec(memory_space=pltpu.SMEM)] + [any_spec] * 5,
        out_specs=pl.BlockSpec(memory_space=pltpu.VMEM),
        scratch_shapes=[
            pltpu.VMEM((nz, rows, width), jnp.float32),
            pltpu.VMEM((nz, rows, width), jnp.float32),
            pltpu.VMEM((nz, rows, width), jnp.float32),
            pltpu.VMEM((nz, nx, ny), jnp.int32),
            pltpu.SemaphoreType.DMA((8,)),
        ],
        compiler_params=pltpu.CompilerParams(vmem_limit_bytes=62 * 1024 * 1024),
    )(coef, source, obstacle, r_lo, r_hi, lanes)
    return lax.psum_scatter(weighted, "scen", scatter_dimension=0, tiled=True)


def solution(mesh):
    in_specs = (P("scen", None, "gx", "gy"), P(None, "gx", "gy"), P("scen"), P("scen"))
    out_specs = P("scen", "gx", "gy")
    return jax.shard_map(
        on_device, mesh=mesh, in_specs=in_specs, out_specs=out_specs, check_vma=False
    )
```

time: 545 us -> 356 us (0.65); the launches traced: 536 us -> 356 us
  other arithmetic: 221 us -> 28.6 us
  Pallas kernels: 0 us -> 169 us
  local copies, waits for them, and re-layouts: 148 us -> 35.2 us
  starting transfers between devices: 44 us -> 13.2 us
  waiting for transfers between devices: 108 us -> 94.3 us
    pallas_call x0 -> x1, Pallas kernels: none -> 169 us  [on_device(): pl.pallas_call(make_kernel(nz, nx, ny, RZ), out_shape=jax.ShapeDtypeStruc...]
    mul x5 -> x0, other arithmetic: 148 us -> none  [the longest x3 120 us: advance(): (centre - advect + diffusion * spread + settling * (upper_cell - falling)...]
    slice x24 -> x6, local copies, waits for them, and re-layouts: 112 us -> 2.49 us  [the longest x2 0.69 us: ghost_pieces(): xhi[..., :H]]
    ppermute x16 -> x4, starting transfers between devices: 44 us -> 13.2 us  [the longest x1 6.03 us: ghost_pieces(): xlo = lax.ppermute(last_rows, 'gx', fx)]
    sub x1 -> x0, other arithmetic: 27.2 us -> none  [advance(): west_side + east_side + south_side + north_side + upper_cell + lower_cell]
    add x1 -> x0, other arithmetic: 23.8 us -> none  [advance(): advect + jnp.maximum(courant_y, 0.0) * (centre - south_side)]
    ppermute x8 -> x2, local copies, waits for them, and re-layouts: 30.9 us -> 9.91 us  [the longest x1 4.96 us: ghost_pieces(): yw = lax.ppermute(jnp.swapaxes(ext_last, -1, -2), 'gy', fy)]
    another operation x0 -> x6, other arithmetic: none -> 16.5 us  [_open_and_c(): return jnp.stack([src * open_cells, open_cells])]
  transfers between devices with their start and end apart: 17 -> 5, of which waited for: 4 -> 1; matrix products, arithmetic and copies ran while one was open for 19% -> 10% of each run, Pallas kernels for 0% -> 0%
where the time goes in v2:
time: 356 us
  Pallas kernels  169 us (47%)
  waiting for transfers between devices  94.3 us (26%)
  local copies, waits for them, and re-layouts  35.2 us (10%)
  other arithmetic  28.6 us (8%)
  between operations  15.1 us (4%)
  starting transfers between devices  13.2 us (4%)
    pallas_call x1, Pallas kernels, on_device(): pl.pallas_call(make_kernel(nz, nx, ny, RZ), out_shape=jax.ShapeDtypeStruc...  169 us
    reduce_scatter x1, waiting for transfers between devices, on_device(): return lax.psum_scatter(weighted, 'scen', scatter_dimension=0, tiled=True)  94.2 us
    another operation x6, other arithmetic, _open_and_c(): return jnp.stack([src * open_cells, open_cells])  16.5 us
    concatenate x1, other arithmetic, ghost_pieces(): lanes = jnp.concatenate([ye, mid, yw], axis=-1)  11.7 us
    another operation x4, local copies, waits for them, and re-layouts, _open_and_c(): return jnp.stack([src * open_cells, open_cells])  11.4 us
    pad x1, local copies, waits for them, and re-layouts, ghost_pieces(): jnp.pad(lanes, ((0, 0), (0, 0), (PAD - H, rows - nx - PAD - H), (0, 0)))  8.49 us
  transfers between devices with their start and end apart: 5, of which 1 were waited for; matrix products, arithmetic and copies ran while one was open for 10% of the time, Pallas kernels for 0%

profile of v2, /device:TPU:1, one launch (start us, length us, event | category | flops | bytes accessed | tf_op | source)
XLA Modules:
  0.0 355.6 jit_solution(2756294484961235102)
XLA Ops:
  6.5 1.1 convert_bitcast_fusion.2
  7.6 1.3 fusion.2
  9.0 6.0 %collective-permute-start = (f32[2,32,4,256]{3,2,1,0:T(4,128)S(1)}, f32[2,32,4,256]{3,2,1,0:T(4,128)S(1)}, u32[]{:S(2)}, u32[]{:S(2)}) collective-permute-start(f32[2,32,4,256]{3,2,1,0:T(4,128)S(1)} %pad_maximum_fusion.1), channel_id=1, source_target_pairs={{0,4},{4,8},{8,12},{1,5},{5,9},{9,13},{2,6},{6,10},{10,14},{3,7},{... | collective-permute-start | bytes 786440 | tf_op jit(solution)/shard_map/ppermute | solution.py:48
  15.1 2.3 collective-permute-start.1
  17.4 9.3 %fusion.1 = (f32[1,32,256,4]{3,2,1,0:T(8,128)}, f32[1,32,256,4]{3,2,1,0:T(8,128)}) fusion(f32[32,256,256]{2,1,0:T(8,128)} %bitcast.26, s32[32,256,256]{2,1,0:T(8,128)} %obs_hbm.1), kind=kLoop, calls=%fused_computation.4 | loop fusion | flops 196608 | bytes 786432 | tf_op jit(solution)/shard_map/stack | solution.py:35
  26.8 4.7 %convert_bitcast_fusion.1 = (f32[1,32,256,4]{3,2,1,0:T(8,128)}, f32[1,32,256,4]{3,2,1,0:T(8,128)}) fusion(s32[32,256,256]{2,1,0:T(8,128)S(1)} %bitcast.24), kind=kLoop, calls=%fused_computation.7 | loop fusion | flops 131072 | bytes 524288 | tf_op jit(solution)/shard_map/stack | solution.py:35
  31.4 2.9 copy.10
  34.3 2.9 copy.11
  37.2 2.9 copy.5
  40.0 2.9 copy.6
  43.0 0.6 copy.12
  43.8 0.6 copy.13
  44.5 3.6 %collective-permute-start.3 = (f32[2,32,4,264]{3,1,2,0:T(8,128)S(1)}, f32[2,32,4,264]{3,1,2,0:T(8,128)S(1)}, u32[]{:S(2)}, u32[]{:S(2)}) collective-permute-start(f32[2,32,4,264]{3,1,2,0:T(8,128)S(1)} %maximum_bitcast_fusion.1), channel_id=1, source_target_pairs={{0,1},{1,2},{2,3},{4,5},{5,6},{6,7},{8,9},{9,10},{10,11},{12,13},{... | collective-permute-start | bytes 811016 | tf_op jit(solution)/shard_map/ppermute | solution.py:54
  48.1 0.6 copy.7
  49.4 1.3 collective-permute-start.2
  52.3 0.6 stack.64.coef
  52.9 1.1 pad.12.rlo_hbm
  54.0 1.1 pad.13.rhi_hbm
  55.1 5.0 %copy.14 = f32[2,32,4,264]{2,3,1,0:T(8,128)} copy(f32[2,32,4,264]{3,1,2,0:T(8,128)S(1)} %collective-permute-done.3) | data formatting | bytes 540672 | tf_op jit(solution)/shard_map/ppermute | solution.py:54
  60.1 5.0 %copy.9 = f32[2,32,4,264]{2,3,1,0:T(8,128)} copy(f32[2,32,4,264]{3,1,2,0:T(8,128)S(1)} %collective-permute-done.2) | data formatting | bytes 540672 | tf_op jit(solution)/shard_map/ppermute | solution.py:55
  65.1 11.7 %pad_maximum_fusion = f32[2,32,264,128]{3,2,1,0:T(8,128)} fusion(f32[2,32,264,4]{3,2,1,0:T(8,128)} %bitcast.27, f32[2,32,264,4]{3,2,1,0:T(8,128)} %bitcast.28, f32[128]{0:T(128)S(1)} %pad.16.clone), kind=kLoop, calls=%fused_computation | loop fusion | flops 4325376 | bytes 9191936 | tf_op jit(solution)/shard_map/concatenate | solution.py:60
  76.7 8.5 %pad.14.lanes_hbm = f32[2,32,288,128]{3,2,1,0:T(8,128)} pad(f32[2,32,264,128]{3,2,1,0:T(8,128)} %pad_maximum_fusion, f32[]{:T(128)} %constant.12.clone.1), padding=0_0x0_0x12_12x0_0 | pad | bytes 18087940 | tf_op jit(solution)/shard_map/jit(_pad)/pad | solution.py:61
  85.2 169.2 %shard_map.46 = f32[16,256,256]{2,1,0:T(8,128)} custom-call(f32[8]{0:T(128)} %stack.64.coef, f32[1,32,256,256]{3,2,1,0:T(8,128)} %src_hbm.1, s32[32,256,256]{2,1,0:T(8,128)} %obs_hbm.1, f32[2,32,16,256]{3,2,1,0:T(8,128)} %pad.12.rlo_hbm, f32[2,32,16,256]{3,2,1,0:T(8,128)} %pad.13.rhi_hbm, f32[2,32,288,128]{3,2,1,0:T(8,128)} %pad.14.lanes_hbm), custom_call_target="tpu_custom_call" | custom-call | tf_op jit(solution)/shard_map/pallas_call | solution.py:221
  254.5 94.2 %reduce-scatter.2.cloned.1.call-done = f32[2,256,256]{2,1,0:T(8,128)} async-done(((f32[16,256,256]{2,1,0:T(8,128)}), f32[2,256,256]{2,1,0:T(8,128)}) %reduce-scatter.2.cloned.1.call-update) | async-done | bytes 524304 | tf_op jit(solution)/shard_map/reduce_scatter | solution.py:235
  (20 shorter events, 1.5 us)
Async XLA Ops:
  6.5 342.2 %reduce-scatter.2.cloned.1.call-start = ((), (), s32[]{:S(2)}) async-start(), calls=%async_computation.1 | async-start | bytes 4718592 | tf_op jit(solution)/shard_map/reduce_scatter | solution.py:235
  9.0 33.9 %collective-permute-start = (f32[2,32,4,256]{3,2,1,0:T(4,128)S(1)}, f32[2,32,4,256]{3,2,1,0:T(4,128)S(1)}, u32[]{:S(2)}, u32[]{:S(2)}) collective-permute-start(f32[2,32,4,256]{3,2,1,0:T(4,128)S(1)} %pad_maximum_fusion.1), channel_id=1, source_target_pairs={{0,4},{4,8},{8,12},{1,5},{5,9},{9,13},{2,6},{6,10},{10,14},{3,7},{... | collective-permute-start | bytes 786440 | tf_op jit(solution)/shard_map/ppermute | solution.py:48
  15.0 11.7 %slice-start = ((s8[8388608]{0:T(1024)(128)(4,1)}), s8[4194304]{0:T(1024)(128)(4,1)S(1)}, s32[]{:S(2)}) async-start(s8[8388608]{0:T(1024)(128)(4,1)} %bitcast.23), calls=%async_computation.2 | async-start | bytes 8388608
  15.1 11.7 %slice-start.1 = ((s8[8388608]{0:T(1024)(128)(4,1)}), s8[4194304]{0:T(1024)(128)(4,1)S(1)}, s32[]{:S(2)}) async-start(s8[8388608]{0:T(1024)(128)(4,1)} %bitcast.23), calls=%async_computation.3 | async-start | bytes 8388608
  15.1 28.5 %collective-permute-start.1 = (f32[2,32,4,256]{3,2,1,0:T(4,128)S(1)}, f32[2,32,4,256]{3,2,1,0:T(4,128)S(1)}, u32[]{:S(2)}, u32[]{:S(2)}) collective-permute-start(f32[2,32,4,256]{3,2,1,0:T(4,128)S(1)} %pad_maximum_fusion.2), channel_id=1, source_target_pairs={{4,0},{8,4},{12,8},{5,1},{9,5},{13,9},{6,2},{10,6},{14,10},{7,3},{... | collective-permute-start | bytes 786440 | tf_op jit(solution)/shard_map/ppermute | solution.py:49
  44.5 10.6 %collective-permute-start.3 = (f32[2,32,4,264]{3,1,2,0:T(8,128)S(1)}, f32[2,32,4,264]{3,1,2,0:T(8,128)S(1)}, u32[]{:S(2)}, u32[]{:S(2)}) collective-permute-start(f32[2,32,4,264]{3,1,2,0:T(8,128)S(1)} %maximum_bitcast_fusion.1), channel_id=1, source_target_pairs={{0,1},{1,2},{2,3},{4,5},{5,6},{6,7},{8,9},{9,10},{10,11},{12,13},{... | collective-permute-start | bytes 811016 | tf_op jit(solution)/shard_map/ppermute | solution.py:54
  49.4 10.7 %collective-permute-start.2 = (f32[2,32,4,264]{3,1,2,0:T(8,128)S(1)}, f32[2,32,4,264]{3,1,2,0:T(8,128)S(1)}, u32[]{:S(2)}, u32[]{:S(2)}) collective-permute-start(f32[2,32,4,264]{3,1,2,0:T(8,128)S(1)} %maximum_bitcast_fusion), channel_id=1, source_target_pairs={{1,0},{2,1},{3,2},{5,4},{6,5},{7,6},{9,8},{10,9},{11,10},{13,12},{... | collective-permute-start | bytes 811016 | tf_op jit(solution)/shard_map/ppermute | solution.py:55
Sparse Core Ops, SparseCore 0:
  254.6 94.0 reduce-scatter.1

commit v3 on v2

--- a/solution.py
+++ b/solution.py
@@ -33,6 +33,11 @@
 def _open_and_c(src, obs):
     open_cells = (1 - obs).astype(jnp.float32)
     return jnp.stack([src * open_cells, open_cells])
+
+
+def _select(count, width, picks):
+    cols = jnp.asarray(picks, jnp.int32)[:, None]
+    return (lax.broadcasted_iota(jnp.int32, (count, width), 1) == cols).astype(jnp.float32)
 
 
 def ghost_pieces(src, obs):
@@ -43,22 +48,25 @@
     bx = [(i + 1, i) for i in range(gxn - 1)]
     fy = [(i, i + 1) for i in range(gyn - 1)]
     by = [(i + 1, i) for i in range(gyn - 1)]
+    hi = lax.Precision.HIGHEST
     last_rows = _open_and_c(src[:, nx - H:, :], obs[:, nx - H:, :])
     first_rows = _open_and_c(src[:, :H, :], obs[:, :H, :])
     xlo = lax.ppermute(last_rows, "gx", fx)
     xhi = lax.ppermute(first_rows, "gx", bx)
-    last_cols = _open_and_c(src[:, :, ny - H:], obs[:, :, ny - H:])
-    first_cols = _open_and_c(src[:, :, :H], obs[:, :, :H])
-    ext_last = jnp.concatenate([xlo[..., ny - H:], last_cols, xhi[..., ny - H:]], axis=2)
-    ext_first = jnp.concatenate([xlo[..., :H], first_cols, xhi[..., :H]], axis=2)
-    yw = lax.ppermute(jnp.swapaxes(ext_last, -1, -2), "gy", fy)
-    ye = lax.ppermute(jnp.swapaxes(ext_first, -1, -2), "gy", by)
-    yw = jnp.swapaxes(yw, -1, -2)
-    ye = jnp.swapaxes(ye, -1, -2)
+    pick = _select(2 * H, ny, list(range(H)) + list(range(ny - H, ny)))
+    src_cols = jnp.einsum("zxy,ky->zkx", src, pick, precision=hi)
+    open_cols = jnp.einsum("zxy,ky->zkx", (1 - obs).astype(jnp.float32), pick, precision=hi)
+    cols = jnp.stack([src_cols * open_cols, open_cols])
+    corner_lo = jnp.swapaxes(jnp.concatenate([xlo[..., :H], xlo[..., ny - H:]], -1), -1, -2)
+    corner_hi = jnp.swapaxes(jnp.concatenate([xhi[..., :H], xhi[..., ny - H:]], -1), -1, -2)
+    ext = jnp.concatenate([corner_lo, cols, corner_hi], axis=-1)
+    yw = lax.ppermute(ext[:, :, H:], "gy", fy)
+    ye = lax.ppermute(ext[:, :, :H], "gy", by)
     rows = nx + 2 * PAD
-    mid = jnp.zeros(ye.shape[:-1] + (EXTRA - 2 * H,), jnp.float32)
-    lanes = jnp.concatenate([ye, mid, yw], axis=-1)
-    lanes = jnp.pad(lanes, ((0, 0), (0, 0), (PAD - H, rows - nx - PAD - H), (0, 0)))
+    yt = jnp.concatenate([ye, yw], axis=2)
+    yt = jnp.pad(yt, ((0, 0), (0, 0), (0, 0), (PAD - H, rows - nx - PAD - H)))
+    place = _select(2 * H, EXTRA, list(range(H)) + list(range(EXTRA - H, EXTRA)))
+    lanes = jnp.einsum("czkr,kj->czrj", yt, place, precision=hi)
     r_lo = jnp.pad(xlo, ((0, 0), (0, 0), (PAD - H, 0), (0, 0)))
     r_hi = jnp.pad(xhi, ((0, 0), (0, 0), (0, PAD - H), (0, 0)))
     return r_lo, r_hi, lanes
@@ -146,13 +154,9 @@
                     low = src[zl, pl.ds(r, RB), :]
                     o = o_buf[z, pl.ds(r, RB), :]
                     new = o * (
-                        k0 * cur
-                        + k_w * west
-                        + k_e * east
-                        + k_s * south
-                        + k_n * north
-                        + ku * up
-                        + diffusion * low
+                        (k0 * cur + k_w * west)
+                        + (k_e * east + k_s * south)
+                        + ((k_n * north + ku * up) + diffusion * low)
                     )
                     dst[z, pl.ds(r, RB), :] = new
                     if acc:
@@ -232,7 +236,9 @@
         ],
         compiler_params=pltpu.CompilerParams(vmem_limit_bytes=62 * 1024 * 1024),
     )(coef, source, obstacle, r_lo, r_hi, lanes)
-    return lax.psum_scatter(weighted, "scen", scatter_dimension=0, tiled=True)
+    count = lax.axis_size("scen")
+    parts = weighted.reshape(count, RZ // count, nx, ny)
+    return lax.all_to_all(parts, "scen", 0, 0, tiled=True).sum(0)
 
 
 def solution(mesh):

time: 356 us -> 272 us (0.76)
  waiting for transfers between devices: 94.3 us -> 1.42 us
  blocking collectives: 0 us -> 54.2 us
  local copies, waits for them, and re-layouts: 35.2 us -> 4.15 us
  matrix products: 0 us -> 22 us
  other arithmetic: 28.6 us -> 7.27 us
  between operations: 15.1 us -> 1.62 us
    reduce_scatter x1 -> x0, waiting for transfers between devices: 94.2 us -> none  [on_device(): return lax.psum_scatter(weighted, 'scen', scatter_dimension=0, tiled=True)]
    all_to_all x0 -> x1, blocking collectives: none -> 54.2 us  [on_device(): return lax.all_to_all(parts, 'scen', 0, 0, tiled=True).sum(0)]
    dot_general x0 -> x3, matrix products: none -> 22 us  [the longest x1 10.4 us: ghost_pieces(): lanes = jnp.einsum('czkr,kj->czrj', yt, place, precision=hi)]
    another operation x6 -> x4, other arithmetic: 16.5 us -> 3.34 us  [_open_and_c(): return jnp.stack([src * open_cells, open_cells])]
    another operation x4 -> x0, local copies, waits for them, and re-layouts: 11.4 us -> none  [_open_and_c(): return jnp.stack([src * open_cells, open_cells])]
    concatenate x1, other arithmetic: 11.7 us -> 0.34 us  [ghost_pieces(): ext = jnp.concatenate([corner_lo, cols, corner_hi], axis=-1)]
    ppermute x2 -> x0, local copies, waits for them, and re-layouts: 9.91 us -> none  [the longest x1 4.96 us: ghost_pieces(): yw = lax.ppermute(jnp.swapaxes(ext_last, -1, -2), 'gy', fy)]
    pad x1 -> x0, local copies, waits for them, and re-layouts: 8.49 us -> none  [ghost_pieces(): jnp.pad(lanes, ((0, 0), (0, 0), (PAD - H, rows - nx - PAD - H), (0, 0)))]
  transfers between devices with their start and end apart: 5 -> 4, of which waited for: 1 -> 1; matrix products, arithmetic and copies ran while one was open for 10% -> 6% of each run, Pallas kernels for 0% -> 0%
where the time goes in v3:
time: 272 us; the launch traced here: 271 us
  Pallas kernels  167 us (61%)
  blocking collectives  54.2 us (20%)
  matrix products  22 us (8%)
  starting transfers between devices  13.6 us (5%)
  other arithmetic  7.27 us (3%)
  local copies, waits for them, and re-layouts  4.15 us (2%)
    pallas_call x1, Pallas kernels, on_device(): pl.pallas_call(make_kernel(nz, nx, ny, RZ), out_shape=jax.ShapeDtypeStruc...  167 us
    all_to_all x1, blocking collectives, on_device(): return lax.all_to_all(parts, 'scen', 0, 0, tiled=True).sum(0)  54.2 us
    dot_general x1, matrix products, ghost_pieces(): lanes = jnp.einsum('czkr,kj->czrj', yt, place, precision=hi)  10.4 us
    dot_general x1, matrix products, ghost_pieces(): jnp.einsum('zxy,ky->zkx', (1 - obs).astype(jnp.float32), pick, precision=hi)  7.7 us
    ppermute x1, starting transfers between devices, ghost_pieces(): xlo = lax.ppermute(last_rows, 'gx', fx)  6.03 us
  transfers between devices with their start and end apart: 4, of which 1 were waited for; matrix products, arithmetic and copies ran while one was open for 6% of the time, Pallas kernels for 0%

profile of v3, /device:TPU:1, one launch (start us, length us, event | category | flops | bytes accessed | tf_op | source)
XLA Modules:
  0.0 271.4 jit_solution(10660392188241380984)
XLA Ops:
  0.0 1.2 convert_bitcast_fusion
  1.2 2.0 fusion.15
  3.3 6.0 %collective-permute-start = (f32[2,32,4,256]{3,2,1,0:T(4,128)S(1)}, f32[2,32,4,256]{3,2,1,0:T(4,128)S(1)}, u32[]{:S(2)}, u32[]{:S(2)}) collective-permute-start(f32[2,32,4,256]{3,2,1,0:T(4,128)S(1)} %pad_maximum_fusion.1), channel_id=1, source_target_pairs={{0,4},{4,8},{8,12},{1,5},{5,9},{9,13},{2,6},{6,10},{10,14},{3,7},{... | collective-permute-start | bytes 786440 | tf_op jit(solution)/shard_map/ppermute | solution.py:54
  9.4 1.9 collective-permute-start.1
  11.3 7.7 %fusion = f32[8,32,256]{2,0,1:T(8,128)S(1)} fusion(s32[32,256,256]{2,1,0:T(8,128)} %obs_hbm.1, s32[8]{0:T(128)} %constant.34.clone), kind=kOutput, calls=%fused_computation | convolution fusion | flops 205522944 | bytes 8650784 | tf_op jit(solution)/shard_map/zxy,ky->zkx/dot_general | solution.py:58
  19.1 3.9 %fusion.5 = f32[1,32,8,256]{3,2,1,0:T(8,128)S(1)} fusion(f32[8,32,256]{2,0,1:T(8,128)S(1)} %fusion, s32[8]{0:T(128)S(1)} %copy-done.1, f32[1,32,256,256]{3,2,1,0:T(8,128)S(1)} %copy-done), kind=kOutput, calls=%fused_computation.8 | convolution fusion | flops 201394176 | bytes 8912928 | tf_op jit(solution)/shard_map/zxy,ky->zkx/dot_general | solution.py:57
  22.9 0.1 fusion.32
  23.1 0.1 maximum_bitcast_fusion
  23.2 0.4 copy.15
  23.7 0.1 fusion.33
  23.8 0.1 maximum_bitcast_fusion.1
  24.0 0.4 copy.16
  24.4 0.3 pad_maximum_fusion
  24.8 0.1 fusion.31
  24.9 1.3 collective-permute-start.2
  26.2 4.4 %collective-permute-start.3 = (f32[2,32,4,264]{3,2,1,0:T(4,128)S(1)}, f32[2,32,4,264]{3,2,1,0:T(4,128)S(1)}, u32[]{:S(2)}, u32[]{:S(2)}) collective-permute-start(f32[2,32,4,264]{3,2,1,0:T(4,128)S(1)} %get-tuple-element.10), channel_id=1, source_target_pairs={{0,1},{1,2},{2,3},{4,5},{5,6},{6,7},{8,9},{9,10},{10,11},{12,13},{... | collective-permute-start | bytes 811016 | tf_op jit(solution)/shard_map/ppermute | solution.py:63
  32.1 0.6 stack.55.coef
  32.7 1.1 pad.13.rhi_hbm
  33.8 1.1 pad.12.rlo_hbm
  34.9 1.4 collective-permute-done.3
  36.3 10.4 %fusion.6.lanes_hbm = f32[2,32,288,128]{3,2,1,0:T(8,128)} fusion(f32[2,32,4,264]{3,2,1,0:T(4,128)S(1)} %collective-permute-done.3, f32[2,32,4,264]{3,2,1,0:T(4,128)S(1)} %collective-permute-done.2, s32[8]{0:T(128)S(1)} %copy-done.2), kind=kOutput, calls=%fused_computation.10 | convolution fusion | flops 227378176 | bytes 9977888 | tf_op jit(solution)/shard_map/czkr,kj->czrj/dot_general | solution.py:69
  46.8 167.1 %shard_map.64 = f32[16,256,256]{2,1,0:T(8,128)} custom-call(f32[8]{0:T(128)} %stack.55.coef, f32[1,32,256,256]{3,2,1,0:T(8,128)} %src_hbm.1, s32[32,256,256]{2,1,0:T(8,128)} %obs_hbm.1, f32[2,32,16,256]{3,2,1,0:T(8,128)} %pad.12.rlo_hbm, f32[2,32,16,256]{3,2,1,0:T(8,128)} %pad.13.rhi_hbm, f32[2,32,288,128]{3,2,1,0:T(8,128)} %fusion.6.lanes_hbm), custom_call_target="tpu_custom_call" | custom-call | tf_op jit(solution)/shard_map/pallas_call | solution.py:225
  213.9 54.2 %all_to_all.5 = f32[8,2,256,256]{3,2,1,0:T(8,128)} all-to-all(f32[8,2,256,256]{3,2,1,0:T(8,128)} %bitcast.38), channel_id=1, replica_groups=mesh['scen'=8,'gx'=4,'gy'=4] {'scen'}, dimensions={0} | all-to-all | bytes 8388608 | tf_op jit(solution)/shard_map/all_to_all | solution.py:241
  268.1 3.3 %reduce_sum.9 = f32[2,256,256]{2,1,0:T(8,128)} reduce(f32[8,2,256,256]{3,2,1,0:T(8,128)} %all_to_all.5, f32[]{:T(128)} %constant.10.clone.1), dimensions={0}, to_apply=%region_0.1 | reduce | flops 917504 | bytes 4718596 | tf_op jit(solution)/shard_map/reduce_sum | solution.py:241
  (11 shorter events, 0.1 us)
Async XLA Ops:
  0.0 19.0 %copy-start.1 = (s32[8]{0:T(128)S(1)}, s32[8]{0:T(128)}, u32[]{:S(2)}) copy-start(s32[8]{0:T(128)} %constant.34.clone) | copy-start | bytes 100
  0.0 19.0 %copy-start = (f32[1,32,256,256]{3,2,1,0:T(8,128)S(1)}, f32[1,32,256,256]{3,2,1,0:T(8,128)}, u32[]{:S(2)}) copy-start(f32[1,32,256,256]{3,2,1,0:T(8,128)} %src_hbm.1) | copy-start | bytes 25165828
  3.3 19.6 %collective-permute-start = (f32[2,32,4,256]{3,2,1,0:T(4,128)S(1)}, f32[2,32,4,256]{3,2,1,0:T(4,128)S(1)}, u32[]{:S(2)}, u32[]{:S(2)}) collective-permute-start(f32[2,32,4,256]{3,2,1,0:T(4,128)S(1)} %pad_maximum_fusion.1), channel_id=1, source_target_pairs={{0,4},{4,8},{8,12},{1,5},{5,9},{9,13},{2,6},{6,10},{10,14},{3,7},{... | collective-permute-start | bytes 786440 | tf_op jit(solution)/shard_map/ppermute | solution.py:54
  9.4 14.3 %collective-permute-start.1 = (f32[2,32,4,256]{3,2,1,0:T(4,128)S(1)}, f32[2,32,4,256]{3,2,1,0:T(4,128)S(1)}, u32[]{:S(2)}, u32[]{:S(2)}) collective-permute-start(f32[2,32,4,256]{3,2,1,0:T(4,128)S(1)} %pad_maximum_fusion.2), channel_id=1, source_target_pairs={{4,0},{8,4},{12,8},{5,1},{9,5},{13,9},{6,2},{10,6},{14,10},{7,3},{... | collective-permute-start | bytes 786440 | tf_op jit(solution)/shard_map/ppermute | solution.py:55
  19.0 17.3 %copy-start.2 = (s32[8]{0:T(128)S(1)}, s32[8]{0:T(128)}, u32[]{:S(2)}) copy-start(s32[8]{0:T(128)} %constant.35.clone) | copy-start | bytes 100
  24.9 10.0 %collective-permute-start.2 = (f32[2,32,4,264]{3,2,1,0:T(4,128)S(1)}, f32[2,32,4,264]{3,2,1,0:T(4,128)S(1)}, u32[]{:S(2)}, u32[]{:S(2)}) collective-permute-start(f32[2,32,4,264]{3,2,1,0:T(4,128)S(1)} %get-tuple-element.9), channel_id=1, source_target_pairs={{1,0},{2,1},{3,2},{5,4},{6,5},{7,6},{9,8},{10,9},{11,10},{13,12},{... | collective-permute-start | bytes 811016 | tf_op jit(solution)/shard_map/ppermute | solution.py:64
  26.2 10.1 %collective-permute-start.3 = (f32[2,32,4,264]{3,2,1,0:T(4,128)S(1)}, f32[2,32,4,264]{3,2,1,0:T(4,128)S(1)}, u32[]{:S(2)}, u32[]{:S(2)}) collective-permute-start(f32[2,32,4,264]{3,2,1,0:T(4,128)S(1)} %get-tuple-element.10), channel_id=1, source_target_pairs={{0,1},{1,2},{2,3},{4,5},{5,6},{6,7},{8,9},{9,10},{10,11},{12,13},{... | collective-permute-start | bytes 811016 | tf_op jit(solution)/shard_map/ppermute | solution.py:63

commit v4 on v3

--- a/solution.py
+++ b/solution.py
@@ -23,6 +23,7 @@
 PAD = 16
 EXTRA = 128
 RB = 8
+ROT_UNROLL = 34
 
 
 def wind_components(sector_id):
@@ -82,7 +83,7 @@
     acc_hi = (PAD + nx) // RB
 
     def kernel(coef, src_hbm, obs_hbm, rlo_hbm, rhi_hbm, lanes_hbm, out_ref,
-               a_buf, b_buf, o_buf, obs_buf, sems):
+               a_buf, b_buf, o_buf, obs_buf, sems, s_buf, n_buf):
         copies = [
             pltpu.make_async_copy(obs_hbm, obs_buf, sems.at[0]),
             pltpu.make_async_copy(rlo_hbm.at[1], o_buf.at[:, pl.ds(0, PAD), pl.ds(0, ny)], sems.at[1]),
@@ -131,9 +132,17 @@
         k0_first = coef[4]
         k0_rest = coef[5]
         weight = coef[6]
-        row_id = lax.broadcasted_iota(jnp.int32, (RB, width), 0)
+        npc = width // 128
+        nacc = ny // 128
+        row_id = lax.broadcasted_iota(jnp.int32, (RB, 128), 0)
+        lane_id = lax.broadcasted_iota(jnp.int32, (RB, 128), 1)
         first_row = row_id == 0
         last_row = row_id == RB - 1
+        first_lane = lane_id == 0
+        last_lane = lane_id == 127
+
+        def pieces(ref, z, r):
+            return tuple(ref[z, pl.ds(r, RB), pl.ds(128 * k, 128)] for k in range(npc))
 
         def step(src, dst, first):
             def level(z, accumulate):
@@ -142,33 +151,51 @@
                 k0 = jnp.where(z == 0, k0_first, k0_rest)
                 ku = jnp.where(z == nz - 1, 0.0, diffusion + settling).astype(jnp.float32)
 
+                def rot(b, c):
+                    r = pl.multiple_of(b * RB, RB)
+                    cur = pieces(src, z, r)
+                    right = tuple(pltpu.roll(v, 1, 1) for v in cur)
+                    left = tuple(pltpu.roll(v, 127, 1) for v in cur)
+                    for k in range(npc):
+                        s_buf[pl.ds(r, RB), pl.ds(128 * k, 128)] = jnp.where(
+                            first_lane, right[(k - 1) % npc], right[k])
+                        n_buf[pl.ds(r, RB), pl.ds(128 * k, 128)] = jnp.where(
+                            last_lane, left[(k + 1) % npc], left[k])
+                    return c
+
+                lax.fori_loop(b_first, b_last + 1, rot, 0, unroll=ROT_UNROLL)
+
                 def blk(b, carry, acc):
                     prev, cur = carry
                     r = pl.multiple_of(b * RB, RB)
-                    nxt = src[z, pl.ds(r + RB, RB), :]
-                    west = jnp.where(first_row, pltpu.roll(prev, 1, 0), pltpu.roll(cur, 1, 0))
-                    east = jnp.where(last_row, pltpu.roll(nxt, RB - 1, 0), pltpu.roll(cur, RB - 1, 0))
-                    south = pltpu.roll(cur, 1, 1)
-                    north = pltpu.roll(cur, width - 1, 1)
-                    up = src[zu, pl.ds(r, RB), :]
-                    low = src[zl, pl.ds(r, RB), :]
-                    o = o_buf[z, pl.ds(r, RB), :]
-                    new = o * (
-                        (k0 * cur + k_w * west)
-                        + (k_e * east + k_s * south)
-                        + ((k_n * north + ku * up) + diffusion * low)
-                    )
-                    dst[z, pl.ds(r, RB), :] = new
-                    if acc:
-                        inner = new[:, :ny]
-                        ro = pl.multiple_of(r - PAD, RB)
-                        if first:
-                            out_ref[z, pl.ds(ro, RB), :] = inner * inner
-                        else:
-                            out_ref[z, pl.ds(ro, RB), :] = out_ref[z, pl.ds(ro, RB), :] + inner * inner
+                    nxt = pieces(src, z, r + RB)
+                    up = pieces(src, zu, r)
+                    low = pieces(src, zl, r)
+                    o = pieces(o_buf, z, r)
+                    ro = pl.multiple_of(r - PAD, RB)
+                    for k in range(npc):
+                        c = cur[k]
+                        west = jnp.where(first_row, pltpu.roll(prev[k], 1, 0), pltpu.roll(c, 1, 0))
+                        east = jnp.where(last_row, pltpu.roll(nxt[k], RB - 1, 0), pltpu.roll(c, RB - 1, 0))
+                        south = s_buf[pl.ds(r, RB), pl.ds(128 * k, 128)]
+                        north = n_buf[pl.ds(r, RB), pl.ds(128 * k, 128)]
+                        new = o[k] * (
+                            (k0 * c + k_w * west)
+                            + (k_e * east + k_s * south)
+                            + ((k_n * north + ku * up[k]) + diffusion * low[k])
+                        )
+                        dst[z, pl.ds(r, RB), pl.ds(128 * k, 128)] = new
+                        if acc and k < nacc:
+                            sq = new * new
+                            if first:
+                                out_ref[z, pl.ds(ro, RB), pl.ds(128 * k, 128)] = sq
+                            else:
+                                out_ref[z, pl.ds(ro, RB), pl.ds(128 * k, 128)] = (
+                                    out_ref[z, pl.ds(ro, RB), pl.ds(128 * k, 128)] + sq
+                                )
                     return (cur, nxt)
 
-                carry = (src[z, pl.ds(0, RB), :], src[z, pl.ds(RB, RB), :])
+                carry = (pieces(src, z, 0), pieces(src, z, RB))
                 if accumulate:
                     carry = lax.fori_loop(b_first, acc_lo, lambda b, c: blk(b, c, False), carry)
                     carry = lax.fori_loop(acc_lo, acc_hi, lambda b, c: blk(b, c, True), carry, unroll=4)
@@ -233,6 +260,8 @@
             pltpu.VMEM((nz, rows, width), jnp.float32),
             pltpu.VMEM((nz, nx, ny), jnp.int32),
             pltpu.SemaphoreType.DMA((8,)),
+            pltpu.VMEM((rows, width), jnp.float32),
+            pltpu.VMEM((rows, width), jnp.float32),
         ],
         compiler_params=pltpu.CompilerParams(vmem_limit_bytes=62 * 1024 * 1024),
     )(coef, source, obstacle, r_lo, r_hi, lanes)

time: 272 us -> 198 us (0.73)
  Pallas kernels: 167 us -> 92.8 us
    pallas_call x1, Pallas kernels: 167 us -> 92.8 us  [on_device(): pl.pallas_call(make_kernel(nz, nx, ny, RZ), out_shape=jax.ShapeDtypeStruc...]
  transfers between devices with their start and end apart: 4 -> 4, of which waited for: 1 -> 1; matrix products, arithmetic and copies ran while one was open for 6% -> 8% of each run, Pallas kernels for 0% -> 0%
where the time goes in v4:
time: 198 us; the launch traced here: 197 us
  Pallas kernels  92.8 us (47%)
  blocking collectives  54.2 us (27%)
  matrix products  22 us (11%)
  starting transfers between devices  13.6 us (7%)
  other arithmetic  7.27 us (4%)
  local copies, waits for them, and re-layouts  4.15 us (2%)
    pallas_call x1, Pallas kernels, on_device(): pl.pallas_call(make_kernel(nz, nx, ny, RZ), out_shape=jax.ShapeDtypeStruc...  92.8 us
    all_to_all x1, blocking collectives, on_device(): return lax.all_to_all(parts, 'scen', 0, 0, tiled=True).sum(0)  54.2 us
    dot_general x1, matrix products, ghost_pieces(): lanes = jnp.einsum('czkr,kj->czrj', yt, place, precision=hi)  10.4 us
    dot_general x1, matrix products, ghost_pieces(): jnp.einsum('zxy,ky->zkx', (1 - obs).astype(jnp.float32), pick, precision=hi)  7.7 us
    ppermute x1, starting transfers between devices, ghost_pieces(): xlo = lax.ppermute(last_rows, 'gx', fx)  6.03 us
    ppermute x1, starting transfers between devices, ghost_pieces(): yw = lax.ppermute(ext[:, :, H:], 'gy', fy)  4.37 us
  transfers between devices with their start and end apart: 4, of which 1 were waited for; matrix products, arithmetic and copies ran while one was open for 8% of the time, Pallas kernels for 0%

profile of v4, /device:TPU:1, one launch (start us, length us, event | category | flops | bytes accessed | tf_op | source)
XLA Modules:
  0.0 197.0 jit_solution(14769547376236946388)
XLA Ops:
  0.0 1.2 convert_bitcast_fusion
  1.2 2.0 %fusion.15 = (f32[1,32,4,256]{3,2,1,0:T(4,128)S(1)}, f32[1,32,4,256]{3,2,1,0:T(4,128)S(1)}) fusion(f32[32,256,256]{2,1,0:T(8,128)} %bitcast.37, s32[32,256,256]{2,1,0:T(8,128)} %obs_hbm.1), kind=kLoop, calls=%fused_computation.22 | loop fusion | flops 196608 | bytes 786432 | tf_op jit(solution)/shard_map/stack | solution.py:36
  3.3 6.0 %collective-permute-start = (f32[2,32,4,256]{3,2,1,0:T(4,128)S(1)}, f32[2,32,4,256]{3,2,1,0:T(4,128)S(1)}, u32[]{:S(2)}, u32[]{:S(2)}) collective-permute-start(f32[2,32,4,256]{3,2,1,0:T(4,128)S(1)} %pad_maximum_fusion.1), channel_id=1, source_target_pairs={{0,4},{4,8},{8,12},{1,5},{5,9},{9,13},{2,6},{6,10},{10,14},{3,7},{... | collective-permute-start | bytes 786440 | tf_op jit(solution)/shard_map/ppermute | solution.py:55
  9.4 1.9 collective-permute-start.1
  11.3 7.7 %fusion = f32[8,32,256]{2,0,1:T(8,128)S(1)} fusion(s32[32,256,256]{2,1,0:T(8,128)} %obs_hbm.1, s32[8]{0:T(128)} %constant.34.clone), kind=kOutput, calls=%fused_computation | convolution fusion | flops 205522944 | bytes 8650784 | tf_op jit(solution)/shard_map/zxy,ky->zkx/dot_general | solution.py:59
  19.1 3.9 %fusion.5 = f32[1,32,8,256]{3,2,1,0:T(8,128)S(1)} fusion(f32[8,32,256]{2,0,1:T(8,128)S(1)} %fusion, s32[8]{0:T(128)S(1)} %copy-done.1, f32[1,32,256,256]{3,2,1,0:T(8,128)S(1)} %copy-done), kind=kOutput, calls=%fused_computation.8 | convolution fusion | flops 201394176 | bytes 8912928 | tf_op jit(solution)/shard_map/zxy,ky->zkx/dot_general | solution.py:58
  22.9 0.1 fusion.32
  23.1 0.1 maximum_bitcast_fusion
  23.2 0.4 copy.15
  23.7 0.1 fusion.33
  23.8 0.1 maximum_bitcast_fusion.1
  24.0 0.4 copy.16
  24.4 0.3 pad_maximum_fusion
  24.8 0.1 fusion.31
  24.9 1.3 collective-permute-start.2
  26.2 4.4 %collective-permute-start.3 = (f32[2,32,4,264]{3,2,1,0:T(4,128)S(1)}, f32[2,32,4,264]{3,2,1,0:T(4,128)S(1)}, u32[]{:S(2)}, u32[]{:S(2)}) collective-permute-start(f32[2,32,4,264]{3,2,1,0:T(4,128)S(1)} %get-tuple-element.10), channel_id=1, source_target_pairs={{0,1},{1,2},{2,3},{4,5},{5,6},{6,7},{8,9},{9,10},{10,11},{12,13},{... | collective-permute-start | bytes 811016 | tf_op jit(solution)/shard_map/ppermute | solution.py:64
  32.1 0.6 stack.55.coef
  32.7 1.1 pad.13.rhi_hbm
  33.8 1.1 pad.12.rlo_hbm
  34.9 1.4 collective-permute-done.3
  36.3 10.4 %fusion.6.lanes_hbm = f32[2,32,288,128]{3,2,1,0:T(8,128)} fusion(f32[2,32,4,264]{3,2,1,0:T(4,128)S(1)} %collective-permute-done.3, f32[2,32,4,264]{3,2,1,0:T(4,128)S(1)} %collective-permute-done.2, s32[8]{0:T(128)S(1)} %copy-done.2), kind=kOutput, calls=%fused_computation.10 | convolution fusion | flops 227378176 | bytes 9977888 | tf_op jit(solution)/shard_map/czkr,kj->czrj/dot_general | solution.py:70
  46.8 92.8 %shard_map.64 = f32[16,256,256]{2,1,0:T(8,128)} custom-call(f32[8]{0:T(128)} %stack.55.coef, f32[1,32,256,256]{3,2,1,0:T(8,128)} %src_hbm.1, s32[32,256,256]{2,1,0:T(8,128)} %obs_hbm.1, f32[2,32,16,256]{3,2,1,0:T(8,128)} %pad.12.rlo_hbm, f32[2,32,16,256]{3,2,1,0:T(8,128)} %pad.13.rhi_hbm, f32[2,32,288,128]{3,2,1,0:T(8,128)} %fusion.6.lanes_hbm), custom_call_target="tpu_custom_call" | custom-call | tf_op jit(solution)/shard_map/pallas_call | solution.py:252
  139.5 54.2 %all_to_all.5 = f32[8,2,256,256]{3,2,1,0:T(8,128)} all-to-all(f32[8,2,256,256]{3,2,1,0:T(8,128)} %bitcast.38), channel_id=1, replica_groups=mesh['scen'=8,'gx'=4,'gy'=4] {'scen'}, dimensions={0} | all-to-all | bytes 8388608 | tf_op jit(solution)/shard_map/all_to_all | solution.py:270
  193.7 3.3 %reduce_sum.9 = f32[2,256,256]{2,1,0:T(8,128)} reduce(f32[8,2,256,256]{3,2,1,0:T(8,128)} %all_to_all.5, f32[]{:T(128)} %constant.10.clone.1), dimensions={0}, to_apply=%region_0.1 | reduce | flops 917504 | bytes 4718596 | tf_op jit(solution)/shard_map/reduce_sum | solution.py:270
  (11 shorter events, 0.1 us)
Async XLA Ops:
  0.0 19.0 %copy-start.1 = (s32[8]{0:T(128)S(1)}, s32[8]{0:T(128)}, u32[]{:S(2)}) copy-start(s32[8]{0:T(128)} %constant.34.clone) | copy-start | bytes 100
  0.0 19.0 %copy-start = (f32[1,32,256,256]{3,2,1,0:T(8,128)S(1)}, f32[1,32,256,256]{3,2,1,0:T(8,128)}, u32[]{:S(2)}) copy-start(f32[1,32,256,256]{3,2,1,0:T(8,128)} %src_hbm.1) | copy-start | bytes 25165828
  3.3 19.6 %collective-permute-start = (f32[2,32,4,256]{3,2,1,0:T(4,128)S(1)}, f32[2,32,4,256]{3,2,1,0:T(4,128)S(1)}, u32[]{:S(2)}, u32[]{:S(2)}) collective-permute-start(f32[2,32,4,256]{3,2,1,0:T(4,128)S(1)} %pad_maximum_fusion.1), channel_id=1, source_target_pairs={{0,4},{4,8},{8,12},{1,5},{5,9},{9,13},{2,6},{6,10},{10,14},{3,7},{... | collective-permute-start | bytes 786440 | tf_op jit(solution)/shard_map/ppermute | solution.py:55
  9.4 14.3 %collective-permute-start.1 = (f32[2,32,4,256]{3,2,1,0:T(4,128)S(1)}, f32[2,32,4,256]{3,2,1,0:T(4,128)S(1)}, u32[]{:S(2)}, u32[]{:S(2)}) collective-permute-start(f32[2,32,4,256]{3,2,1,0:T(4,128)S(1)} %pad_maximum_fusion.2), channel_id=1, source_target_pairs={{4,0},{8,4},{12,8},{5,1},{9,5},{13,9},{6,2},{10,6},{14,10},{7,3},{... | collective-permute-start | bytes 786440 | tf_op jit(solution)/shard_map/ppermute | solution.py:56
  19.0 17.3 %copy-start.2 = (s32[8]{0:T(128)S(1)}, s32[8]{0:T(128)}, u32[]{:S(2)}) copy-start(s32[8]{0:T(128)} %constant.35.clone) | copy-start | bytes 100
  24.9 10.0 %collective-permute-start.2 = (f32[2,32,4,264]{3,2,1,0:T(4,128)S(1)}, f32[2,32,4,264]{3,2,1,0:T(4,128)S(1)}, u32[]{:S(2)}, u32[]{:S(2)}) collective-permute-start(f32[2,32,4,264]{3,2,1,0:T(4,128)S(1)} %get-tuple-element.9), channel_id=1, source_target_pairs={{1,0},{2,1},{3,2},{5,4},{6,5},{7,6},{9,8},{10,9},{11,10},{13,12},{... | collective-permute-start | bytes 811016 | tf_op jit(solution)/shard_map/ppermute | solution.py:65
  26.2 10.1 %collective-permute-start.3 = (f32[2,32,4,264]{3,2,1,0:T(4,128)S(1)}, f32[2,32,4,264]{3,2,1,0:T(4,128)S(1)}, u32[]{:S(2)}, u32[]{:S(2)}) collective-permute-start(f32[2,32,4,264]{3,2,1,0:T(4,128)S(1)} %get-tuple-element.10), channel_id=1, source_target_pairs={{0,1},{1,2},{2,3},{4,5},{5,6},{6,7},{8,9},{9,10},{10,11},{12,13},{... | collective-permute-start | bytes 811016 | tf_op jit(solution)/shard_map/ppermute | solution.py:64

commit v5 on v4

--- a/solution.py
+++ b/solution.py
@@ -24,6 +24,8 @@
 EXTRA = 128
 RB = 8
 ROT_UNROLL = 34
+ACC_UNROLL = 32
+PLAIN_UNROLL = 34
 
 
 def wind_components(sector_id):
@@ -198,10 +200,10 @@
                 carry = (pieces(src, z, 0), pieces(src, z, RB))
                 if accumulate:
                     carry = lax.fori_loop(b_first, acc_lo, lambda b, c: blk(b, c, False), carry)
-                    carry = lax.fori_loop(acc_lo, acc_hi, lambda b, c: blk(b, c, True), carry, unroll=4)
+                    carry = lax.fori_loop(acc_lo, acc_hi, lambda b, c: blk(b, c, True), carry, unroll=ACC_UNROLL)
                     carry = lax.fori_loop(acc_hi, b_last + 1, lambda b, c: blk(b, c, False), carry)
                 else:
-                    carry = lax.fori_loop(b_first, b_last + 1, lambda b, c: blk(b, c, False), carry, unroll=2)
+                    carry = lax.fori_loop(b_first, b_last + 1, lambda b, c: blk(b, c, False), carry, unroll=PLAIN_UNROLL)
 
             def lvl_acc(z, c):
                 level(z, True)

time: 198 us -> 160 us (0.81)
  Pallas kernels: 92.8 us -> 54.8 us
    pallas_call x1, Pallas kernels: 92.8 us -> 54.8 us  [on_device(): pl.pallas_call(make_kernel(nz, nx, ny, RZ), out_shape=jax.ShapeDtypeStruc...]
  transfers between devices with their start and end apart: 4 -> 4, of which waited for: 1 -> 1; matrix products, arithmetic and copies ran while one was open for 8% -> 10% of each run, Pallas kernels for 0% -> 0%
where the time goes in v5:
time: 160 us; the launch traced here: 159 us
  Pallas kernels  54.8 us (34%)
  blocking collectives  54.2 us (34%)
  matrix products  22 us (14%)
  starting transfers between devices  13.6 us (8%)
  other arithmetic  7.27 us (5%)
  local copies, waits for them, and re-layouts  4.15 us (3%)
  between operations  1.62 us (1%)
    pallas_call x1, Pallas kernels, on_device(): pl.pallas_call(make_kernel(nz, nx, ny, RZ), out_shape=jax.ShapeDtypeStruc...  54.8 us
    all_to_all x1, blocking collectives, on_device(): return lax.all_to_all(parts, 'scen', 0, 0, tiled=True).sum(0)  54.2 us
    dot_general x1, matrix products, ghost_pieces(): lanes = jnp.einsum('czkr,kj->czrj', yt, place, precision=hi)  10.4 us
    dot_general x1, matrix products, ghost_pieces(): jnp.einsum('zxy,ky->zkx', (1 - obs).astype(jnp.float32), pick, precision=hi)  7.7 us
    ppermute x1, starting transfers between devices, ghost_pieces(): xlo = lax.ppermute(last_rows, 'gx', fx)  6.03 us
    ppermute x1, starting transfers between devices, ghost_pieces(): yw = lax.ppermute(ext[:, :, H:], 'gy', fy)  4.37 us
    dot_general x1, matrix products, ghost_pieces(): src_cols = jnp.einsum('zxy,ky->zkx', src, pick, precision=hi)  3.88 us
    another operation x4, other arithmetic, _open_and_c(): return jnp.stack([src * open_cells, open_cells])  3.34 us
  transfers between devices with their start and end apart: 4, of which 1 were waited for; matrix products, arithmetic and copies ran while one was open for 10% of the time, Pallas kernels for 0%

profile of v5, /device:TPU:1, one launch (start us, length us, event | category | flops | bytes accessed | tf_op | source)
XLA Modules:
  0.0 159.1 jit_solution(1385292977143440647)
XLA Ops:
  0.0 1.2 convert_bitcast_fusion
  1.2 2.0 %fusion.15 = (f32[1,32,4,256]{3,2,1,0:T(4,128)S(1)}, f32[1,32,4,256]{3,2,1,0:T(4,128)S(1)}) fusion(f32[32,256,256]{2,1,0:T(8,128)} %bitcast.37, s32[32,256,256]{2,1,0:T(8,128)} %obs_hbm.1), kind=kLoop, calls=%fused_computation.22 | loop fusion | flops 196608 | bytes 786432 | tf_op jit(solution)/shard_map/stack | solution.py:38
  3.3 6.0 %collective-permute-start = (f32[2,32,4,256]{3,2,1,0:T(4,128)S(1)}, f32[2,32,4,256]{3,2,1,0:T(4,128)S(1)}, u32[]{:S(2)}, u32[]{:S(2)}) collective-permute-start(f32[2,32,4,256]{3,2,1,0:T(4,128)S(1)} %pad_maximum_fusion.1), channel_id=1, source_target_pairs={{0,4},{4,8},{8,12},{1,5},{5,9},{9,13},{2,6},{6,10},{10,14},{3,7},{... | collective-permute-start | bytes 786440 | tf_op jit(solution)/shard_map/ppermute | solution.py:57
  9.4 1.9 %collective-permute-start.1 = (f32[2,32,4,256]{3,2,1,0:T(4,128)S(1)}, f32[2,32,4,256]{3,2,1,0:T(4,128)S(1)}, u32[]{:S(2)}, u32[]{:S(2)}) collective-permute-start(f32[2,32,4,256]{3,2,1,0:T(4,128)S(1)} %pad_maximum_fusion.2), channel_id=1, source_target_pairs={{4,0},{8,4},{12,8},{5,1},{9,5},{13,9},{6,2},{10,6},{14,10},{7,3},{... | collective-permute-start | bytes 786440 | tf_op jit(solution)/shard_map/ppermute | solution.py:58
  11.3 7.7 %fusion = f32[8,32,256]{2,0,1:T(8,128)S(1)} fusion(s32[32,256,256]{2,1,0:T(8,128)} %obs_hbm.1, s32[8]{0:T(128)} %constant.34.clone), kind=kOutput, calls=%fused_computation | convolution fusion | flops 205522944 | bytes 8650784 | tf_op jit(solution)/shard_map/zxy,ky->zkx/dot_general | solution.py:61
  19.1 3.9 %fusion.5 = f32[1,32,8,256]{3,2,1,0:T(8,128)S(1)} fusion(f32[8,32,256]{2,0,1:T(8,128)S(1)} %fusion, s32[8]{0:T(128)S(1)} %copy-done.1, f32[1,32,256,256]{3,2,1,0:T(8,128)S(1)} %copy-done), kind=kOutput, calls=%fused_computation.8 | convolution fusion | flops 201394176 | bytes 8912928 | tf_op jit(solution)/shard_map/zxy,ky->zkx/dot_general | solution.py:60
  22.9 0.1 fusion.32
  23.1 0.1 maximum_bitcast_fusion
  23.2 0.4 copy.15
  23.7 0.1 fusion.33
  23.8 0.1 maximum_bitcast_fusion.1
  24.0 0.4 copy.16
  24.4 0.3 pad_maximum_fusion
  24.8 0.1 fusion.31
  24.9 1.3 collective-permute-start.2
  26.2 4.4 %collective-permute-start.3 = (f32[2,32,4,264]{3,2,1,0:T(4,128)S(1)}, f32[2,32,4,264]{3,2,1,0:T(4,128)S(1)}, u32[]{:S(2)}, u32[]{:S(2)}) collective-permute-start(f32[2,32,4,264]{3,2,1,0:T(4,128)S(1)} %get-tuple-element.10), channel_id=1, source_target_pairs={{0,1},{1,2},{2,3},{4,5},{5,6},{6,7},{8,9},{9,10},{10,11},{12,13},{... | collective-permute-start | bytes 811016 | tf_op jit(solution)/shard_map/ppermute | solution.py:66
  32.1 0.6 stack.55.coef
  32.7 1.1 pad.13.rhi_hbm
  33.8 1.1 pad.12.rlo_hbm
  34.9 1.4 collective-permute-done.3
  36.3 10.4 %fusion.6.lanes_hbm = f32[2,32,288,128]{3,2,1,0:T(8,128)} fusion(f32[2,32,4,264]{3,2,1,0:T(4,128)S(1)} %collective-permute-done.3, f32[2,32,4,264]{3,2,1,0:T(4,128)S(1)} %collective-permute-done.2, s32[8]{0:T(128)S(1)} %copy-done.2), kind=kOutput, calls=%fused_computation.10 | convolution fusion | flops 227378176 | bytes 9977888 | tf_op jit(solution)/shard_map/czkr,kj->czrj/dot_general | solution.py:72
  46.8 54.8 %shard_map.64 = f32[16,256,256]{2,1,0:T(8,128)} custom-call(f32[8]{0:T(128)} %stack.55.coef, f32[1,32,256,256]{3,2,1,0:T(8,128)} %src_hbm.1, s32[32,256,256]{2,1,0:T(8,128)} %obs_hbm.1, f32[2,32,16,256]{3,2,1,0:T(8,128)} %pad.12.rlo_hbm, f32[2,32,16,256]{3,2,1,0:T(8,128)} %pad.13.rhi_hbm, f32[2,32,288,128]{3,2,1,0:T(8,128)} %fusion.6.lanes_hbm), custom_call_target="tpu_custom_call" | custom-call | tf_op jit(solution)/shard_map/pallas_call | solution.py:254
  101.6 54.2 %all_to_all.5 = f32[8,2,256,256]{3,2,1,0:T(8,128)} all-to-all(f32[8,2,256,256]{3,2,1,0:T(8,128)} %bitcast.38), channel_id=1, replica_groups=mesh['scen'=8,'gx'=4,'gy'=4] {'scen'}, dimensions={0} | all-to-all | bytes 8388608 | tf_op jit(solution)/shard_map/all_to_all | solution.py:272
  155.7 3.3 %reduce_sum.9 = f32[2,256,256]{2,1,0:T(8,128)} reduce(f32[8,2,256,256]{3,2,1,0:T(8,128)} %all_to_all.5, f32[]{:T(128)} %constant.10.clone.1), dimensions={0}, to_apply=%region_0.1 | reduce | flops 917504 | bytes 4718596 | tf_op jit(solution)/shard_map/reduce_sum | solution.py:272
  (11 shorter events, 0.1 us)
Async XLA Ops:
  0.0 19.0 %copy-start.1 = (s32[8]{0:T(128)S(1)}, s32[8]{0:T(128)}, u32[]{:S(2)}) copy-start(s32[8]{0:T(128)} %constant.34.clone) | copy-start | bytes 100
  0.0 19.0 %copy-start = (f32[1,32,256,256]{3,2,1,0:T(8,128)S(1)}, f32[1,32,256,256]{3,2,1,0:T(8,128)}, u32[]{:S(2)}) copy-start(f32[1,32,256,256]{3,2,1,0:T(8,128)} %src_hbm.1) | copy-start | bytes 25165828
  3.3 19.6 %collective-permute-start = (f32[2,32,4,256]{3,2,1,0:T(4,128)S(1)}, f32[2,32,4,256]{3,2,1,0:T(4,128)S(1)}, u32[]{:S(2)}, u32[]{:S(2)}) collective-permute-start(f32[2,32,4,256]{3,2,1,0:T(4,128)S(1)} %pad_maximum_fusion.1), channel_id=1, source_target_pairs={{0,4},{4,8},{8,12},{1,5},{5,9},{9,13},{2,6},{6,10},{10,14},{3,7},{... | collective-permute-start | bytes 786440 | tf_op jit(solution)/shard_map/ppermute | solution.py:57
  9.4 14.3 %collective-permute-start.1 = (f32[2,32,4,256]{3,2,1,0:T(4,128)S(1)}, f32[2,32,4,256]{3,2,1,0:T(4,128)S(1)}, u32[]{:S(2)}, u32[]{:S(2)}) collective-permute-start(f32[2,32,4,256]{3,2,1,0:T(4,128)S(1)} %pad_maximum_fusion.2), channel_id=1, source_target_pairs={{4,0},{8,4},{12,8},{5,1},{9,5},{13,9},{6,2},{10,6},{14,10},{7,3},{... | collective-permute-start | bytes 786440 | tf_op jit(solution)/shard_map/ppermute | solution.py:58
  19.0 17.3 %copy-start.2 = (s32[8]{0:T(128)S(1)}, s32[8]{0:T(128)}, u32[]{:S(2)}) copy-start(s32[8]{0:T(128)} %constant.35.clone) | copy-start | bytes 100
  24.9 10.0 %collective-permute-start.2 = (f32[2,32,4,264]{3,2,1,0:T(4,128)S(1)}, f32[2,32,4,264]{3,2,1,0:T(4,128)S(1)}, u32[]{:S(2)}, u32[]{:S(2)}) collective-permute-start(f32[2,32,4,264]{3,2,1,0:T(4,128)S(1)} %get-tuple-element.9), channel_id=1, source_target_pairs={{1,0},{2,1},{3,2},{5,4},{6,5},{7,6},{9,8},{10,9},{11,10},{13,12},{... | collective-permute-start | bytes 811016 | tf_op jit(solution)/shard_map/ppermute | solution.py:67
  26.2 10.1 %collective-permute-start.3 = (f32[2,32,4,264]{3,2,1,0:T(4,128)S(1)}, f32[2,32,4,264]{3,2,1,0:T(4,128)S(1)}, u32[]{:S(2)}, u32[]{:S(2)}) collective-permute-start(f32[2,32,4,264]{3,2,1,0:T(4,128)S(1)} %get-tuple-element.10), channel_id=1, source_target_pairs={{0,1},{1,2},{2,3},{4,5},{5,6},{6,7},{8,9},{9,10},{10,11},{12,13},{... | collective-permute-start | bytes 811016 | tf_op jit(solution)/shard_map/ppermute | solution.py:66

commit v6 on v5

--- a/solution.py
+++ b/solution.py
@@ -67,9 +67,8 @@
     ye = lax.ppermute(ext[:, :, :H], "gy", by)
     rows = nx + 2 * PAD
     yt = jnp.concatenate([ye, yw], axis=2)
-    yt = jnp.pad(yt, ((0, 0), (0, 0), (0, 0), (PAD - H, rows - nx - PAD - H)))
-    place = _select(2 * H, EXTRA, list(range(H)) + list(range(EXTRA - H, EXTRA)))
-    lanes = jnp.einsum("czkr,kj->czrj", yt, place, precision=hi)
+    span = -(-rows // 128) * 128
+    lanes = jnp.pad(yt, ((0, 0), (0, 0), (0, 0), (PAD - H, span - nx - PAD - H)))
     r_lo = jnp.pad(xlo, ((0, 0), (0, 0), (PAD - H, 0), (0, 0)))
     r_hi = jnp.pad(xhi, ((0, 0), (0, 0), (0, PAD - H), (0, 0)))
     return r_lo, r_hi, lanes
@@ -84,21 +83,34 @@
     acc_lo = PAD // RB
     acc_hi = (PAD + nx) // RB
 
-    def kernel(coef, src_hbm, obs_hbm, rlo_hbm, rhi_hbm, lanes_hbm, out_ref,
+    def kernel(coef, src_hbm, obs_hbm, rlo_hbm, rhi_hbm, lanes_ref, out_ref,
                a_buf, b_buf, o_buf, obs_buf, sems, s_buf, n_buf):
         copies = [
             pltpu.make_async_copy(obs_hbm, obs_buf, sems.at[0]),
             pltpu.make_async_copy(rlo_hbm.at[1], o_buf.at[:, pl.ds(0, PAD), pl.ds(0, ny)], sems.at[1]),
             pltpu.make_async_copy(rhi_hbm.at[1], o_buf.at[:, pl.ds(PAD + nx, PAD), pl.ds(0, ny)], sems.at[2]),
-            pltpu.make_async_copy(lanes_hbm.at[1], o_buf.at[:, :, pl.ds(ny, EXTRA)], sems.at[3]),
             pltpu.make_async_copy(src_hbm.at[0], a_buf.at[:, pl.ds(PAD, nx), pl.ds(0, ny)], sems.at[4]),
             pltpu.make_async_copy(rlo_hbm.at[0], a_buf.at[:, pl.ds(0, PAD), pl.ds(0, ny)], sems.at[5]),
             pltpu.make_async_copy(rhi_hbm.at[0], a_buf.at[:, pl.ds(PAD + nx, PAD), pl.ds(0, ny)], sems.at[6]),
-            pltpu.make_async_copy(lanes_hbm.at[0], a_buf.at[:, :, pl.ds(ny, EXTRA)], sems.at[7]),
         ]
         for cp in copies:
             cp.start()
 
+        k_id = lax.broadcasted_iota(jnp.int32, (2 * H, EXTRA), 0)
+        j_id = lax.broadcasted_iota(jnp.int32, (2 * H, EXTRA), 1)
+        dest = jnp.where(k_id < H, k_id, k_id + EXTRA - 2 * H)
+        place = (j_id == dest).astype(jnp.float32)
+
+        def put_lanes(z, c):
+            for buf, part in ((a_buf, 0), (o_buf, 1)):
+                placed = lax.dot_general(
+                    lanes_ref[part, z], place, (((0,), (0,)), ((), ())),
+                    precision=lax.Precision.HIGHEST, preferred_element_type=jnp.float32)
+                buf[z, :, pl.ds(ny, EXTRA)] = placed[:rows]
+            return c
+
+        lax.fori_loop(0, nz, put_lanes, 0)
+
         zeros = jnp.zeros((RB, width), jnp.float32)
 
         def clear(z, c):
@@ -115,7 +127,7 @@
             return c
 
         lax.fori_loop(0, nz, to_open, 0)
-        copies[4].wait()
+        copies[3].wait()
 
         def to_c0(z, c):
             a_buf[z, pl.ds(PAD, nx), pl.ds(0, ny)] = (
@@ -124,7 +136,7 @@
             return c
 
         lax.fori_loop(0, nz, to_c0, 0)
-        for cp in copies[1:4] + copies[5:]:
+        for cp in copies[1:3] + copies[4:]:
             cp.wait()
 
         k_w = coef[0]
@@ -254,7 +266,8 @@
     weighted = pl.pallas_call(
         make_kernel(nz, nx, ny, RZ),
         out_shape=jax.ShapeDtypeStruct((RZ, nx, ny), jnp.float32),
-        in_specs=[pl.BlockSpec(memory_space=pltpu.SMEM)] + [any_spec] * 5,
+        in_specs=[pl.BlockSpec(memory_space=pltpu.SMEM)] + [any_spec] * 4
+        + [pl.BlockSpec(memory_space=pltpu.VMEM)],
         out_specs=pl.BlockSpec(memory_space=pltpu.VMEM),
         scratch_shapes=[
             pltpu.VMEM((nz, rows, width), jnp.float32),

time: 160 us -> 172 us (1.075)
  local copies, waits for them, and re-layouts: 4.15 us -> 18.5 us
  matrix products: 22 us -> 8.18 us
  Pallas kernels: 54.8 us -> 65.3 us
    unnamed x6 -> x13, local copies, waits for them, and re-layouts: 0.02 us -> 13.7 us
    pallas_call x1, Pallas kernels: 54.8 us -> 65.3 us  [on_device(): pl.pallas_call(make_kernel(nz, nx, ny, RZ), out_shape=jax.ShapeDtypeStruc...]
    dot_general x1 -> x0, matrix products: 10.4 us -> none  [ghost_pieces(): lanes = jnp.einsum('czkr,kj->czrj', yt, place, precision=hi)]
    dot_general x1, matrix products: 7.7 us -> 4.3 us  [ghost_pieces(): jnp.einsum('zxy,ky->zkx', (1 - obs).astype(jnp.float32), pick, precision=hi)]
    another operation x4 -> x5, other arithmetic: 3.34 us -> 1.14 us  [_open_and_c(): return jnp.stack([src * open_cells, open_cells])]
  transfers between devices with their start and end apart: 4 -> 4, of which waited for: 1 -> 2; matrix products, arithmetic and copies ran while one was open for 10% -> 7% of each run, Pallas kernels for 0% -> 0%
where the time goes in v6:
time: 172 us; the launch traced here: 171 us
  Pallas kernels  65.3 us (38%)
  blocking collectives  54.6 us (32%)
  local copies, waits for them, and re-layouts  18.5 us (11%)
  starting transfers between devices  13.8 us (8%)
  matrix products  8.18 us (5%)
  other arithmetic  6.31 us (4%)
  waiting for transfers between devices  2.32 us (1%)
    pallas_call x1, Pallas kernels, on_device(): pl.pallas_call(make_kernel(nz, nx, ny, RZ), out_shape=jax.ShapeDtypeStruc...  65.3 us
    all_to_all x1, blocking collectives, on_device(): return lax.all_to_all(parts, 'scen', 0, 0, tiled=True).sum(0)  54.6 us
    unnamed x13, local copies, waits for them, and re-layouts  13.7 us
    ppermute x1, starting transfers between devices, ghost_pieces(): xlo = lax.ppermute(last_rows, 'gx', fx)  4.84 us
    ppermute x1, starting transfers between devices, ghost_pieces(): yw = lax.ppermute(ext[:, :, H:], 'gy', fy)  4.41 us
    dot_general x1, matrix products, ghost_pieces(): jnp.einsum('zxy,ky->zkx', (1 - obs).astype(jnp.float32), pick, precision=hi)  4.3 us
    dot_general x1, matrix products, ghost_pieces(): src_cols = jnp.einsum('zxy,ky->zkx', src, pick, precision=hi)  3.88 us
  transfers between devices with their start and end apart: 4, of which 2 were waited for; matrix products, arithmetic and copies ran while one was open for 7% of the time, Pallas kernels for 0%

profile of v6, /device:TPU:1, one launch (start us, length us, event | category | flops | bytes accessed | tf_op | source)
XLA Modules:
  0.0 170.7 jit_solution(15572298854267583304)
XLA Ops:
  0.0 1.2 fusion.28
  1.3 11.7 %copy.58 = f32[1,32,256,256]{3,1,2,0:T(8,128)} copy(f32[1,32,256,256]{3,2,1,0:T(8,128)} %src_hbm.1) | data formatting | bytes 16777216 | tf_op args[0]
  13.0 1.0 fusion.16
  14.0 3.3 %collective-permute-start.1 = (f32[2,32,4,256]{3,1,2,0:T(8,128)S(1)}, f32[2,32,4,256]{3,1,2,0:T(8,128)S(1)}, u32[]{:S(2)}, u32[]{:S(2)}) collective-permute-start(f32[2,32,4,256]{3,1,2,0:T(8,128)S(1)} %pad_maximum_fusion.2), channel_id=1, source_target_pairs={{4,0},{8,4},{12,8},{5,1},{9,5},{13,9},{6,2},{10,6},{14,10},{7,3},{... | collective-permute-start | bytes 786440 | tf_op jit(solution)/shard_map/ppermute | solution.py:58
  17.4 4.8 %collective-permute-start = (f32[2,32,4,256]{3,1,2,0:T(8,128)S(1)}, f32[2,32,4,256]{3,1,2,0:T(8,128)S(1)}, u32[]{:S(2)}, u32[]{:S(2)}) collective-permute-start(f32[2,32,4,256]{3,1,2,0:T(8,128)S(1)} %pad_maximum_fusion.1), channel_id=1, source_target_pairs={{0,4},{4,8},{8,12},{1,5},{5,9},{9,13},{2,6},{6,10},{10,14},{3,7},{... | collective-permute-start | bytes 786440 | tf_op jit(solution)/shard_map/ppermute | solution.py:57
  22.3 4.3 %fusion.2 = f32[8,32,256]{2,0,1:T(8,128)S(1)} fusion(s32[32,256,256]{2,1,0:T(8,128)S(1)} %copy-done, s32[8]{0:T(128)S(1)} %copy-done.1), kind=kOutput, calls=%fused_computation.3 | convolution fusion | flops 205522944 | bytes 8650784 | tf_op jit(solution)/shard_map/zxy,ky->zkx/dot_general | solution.py:61
  26.6 3.9 %fusion.12 = f32[1,32,8,256]{3,2,1,0:T(8,128)S(1)} fusion(f32[1,32,256,256]{3,2,1,0:T(8,128)S(1)} %bitcast.42, f32[8,32,256]{2,0,1:T(8,128)S(1)} %fusion.2, s32[8]{0:T(128)S(1)} %copy-done.1), kind=kOutput, calls=%fused_computation.11 | convolution fusion | flops 201394176 | bytes 8912928 | tf_op jit(solution)/shard_map/zxy,ky->zkx/dot_general | solution.py:60
  30.6 0.5 copy.41
  31.1 0.5 copy.42
  31.7 0.5 copy.39
  32.2 0.5 copy.40
  32.9 0.3 pad_maximum_fusion
  33.3 1.3 collective-permute-start.2
  34.6 4.4 %collective-permute-start.3 = (f32[2,32,4,264]{3,2,1,0:T(4,128)S(1)}, f32[2,32,4,264]{3,2,1,0:T(4,128)S(1)}, u32[]{:S(2)}, u32[]{:S(2)}) collective-permute-start(f32[2,32,4,264]{3,2,1,0:T(4,128)S(1)} %get-tuple-element.10), channel_id=1, source_target_pairs={{0,1},{1,2},{2,3},{4,5},{5,6},{6,7},{8,9},{9,10},{10,11},{12,13},{... | collective-permute-start | bytes 811016 | tf_op jit(solution)/shard_map/ppermute | solution.py:66
  40.6 0.6 stack.55.coef
  41.4 1.1 pad.13.rhi_hbm
  42.5 0.2 copy.28
  42.7 1.1 pad.12.rlo_hbm
  43.8 0.6 collective-permute-done.2
  44.3 1.8 %collective-permute-done.3 = f32[2,32,4,264]{3,2,1,0:T(4,128)S(1)} collective-permute-done((f32[2,32,4,264]{3,2,1,0:T(4,128)S(1)}, f32[2,32,4,264]{3,2,1,0:T(4,128)S(1)}, u32[]{:S(2)}, u32[]{:S(2)}) %collective-permute-start.3) | collective-permute-done | bytes 270368 | tf_op jit(solution)/shard_map/ppermute | solution.py:66
  46.1 1.4 select_maximum_fusion.lanes_ref
  47.5 65.3 %shard_map.55 = f32[16,256,256]{2,1,0:T(8,128)} custom-call(f32[8]{0:T(128)} %stack.55.coef, f32[1,32,256,256]{3,2,1,0:T(8,128)} %src_hbm.1, s32[32,256,256]{2,1,0:T(8,128)} %obs_hbm.1, f32[2,32,16,256]{3,2,1,0:T(8,128)} %pad.12.rlo_hbm, f32[2,32,16,256]{3,2,1,0:T(8,128)} %pad.13.rhi_hbm, f32[2,32,8,384]{3,2,1,0:T(8,128)} %select_maximum_fusion.lanes_ref), custom_call_target="tpu_custom_call" | custom-call | tf_op jit(solution)/shard_map/pallas_call | solution.py:266
  112.8 54.6 %all_to_all.5 = f32[8,2,256,256]{3,2,1,0:T(8,128)} all-to-all(f32[8,2,256,256]{3,2,1,0:T(8,128)} %bitcast.43), channel_id=1, replica_groups=mesh['scen'=8,'gx'=4,'gy'=4] {'scen'}, dimensions={0} | all-to-all | bytes 8388608 | tf_op jit(solution)/shard_map/all_to_all | solution.py:285
  167.4 3.3 %reduce_sum.9 = f32[2,256,256]{2,1,0:T(8,128)} reduce(f32[8,2,256,256]{3,2,1,0:T(8,128)} %all_to_all.5, f32[]{:T(128)} %constant.9.clone.1), dimensions={0}, to_apply=%region_0.1 | reduce | flops 917504 | bytes 4718596 | tf_op jit(solution)/shard_map/reduce_sum | solution.py:285
  (20 shorter events, 0.8 us)
Async XLA Ops:
  0.0 26.6 %slice-start = ((s8[8388608]{0:T(1024)(128)(4,1)}), s8[4194304]{0:T(1024)(128)(4,1)S(1)}, s32[]{:S(2)}) async-start(s8[8388608]{0:T(1024)(128)(4,1)} %bitcast.41), calls=%async_computation.1 | async-start | bytes 8388608
  1.2 21.0 %copy-start = (s32[32,256,256]{2,1,0:T(8,128)S(1)}, s32[32,256,256]{2,1,0:T(8,128)}, u32[]{:S(2)}) copy-start(s32[32,256,256]{2,1,0:T(8,128)} %obs_hbm.1) | copy-start | bytes 25165828
  1.2 21.0 %copy-start.1 = (s32[8]{0:T(128)S(1)}, s32[8]{0:T(128)}, u32[]{:S(2)}) copy-start(s32[8]{0:T(128)} %constant.32.clone) | copy-start | bytes 100
  1.3 25.3 %slice-start.1 = ((s8[8388608]{0:T(1024)(128)(4,1)}), s8[4194304]{0:T(1024)(128)(4,1)S(1)}, s32[]{:S(2)}) async-start(s8[8388608]{0:T(1024)(128)(4,1)} %bitcast.41), calls=%async_computation.2 | async-start | bytes 8388608
  14.0 16.5 %collective-permute-start.1 = (f32[2,32,4,256]{3,1,2,0:T(8,128)S(1)}, f32[2,32,4,256]{3,1,2,0:T(8,128)S(1)}, u32[]{:S(2)}, u32[]{:S(2)}) collective-permute-start(f32[2,32,4,256]{3,1,2,0:T(8,128)S(1)} %pad_maximum_fusion.2), channel_id=1, source_target_pairs={{4,0},{8,4},{12,8},{5,1},{9,5},{13,9},{6,2},{10,6},{14,10},{7,3},{... | collective-permute-start | bytes 786440 | tf_op jit(solution)/shard_map/ppermute | solution.py:58
  17.4 14.2 %collective-permute-start = (f32[2,32,4,256]{3,1,2,0:T(8,128)S(1)}, f32[2,32,4,256]{3,1,2,0:T(8,128)S(1)}, u32[]{:S(2)}, u32[]{:S(2)}) collective-permute-start(f32[2,32,4,256]{3,1,2,0:T(8,128)S(1)} %pad_maximum_fusion.1), channel_id=1, source_target_pairs={{0,4},{4,8},{8,12},{1,5},{5,9},{9,13},{2,6},{6,10},{10,14},{3,7},{... | collective-permute-start | bytes 786440 | tf_op jit(solution)/shard_map/ppermute | solution.py:57
  33.3 11.0 %collective-permute-start.2 = (f32[2,32,4,264]{3,2,1,0:T(4,128)S(1)}, f32[2,32,4,264]{3,2,1,0:T(4,128)S(1)}, u32[]{:S(2)}, u32[]{:S(2)}) collective-permute-start(f32[2,32,4,264]{3,2,1,0:T(4,128)S(1)} %get-tuple-element.9), channel_id=1, source_target_pairs={{1,0},{2,1},{3,2},{5,4},{6,5},{7,6},{9,8},{10,9},{11,10},{13,12},{... | collective-permute-start | bytes 811016 | tf_op jit(solution)/shard_map/ppermute | solution.py:67
  34.6 11.4 %collective-permute-start.3 = (f32[2,32,4,264]{3,2,1,0:T(4,128)S(1)}, f32[2,32,4,264]{3,2,1,0:T(4,128)S(1)}, u32[]{:S(2)}, u32[]{:S(2)}) collective-permute-start(f32[2,32,4,264]{3,2,1,0:T(4,128)S(1)} %get-tuple-element.10), channel_id=1, source_target_pairs={{0,1},{1,2},{2,3},{4,5},{5,6},{6,7},{8,9},{9,10},{10,11},{12,13},{... | collective-permute-start | bytes 811016 | tf_op jit(solution)/shard_map/ppermute | solution.py:66

commit v7 on v4

--- a/solution.py
+++ b/solution.py
@@ -23,7 +23,6 @@
 PAD = 16
 EXTRA = 128
 RB = 8
-ROT_UNROLL = 34
 
 
 def wind_components(sector_id):
@@ -73,26 +72,30 @@
     return r_lo, r_hi, lanes
 
 
-def make_kernel(nz, nx, ny, rz):
-    rows = nx + 2 * PAD
+def make_kernel(nz, nx, ny, rz, half):
+    nh = nx // 2
+    rows = nh + 2 * PAD
     width = ny + EXTRA
     nblk = rows // RB
     b_first = 1
     b_last = nblk - 2
     acc_lo = PAD // RB
-    acc_hi = (PAD + nx) // RB
-
-    def kernel(coef, src_hbm, obs_hbm, rlo_hbm, rhi_hbm, lanes_hbm, out_ref,
+    acc_hi = (PAD + nh) // RB
+    nb = nh + PAD
+    s0 = 0 if half == 0 else nx - nb
+    b0 = PAD if half == 0 else 0
+    g0 = 0 if half == 0 else nb
+    lane0 = 0 if half == 0 else nh
+
+    def kernel(coef, src_hbm, obs_hbm, ghost_hbm, lanes_hbm, out_ref,
                a_buf, b_buf, o_buf, obs_buf, sems, s_buf, n_buf):
         copies = [
-            pltpu.make_async_copy(obs_hbm, obs_buf, sems.at[0]),
-            pltpu.make_async_copy(rlo_hbm.at[1], o_buf.at[:, pl.ds(0, PAD), pl.ds(0, ny)], sems.at[1]),
-            pltpu.make_async_copy(rhi_hbm.at[1], o_buf.at[:, pl.ds(PAD + nx, PAD), pl.ds(0, ny)], sems.at[2]),
-            pltpu.make_async_copy(lanes_hbm.at[1], o_buf.at[:, :, pl.ds(ny, EXTRA)], sems.at[3]),
-            pltpu.make_async_copy(src_hbm.at[0], a_buf.at[:, pl.ds(PAD, nx), pl.ds(0, ny)], sems.at[4]),
-            pltpu.make_async_copy(rlo_hbm.at[0], a_buf.at[:, pl.ds(0, PAD), pl.ds(0, ny)], sems.at[5]),
-            pltpu.make_async_copy(rhi_hbm.at[0], a_buf.at[:, pl.ds(PAD + nx, PAD), pl.ds(0, ny)], sems.at[6]),
-            pltpu.make_async_copy(lanes_hbm.at[0], a_buf.at[:, :, pl.ds(ny, EXTRA)], sems.at[7]),
+            pltpu.make_async_copy(obs_hbm.at[:, pl.ds(s0, nb), :], obs_buf, sems.at[0]),
+            pltpu.make_async_copy(ghost_hbm.at[1], o_buf.at[:, pl.ds(g0, PAD), pl.ds(0, ny)], sems.at[1]),
+            pltpu.make_async_copy(lanes_hbm.at[1, :, pl.ds(lane0, rows)], o_buf.at[:, :, pl.ds(ny, EXTRA)], sems.at[3]),
+            pltpu.make_async_copy(src_hbm.at[0, :, pl.ds(s0, nb), :], a_buf.at[:, pl.ds(b0, nb), pl.ds(0, ny)], sems.at[4]),
+            pltpu.make_async_copy(ghost_hbm.at[0], a_buf.at[:, pl.ds(g0, PAD), pl.ds(0, ny)], sems.at[5]),
+            pltpu.make_async_copy(lanes_hbm.at[0, :, pl.ds(lane0, rows)], a_buf.at[:, :, pl.ds(ny, EXTRA)], sems.at[7]),
         ]
         for cp in copies:
             cp.start()
@@ -109,20 +112,20 @@
         copies[0].wait()
 
         def to_open(z, c):
-            o_buf[z, pl.ds(PAD, nx), pl.ds(0, ny)] = (1 - obs_buf[z]).astype(jnp.float32)
+            o_buf[z, pl.ds(b0, nb), pl.ds(0, ny)] = (1 - obs_buf[z]).astype(jnp.float32)
             return c
 
         lax.fori_loop(0, nz, to_open, 0)
-        copies[4].wait()
+        copies[3].wait()
 
         def to_c0(z, c):
-            a_buf[z, pl.ds(PAD, nx), pl.ds(0, ny)] = (
-                a_buf[z, pl.ds(PAD, nx), pl.ds(0, ny)] * o_buf[z, pl.ds(PAD, nx), pl.ds(0, ny)]
+            a_buf[z, pl.ds(b0, nb), pl.ds(0, ny)] = (
+                a_buf[z, pl.ds(b0, nb), pl.ds(0, ny)] * o_buf[z, pl.ds(b0, nb), pl.ds(0, ny)]
             )
             return c
 
         lax.fori_loop(0, nz, to_c0, 0)
-        for cp in copies[1:4] + copies[5:]:
+        for cp in copies[1:3] + copies[4:]:
             cp.wait()
 
         k_w = coef[0]
@@ -163,7 +166,7 @@
                             last_lane, left[(k + 1) % npc], left[k])
                     return c
 
-                lax.fori_loop(b_first, b_last + 1, rot, 0, unroll=ROT_UNROLL)
+                lax.fori_loop(b_first, b_last + 1, rot, 0, unroll=True)
 
                 def blk(b, carry, acc):
                     prev, cur = carry
@@ -198,10 +201,10 @@
                 carry = (pieces(src, z, 0), pieces(src, z, RB))
                 if accumulate:
                     carry = lax.fori_loop(b_first, acc_lo, lambda b, c: blk(b, c, False), carry)
-                    carry = lax.fori_loop(acc_lo, acc_hi, lambda b, c: blk(b, c, True), carry, unroll=4)
+                    carry = lax.fori_loop(acc_lo, acc_hi, lambda b, c: blk(b, c, True), carry, unroll=True)
                     carry = lax.fori_loop(acc_hi, b_last + 1, lambda b, c: blk(b, c, False), carry)
                 else:
-                    carry = lax.fori_loop(b_first, b_last + 1, lambda b, c: blk(b, c, False), carry, unroll=2)
+                    carry = lax.fori_loop(b_first, b_last + 1, lambda b, c: blk(b, c, False), carry, unroll=True)
 
             def lvl_acc(z, c):
                 level(z, True)
@@ -219,7 +222,7 @@
             step(bufs[n % 2], bufs[(n + 1) % 2], n == 0)
 
         def leth(z, c):
-            for q in range(nx // 32):
+            for q in range(nh // 32):
                 load = out_ref[z, pl.ds(q * 32, 32), :]
                 probit = probit_a + probit_b * jnp.log(load + load_eps)
                 lethal = 0.5 * (1.0 + lax.erf((probit - 5.0) / math.sqrt(2.0)))
@@ -229,6 +232,12 @@
         lax.fori_loop(0, rz, leth, 0)
 
     return kernel
+
+
+def _reduce_sync(weighted):
+    count = lax.axis_size("scen")
+    parts = weighted.reshape((count, RZ // count) + weighted.shape[1:])
+    return lax.all_to_all(parts, "scen", 0, 0, tiled=True).sum(0)
 
 
 def on_device(source, obstacle, sector, freq_class):
@@ -246,28 +255,32 @@
          weight, jnp.float32(0.0)]
     ).astype(jnp.float32)
     r_lo, r_hi, lanes = ghost_pieces(src, obstacle)
-    rows = nx + 2 * PAD
+    nh = nx // 2
+    rows = nh + 2 * PAD
     width = ny + EXTRA
     any_spec = pl.BlockSpec(memory_space=pl.ANY)
-    weighted = pl.pallas_call(
-        make_kernel(nz, nx, ny, RZ),
-        out_shape=jax.ShapeDtypeStruct((RZ, nx, ny), jnp.float32),
-        in_specs=[pl.BlockSpec(memory_space=pltpu.SMEM)] + [any_spec] * 5,
-        out_specs=pl.BlockSpec(memory_space=pltpu.VMEM),
-        scratch_shapes=[
-            pltpu.VMEM((nz, rows, width), jnp.float32),
-            pltpu.VMEM((nz, rows, width), jnp.float32),
-            pltpu.VMEM((nz, rows, width), jnp.float32),
-            pltpu.VMEM((nz, nx, ny), jnp.int32),
-            pltpu.SemaphoreType.DMA((8,)),
-            pltpu.VMEM((rows, width), jnp.float32),
-            pltpu.VMEM((rows, width), jnp.float32),
-        ],
-        compiler_params=pltpu.CompilerParams(vmem_limit_bytes=62 * 1024 * 1024),
-    )(coef, source, obstacle, r_lo, r_hi, lanes)
-    count = lax.axis_size("scen")
-    parts = weighted.reshape(count, RZ // count, nx, ny)
-    return lax.all_to_all(parts, "scen", 0, 0, tiled=True).sum(0)
+    halves = []
+    for half, ghost in ((0, r_lo), (1, r_hi)):
+        halves.append(pl.pallas_call(
+            make_kernel(nz, nx, ny, RZ, half),
+            out_shape=jax.ShapeDtypeStruct((RZ, nh, ny), jnp.float32),
+            in_specs=[pl.BlockSpec(memory_space=pltpu.SMEM)] + [any_spec] * 4,
+            out_specs=pl.BlockSpec(memory_space=pltpu.VMEM),
+            scratch_shapes=[
+                pltpu.VMEM((nz, rows, width), jnp.float32),
+                pltpu.VMEM((nz, rows, width), jnp.float32),
+                pltpu.VMEM((nz, rows, width), jnp.float32),
+                pltpu.VMEM((nz, nh + PAD, ny), jnp.int32),
+                pltpu.SemaphoreType.DMA((8,)),
+                pltpu.VMEM((rows, width), jnp.float32),
+                pltpu.VMEM((rows, width), jnp.float32),
+            ],
+            compiler_params=pltpu.CompilerParams(vmem_limit_bytes=62 * 1024 * 1024),
+        )(coef, source, obstacle, ghost, lanes))
+        if half == 0:
+            first = _reduce_sync(halves[0])
+    second = _reduce_sync(halves[1])
+    return jnp.concatenate([first, second], axis=1)
 
 
 def solution(mesh):

time: 198 us -> 154 us (0.78)
  blocking collectives: 54.2 us -> 0 us
  waiting for transfers between devices: 1.42 us -> 27.8 us
  Pallas kernels: 92.8 us -> 67.3 us
  starting transfers between devices: 13.6 us -> 24 us
    all_to_all x1 -> x0, blocking collectives: 54.2 us -> none  [on_device(): return lax.all_to_all(parts, 'scen', 0, 0, tiled=True).sum(0)]
    pallas_call x1 -> x2, Pallas kernels: 92.8 us -> 67.3 us  [on_device(): pl.pallas_call(make_kernel(nz, nx, ny, RZ, half), out_shape=jax.ShapeDtyp...]
    all_to_all x0 -> x2, waiting for transfers between devices: none -> 25.3 us  [_reduce_sync(): return lax.all_to_all(parts, 'scen', 0, 0, tiled=True).sum(0)]
    all_to_all x0 -> x2, starting transfers between devices: none -> 10.4 us  [_reduce_sync(): return lax.all_to_all(parts, 'scen', 0, 0, tiled=True).sum(0)]
  transfers between devices with their start and end apart: 4 -> 6, of which waited for: 1 -> 3; matrix products, arithmetic and copies ran while one was open for 8% -> 11% of each run, Pallas kernels for 0% -> 22%
where the time goes in v7:
time: 154 us
  Pallas kernels  67.3 us (44%)
  waiting for transfers between devices  27.8 us (18%)
  starting transfers between devices  24 us (16%)
  matrix products  22 us (14%)
  other arithmetic  6.68 us (4%)
  local copies, waits for them, and re-layouts  4.16 us (3%)
  between operations  1.64 us (1%)
    pallas_call x2, Pallas kernels, on_device(): pl.pallas_call(make_kernel(nz, nx, ny, RZ, half), out_shape=jax.ShapeDtyp...  67.3 us
    all_to_all x2, waiting for transfers between devices, _reduce_sync(): return lax.all_to_all(parts, 'scen', 0, 0, tiled=True).sum(0)  25.3 us
    dot_general x1, matrix products, ghost_pieces(): lanes = jnp.einsum('czkr,kj->czrj', yt, place, precision=hi)  10.4 us
    all_to_all x2, starting transfers between devices, _reduce_sync(): return lax.all_to_all(parts, 'scen', 0, 0, tiled=True).sum(0)  10.4 us
    dot_general x1, matrix products, ghost_pieces(): jnp.einsum('zxy,ky->zkx', (1 - obs).astype(jnp.float32), pick, precision=hi)  7.7 us
    ppermute x1, starting transfers between devices, ghost_pieces(): xlo = lax.ppermute(last_rows, 'gx', fx)  6.03 us
    ppermute x1, starting transfers between devices, ghost_pieces(): yw = lax.ppermute(ext[:, :, H:], 'gy', fy)  4.37 us
    dot_general x1, matrix products, ghost_pieces(): src_cols = jnp.einsum('zxy,ky->zkx', src, pick, precision=hi)  3.88 us
  transfers between devices with their start and end apart: 6, of which 3 were waited for; matrix products, arithmetic and copies ran while one was open for 11% of the time, Pallas kernels for 22%

profile of v7, /device:TPU:1, one launch (start us, length us, event | category | flops | bytes accessed | tf_op | source)
XLA Modules:
  0.0 153.6 jit_solution(5895734786295881900)
XLA Ops:
  0.0 1.2 convert_bitcast_fusion.1
  1.2 2.0 %fusion.16 = (f32[1,32,4,256]{3,2,1,0:T(4,128)S(1)}, f32[1,32,4,256]{3,2,1,0:T(4,128)S(1)}) fusion(f32[32,256,256]{2,1,0:T(8,128)} %bitcast.38, s32[32,256,256]{2,1,0:T(8,128)} %obs_hbm.3), kind=kLoop, calls=%fused_computation.25 | loop fusion | flops 196608 | bytes 786432 | tf_op jit(solution)/shard_map/stack | solution.py:35
  3.3 6.0 %collective-permute-start = (f32[2,32,4,256]{3,2,1,0:T(4,128)S(1)}, f32[2,32,4,256]{3,2,1,0:T(4,128)S(1)}, u32[]{:S(2)}, u32[]{:S(2)}) collective-permute-start(f32[2,32,4,256]{3,2,1,0:T(4,128)S(1)} %pad_maximum_fusion.2), channel_id=1, source_target_pairs={{0,4},{4,8},{8,12},{1,5},{5,9},{9,13},{2,6},{6,10},{10,14},{3,7},{... | collective-permute-start | bytes 786440 | tf_op jit(solution)/shard_map/ppermute | solution.py:54
  9.4 1.9 %collective-permute-start.1 = (f32[2,32,4,256]{3,2,1,0:T(4,128)S(1)}, f32[2,32,4,256]{3,2,1,0:T(4,128)S(1)}, u32[]{:S(2)}, u32[]{:S(2)}) collective-permute-start(f32[2,32,4,256]{3,2,1,0:T(4,128)S(1)} %pad_maximum_fusion.3), channel_id=1, source_target_pairs={{4,0},{8,4},{12,8},{5,1},{9,5},{13,9},{6,2},{10,6},{14,10},{7,3},{... | collective-permute-start | bytes 786440 | tf_op jit(solution)/shard_map/ppermute | solution.py:55
  11.3 7.7 %fusion = f32[8,32,256]{2,0,1:T(8,128)S(1)} fusion(s32[32,256,256]{2,1,0:T(8,128)} %obs_hbm.3, s32[8]{0:T(128)} %constant.34.clone), kind=kOutput, calls=%fused_computation | convolution fusion | flops 205522944 | bytes 8650784 | tf_op jit(solution)/shard_map/zxy,ky->zkx/dot_general | solution.py:58
  19.1 3.9 %fusion.5 = f32[1,32,8,256]{3,2,1,0:T(8,128)S(1)} fusion(f32[8,32,256]{2,0,1:T(8,128)S(1)} %fusion, s32[8]{0:T(128)S(1)} %copy-done.1, f32[1,32,256,256]{3,2,1,0:T(8,128)S(1)} %copy-done), kind=kOutput, calls=%fused_computation.8 | convolution fusion | flops 201394176 | bytes 8912928 | tf_op jit(solution)/shard_map/zxy,ky->zkx/dot_general | solution.py:57
  23.2 0.4 copy.15
  24.0 0.4 copy.16
  24.4 0.3 pad_maximum_fusion
  24.9 1.3 collective-permute-start.2
  26.2 4.4 %collective-permute-start.3 = (f32[2,32,4,264]{3,2,1,0:T(4,128)S(1)}, f32[2,32,4,264]{3,2,1,0:T(4,128)S(1)}, u32[]{:S(2)}, u32[]{:S(2)}) collective-permute-start(f32[2,32,4,264]{3,2,1,0:T(4,128)S(1)} %get-tuple-element.10), channel_id=1, source_target_pairs={{0,1},{1,2},{2,3},{4,5},{5,6},{6,7},{8,9},{9,10},{10,11},{12,13},{... | collective-permute-start | bytes 811016 | tf_op jit(solution)/shard_map/ppermute | solution.py:63
  32.1 0.6 stack.55.coef
  32.7 1.1 pad.12.ghost_hbm
  33.8 0.8 collective-permute-done.2
  34.6 1.8 %collective-permute-done.3 = f32[2,32,4,264]{3,2,1,0:T(4,128)S(1)} collective-permute-done((f32[2,32,4,264]{3,2,1,0:T(4,128)S(1)}, f32[2,32,4,264]{3,2,1,0:T(4,128)S(1)}, u32[]{:S(2)}, u32[]{:S(2)}) %collective-permute-start.3) | collective-permute-done | bytes 270368 | tf_op jit(solution)/shard_map/ppermute | solution.py:63
  36.3 10.4 %fusion.6.lanes_hbm = f32[2,32,288,128]{3,2,1,0:T(8,128)} fusion(f32[2,32,4,264]{3,2,1,0:T(4,128)S(1)} %collective-permute-done.3, f32[2,32,4,264]{3,2,1,0:T(4,128)S(1)} %collective-permute-done.2, s32[8]{0:T(128)S(1)} %copy-done.2), kind=kOutput, calls=%fused_computation.10 | convolution fusion | flops 227378176 | bytes 9977888 | tf_op jit(solution)/shard_map/czkr,kj->czrj/dot_general | solution.py:69
  46.8 33.7 %shard_map.64 = f32[16,128,256]{2,1,0:T(8,128)} custom-call(f32[8]{0:T(128)} %stack.55.coef, f32[1,32,256,256]{3,2,1,0:T(8,128)} %src_hbm.3, s32[32,256,256]{2,1,0:T(8,128)} %obs_hbm.3, f32[2,32,16,256]{3,2,1,0:T(8,128)} %pad.12.ghost_hbm, f32[2,32,288,128]{3,2,1,0:T(8,128)} %fusion.6.lanes_hbm), custom_call_target="tpu_custom_call" | custom-call | tf_op jit(solution)/shard_map/pallas_call | solution.py:264
  80.4 5.2 %all-to-all-start = ((f32[8,2,128,256]{3,2,1,0:T(8,128)}), f32[8,2,128,256]{3,2,1,0:T(8,128)}, u32[]{:S(2)}, u32[]{:S(2)}) async-start(f32[8,2,128,256]{3,2,1,0:T(8,128)} %bitcast.40), calls=%async_computation | async-start | bytes 4194304 | tf_op jit(solution)/shard_map/all_to_all | solution.py:240
  85.7 1.1 pad.14.ghost_hbm
  86.8 33.7 %shard_map.65 = f32[16,128,256]{2,1,0:T(8,128)} custom-call(f32[8]{0:T(128)} %stack.55.coef, f32[1,32,256,256]{3,2,1,0:T(8,128)} %src_hbm.3, s32[32,256,256]{2,1,0:T(8,128)} %obs_hbm.3, f32[2,32,16,256]{3,2,1,0:T(8,128)} %pad.14.ghost_hbm, f32[2,32,288,128]{3,2,1,0:T(8,128)} %fusion.6.lanes_hbm), custom_call_target="tpu_custom_call" | custom-call | tf_op jit(solution)/shard_map/pallas_call | solution.py:264
  120.5 5.2 %all-to-all-start.1 = ((f32[8,2,128,256]{3,2,1,0:T(8,128)}), f32[8,2,128,256]{3,2,1,0:T(8,128)S(1)}, u32[]{:S(2)}, u32[]{:S(2)}) async-start(f32[8,2,128,256]{3,2,1,0:T(8,128)} %bitcast.39), calls=%async_computation.1 | async-start | bytes 4194304 | tf_op jit(solution)/shard_map/all_to_all | solution.py:240
  125.6 1.8 %reduce_sum.18 = f32[2,128,256]{2,1,0:T(8,128)S(1)} reduce(f32[8,2,128,256]{3,2,1,0:T(8,128)} %all-to-all-done, f32[]{:T(128)} %constant.10.clone.1), dimensions={0}, to_apply=%region_0.1 | reduce | flops 458752 | bytes 2359300 | tf_op jit(solution)/shard_map/reduce_sum | solution.py:240
  127.4 25.2 %all-to-all-done.1 = f32[8,2,128,256]{3,2,1,0:T(8,128)S(1)} async-done(((f32[8,2,128,256]{3,2,1,0:T(8,128)}), f32[8,2,128,256]{3,2,1,0:T(8,128)S(1)}, u32[]{:S(2)}, u32[]{:S(2)}) %all-to-all-start.1) | async-done | bytes 2097184 | tf_op jit(solution)/shard_map/all_to_all | solution.py:240
  152.8 0.8 pad_maximum_fusion.1
  (17 shorter events, 1.0 us)
Async XLA Ops:
  0.0 19.0 %copy-start.1 = (s32[8]{0:T(128)S(1)}, s32[8]{0:T(128)}, u32[]{:S(2)}) copy-start(s32[8]{0:T(128)} %constant.34.clone) | copy-start | bytes 100
  0.0 19.0 %copy-start = (f32[1,32,256,256]{3,2,1,0:T(8,128)S(1)}, f32[1,32,256,256]{3,2,1,0:T(8,128)}, u32[]{:S(2)}) copy-start(f32[1,32,256,256]{3,2,1,0:T(8,128)} %src_hbm.3) | copy-start | bytes 25165828
  3.3 19.6 %collective-permute-start = (f32[2,32,4,256]{3,2,1,0:T(4,128)S(1)}, f32[2,32,4,256]{3,2,1,0:T(4,128)S(1)}, u32[]{:S(2)}, u32[]{:S(2)}) collective-permute-start(f32[2,32,4,256]{3,2,1,0:T(4,128)S(1)} %pad_maximum_fusion.2), channel_id=1, source_target_pairs={{0,4},{4,8},{8,12},{1,5},{5,9},{9,13},{2,6},{6,10},{10,14},{3,7},{... | collective-permute-start | bytes 786440 | tf_op jit(solution)/shard_map/ppermute | solution.py:54
  9.4 14.3 %collective-permute-start.1 = (f32[2,32,4,256]{3,2,1,0:T(4,128)S(1)}, f32[2,32,4,256]{3,2,1,0:T(4,128)S(1)}, u32[]{:S(2)}, u32[]{:S(2)}) collective-permute-start(f32[2,32,4,256]{3,2,1,0:T(4,128)S(1)} %pad_maximum_fusion.3), channel_id=1, source_target_pairs={{4,0},{8,4},{12,8},{5,1},{9,5},{13,9},{6,2},{10,6},{14,10},{7,3},{... | collective-permute-start | bytes 786440 | tf_op jit(solution)/shard_map/ppermute | solution.py:55
  19.0 17.3 %copy-start.2 = (s32[8]{0:T(128)S(1)}, s32[8]{0:T(128)}, u32[]{:S(2)}) copy-start(s32[8]{0:T(128)} %constant.35.clone) | copy-start | bytes 100
  24.9 9.7 %collective-permute-start.2 = (f32[2,32,4,264]{3,2,1,0:T(4,128)S(1)}, f32[2,32,4,264]{3,2,1,0:T(4,128)S(1)}, u32[]{:S(2)}, u32[]{:S(2)}) collective-permute-start(f32[2,32,4,264]{3,2,1,0:T(4,128)S(1)} %get-tuple-element.9), channel_id=1, source_target_pairs={{1,0},{2,1},{3,2},{5,4},{6,5},{7,6},{9,8},{10,9},{11,10},{13,12},{... | collective-permute-start | bytes 811016 | tf_op jit(solution)/shard_map/ppermute | solution.py:64
  26.2 10.1 %collective-permute-start.3 = (f32[2,32,4,264]{3,2,1,0:T(4,128)S(1)}, f32[2,32,4,264]{3,2,1,0:T(4,128)S(1)}, u32[]{:S(2)}, u32[]{:S(2)}) collective-permute-start(f32[2,32,4,264]{3,2,1,0:T(4,128)S(1)} %get-tuple-element.10), channel_id=1, source_target_pairs={{0,1},{1,2},{2,3},{4,5},{5,6},{6,7},{8,9},{9,10},{10,11},{12,13},{... | collective-permute-start | bytes 811016 | tf_op jit(solution)/shard_map/ppermute | solution.py:63
  80.4 40.0 %all-to-all-start = ((f32[8,2,128,256]{3,2,1,0:T(8,128)}), f32[8,2,128,256]{3,2,1,0:T(8,128)}, u32[]{:S(2)}, u32[]{:S(2)}) async-start(f32[8,2,128,256]{3,2,1,0:T(8,128)} %bitcast.40), calls=%async_computation | async-start | bytes 4194304 | tf_op jit(solution)/shard_map/all_to_all | solution.py:240
  120.5 32.2 %all-to-all-start.1 = ((f32[8,2,128,256]{3,2,1,0:T(8,128)}), f32[8,2,128,256]{3,2,1,0:T(8,128)S(1)}, u32[]{:S(2)}, u32[]{:S(2)}) async-start(f32[8,2,128,256]{3,2,1,0:T(8,128)} %bitcast.39), calls=%async_computation.1 | async-start | bytes 4194304 | tf_op jit(solution)/shard_map/all_to_all | solution.py:240

commit v8 on v7

--- a/solution.py
+++ b/solution.py
@@ -38,6 +38,17 @@
 def _select(count, width, picks):
     cols = jnp.asarray(picks, jnp.int32)[:, None]
     return (lax.broadcasted_iota(jnp.int32, (count, width), 1) == cols).astype(jnp.float32)
+
+
+def _split3(x):
+    def bf(v):
+        return lax.reduce_precision(v, exponent_bits=8, mantissa_bits=7)
+
+    top = bf(x)
+    rest = x - top
+    mid = bf(rest)
+    low = rest - mid
+    return (top.astype(jnp.bfloat16), mid.astype(jnp.bfloat16), low.astype(jnp.bfloat16))
 
 
 def ghost_pieces(src, obs):
@@ -55,7 +66,9 @@
     xhi = lax.ppermute(first_rows, "gx", bx)
     pick = _select(2 * H, ny, list(range(H)) + list(range(ny - H, ny)))
     src_cols = jnp.einsum("zxy,ky->zkx", src, pick, precision=hi)
-    open_cols = jnp.einsum("zxy,ky->zkx", (1 - obs).astype(jnp.float32), pick, precision=hi)
+    open_cols = jnp.einsum(
+        "zxy,ky->zkx", (1 - obs).astype(jnp.bfloat16), pick.astype(jnp.bfloat16),
+        preferred_element_type=jnp.float32)
     cols = jnp.stack([src_cols * open_cols, open_cols])
     corner_lo = jnp.swapaxes(jnp.concatenate([xlo[..., :H], xlo[..., ny - H:]], -1), -1, -2)
     corner_hi = jnp.swapaxes(jnp.concatenate([xhi[..., :H], xhi[..., ny - H:]], -1), -1, -2)
@@ -66,7 +79,10 @@
     yt = jnp.concatenate([ye, yw], axis=2)
     yt = jnp.pad(yt, ((0, 0), (0, 0), (0, 0), (PAD - H, rows - nx - PAD - H)))
     place = _select(2 * H, EXTRA, list(range(H)) + list(range(EXTRA - H, EXTRA)))
-    lanes = jnp.einsum("czkr,kj->czrj", yt, place, precision=hi)
+    place = jnp.concatenate([place] * 3, 0).astype(jnp.bfloat16)
+    lanes = jnp.einsum(
+        "czkr,kj->czrj", jnp.concatenate(_split3(yt), 2), place,
+        preferred_element_type=jnp.float32)
     r_lo = jnp.pad(xlo, ((0, 0), (0, 0), (PAD - H, 0), (0, 0)))
     r_hi = jnp.pad(xhi, ((0, 0), (0, 0), (0, PAD - H), (0, 0)))
     return r_lo, r_hi, lanes

time: 154 us -> 146 us (0.948)
  matrix products: 22 us -> 13.1 us
    dot_general x2, matrix products: 18.1 us -> 9.18 us  [the longest x1 4.64 us: ghost_pieces(): jnp.einsum('zxy,ky->zkx', (1 - obs).astype(jnp.bfloat16), pick.astype(jnp...]
  transfers between devices with their start and end apart: 6 -> 6, of which waited for: 3 -> 3; matrix products, arithmetic and copies ran while one was open for 11% -> 10% of each run, Pallas kernels for 22% -> 23%
where the time goes in v8:
time: 146 us; the launch traced here: 145 us
  Pallas kernels  67.3 us (46%)
  waiting for transfers between devices  28.7 us (20%)
  starting transfers between devices  24.2 us (17%)
  matrix products  13.1 us (9%)
  other arithmetic  6.44 us (4%)
  local copies, waits for them, and re-layouts  4.13 us (3%)
  between operations  1.65 us (1%)
    pallas_call x2, Pallas kernels, on_device(): pl.pallas_call(make_kernel(nz, nx, ny, RZ, half), out_shape=jax.ShapeDtyp...  67.3 us
    all_to_all x2, waiting for transfers between devices, _reduce_sync(): return lax.all_to_all(parts, 'scen', 0, 0, tiled=True).sum(0)  25.6 us
    all_to_all x2, starting transfers between devices, _reduce_sync(): return lax.all_to_all(parts, 'scen', 0, 0, tiled=True).sum(0)  10.4 us
    ppermute x1, starting transfers between devices, ghost_pieces(): xlo = lax.ppermute(last_rows, 'gx', fx)  6.03 us
    dot_general x1, matrix products, ghost_pieces(): jnp.einsum('zxy,ky->zkx', (1 - obs).astype(jnp.bfloat16), pick.astype(jnp...  4.64 us
    dot_general x1, matrix products, ghost_pieces(): jnp.einsum('czkr,kj->czrj', jnp.concatenate(_split3(yt), 2), place, prefe...  4.54 us
    ppermute x1, starting transfers between devices, ghost_pieces(): yw = lax.ppermute(ext[:, :, H:], 'gy', fy)  4.19 us
    dot_general x1, matrix products, ghost_pieces(): src_cols = jnp.einsum('zxy,ky->zkx', src, pick, precision=hi)  3.89 us
  transfers between devices with their start and end apart: 6, of which 3 were waited for; matrix products, arithmetic and copies ran while one was open for 10% of the time, Pallas kernels for 23%

profile of v8, /device:TPU:1, one launch (start us, length us, event | category | flops | bytes accessed | tf_op | source)
XLA Modules:
  0.0 145.5 jit_solution(7823970738389658748)
XLA Ops:
  0.0 1.1 convert_bitcast_fusion.1
  1.1 1.3 fusion.13
  2.5 6.0 %collective-permute-start = (f32[2,32,4,256]{3,2,1,0:T(4,128)S(1)}, f32[2,32,4,256]{3,2,1,0:T(4,128)S(1)}, u32[]{:S(2)}, u32[]{:S(2)}) collective-permute-start(f32[2,32,4,256]{3,2,1,0:T(4,128)S(1)} %pad_maximum_fusion.2), channel_id=1, source_target_pairs={{0,4},{4,8},{8,12},{1,5},{5,9},{9,13},{2,6},{6,10},{10,14},{3,7},{... | collective-permute-start | bytes 786440 | tf_op jit(solution)/shard_map/ppermute | solution.py:65
  8.6 2.3 %collective-permute-start.1 = (f32[2,32,4,256]{3,2,1,0:T(4,128)S(1)}, f32[2,32,4,256]{3,2,1,0:T(4,128)S(1)}, u32[]{:S(2)}, u32[]{:S(2)}) collective-permute-start(f32[2,32,4,256]{3,2,1,0:T(4,128)S(1)} %pad_maximum_fusion.3), channel_id=1, source_target_pairs={{4,0},{8,4},{12,8},{5,1},{9,5},{13,9},{6,2},{10,6},{14,10},{7,3},{... | collective-permute-start | bytes 786440 | tf_op jit(solution)/shard_map/ppermute | solution.py:66
  10.9 4.6 %fusion = f32[8,32,256]{2,0,1:T(8,128)S(1)} fusion(s32[32,256,256]{2,1,0:T(8,128)} %obs_hbm.3, s32[8]{0:T(128)} %constant.34.clone), kind=kOutput, calls=%fused_computation.1 | convolution fusion | flops 37754880 | bytes 8650784 | tf_op jit(solution)/shard_map/zxy,ky->zkx/dot_general | solution.py:69
  15.6 3.9 %fusion.9 = f32[1,32,8,256]{3,2,1,0:T(8,128)S(1)} fusion(f32[8,32,256]{2,0,1:T(8,128)S(1)} %fusion, s32[8]{0:T(128)S(1)} %copy-done.1, f32[1,32,256,256]{3,2,1,0:T(8,128)S(1)} %copy-done), kind=kOutput, calls=%fused_computation.13 | convolution fusion | flops 201394176 | bytes 8912928 | tf_op jit(solution)/shard_map/zxy,ky->zkx/dot_general | solution.py:68
  19.7 0.4 copy.15
  20.5 0.4 copy.16
  21.4 1.3 collective-permute-start.2
  22.7 4.2 %collective-permute-start.3 = (f32[2,32,4,264]{3,2,1,0:T(4,128)S(1)}, f32[2,32,4,264]{3,2,1,0:T(4,128)S(1)}, u32[]{:S(2)}, u32[]{:S(2)}) collective-permute-start(f32[2,32,4,264]{3,2,1,0:T(4,128)S(1)} %get-tuple-element.13), channel_id=1, source_target_pairs={{0,1},{1,2},{2,3},{4,5},{5,6},{6,7},{8,9},{9,10},{10,11},{12,13},{... | collective-permute-start | bytes 811016 | tf_op jit(solution)/shard_map/ppermute | solution.py:76
  28.4 0.6 stack.55.coef
  29.1 1.1 pad.12.ghost_hbm
  30.2 1.3 collective-permute-done.2
  31.5 1.8 %collective-permute-done.3 = f32[2,32,4,264]{3,2,1,0:T(4,128)S(1)} collective-permute-done((f32[2,32,4,264]{3,2,1,0:T(4,128)S(1)}, f32[2,32,4,264]{3,2,1,0:T(4,128)S(1)}, u32[]{:S(2)}, u32[]{:S(2)}) %collective-permute-start.3) | collective-permute-done | bytes 270368 | tf_op jit(solution)/shard_map/ppermute | solution.py:76
  33.3 0.5 reduce-precision_convert_fusion.1
  33.8 4.5 %fusion.2.lanes_hbm = f32[2,32,288,128]{3,2,1,0:T(8,128)} fusion(bf16[2,32,8,288]{3,2,1,0:T(8,128)(2,1)S(1)} %get-tuple-element.10, bf16[2,32,8,288]{3,2,1,0:T(8,128)(2,1)S(1)} %get-tuple-element.11, bf16[2,32,8,288]{3,2,1,0:T(8,128)(2,1)S(1)} %get-tuple-element.9, pred[8,128]{1,0:T(8,128)(4,1)S(1)} %iota_compare_fusion.3), kind=kOutput, calls=%fused_computation.5 | convolution fusion | flops 115912704 | bytes 10322944 | tf_op jit(solution)/shard_map/czkr,kj->czrj/dot_general | solution.py:83
  38.4 33.7 %shard_map.64 = f32[16,128,256]{2,1,0:T(8,128)} custom-call(f32[8]{0:T(128)} %stack.55.coef, f32[1,32,256,256]{3,2,1,0:T(8,128)} %src_hbm.3, s32[32,256,256]{2,1,0:T(8,128)} %obs_hbm.3, f32[2,32,16,256]{3,2,1,0:T(8,128)} %pad.12.ghost_hbm, f32[2,32,288,128]{3,2,1,0:T(8,128)} %fusion.2.lanes_hbm), custom_call_target="tpu_custom_call" | custom-call | tf_op jit(solution)/shard_map/pallas_call | solution.py:280
  72.0 5.2 %all-to-all-start = ((f32[8,2,128,256]{3,2,1,0:T(8,128)}), f32[8,2,128,256]{3,2,1,0:T(8,128)}, u32[]{:S(2)}, u32[]{:S(2)}) async-start(f32[8,2,128,256]{3,2,1,0:T(8,128)} %bitcast.42), calls=%async_computation | async-start | bytes 4194304 | tf_op jit(solution)/shard_map/all_to_all | solution.py:256
  77.3 1.1 pad.14.ghost_hbm
  78.4 33.7 %shard_map.65 = f32[16,128,256]{2,1,0:T(8,128)} custom-call(f32[8]{0:T(128)} %stack.55.coef, f32[1,32,256,256]{3,2,1,0:T(8,128)} %src_hbm.3, s32[32,256,256]{2,1,0:T(8,128)} %obs_hbm.3, f32[2,32,16,256]{3,2,1,0:T(8,128)} %pad.14.ghost_hbm, f32[2,32,288,128]{3,2,1,0:T(8,128)} %fusion.2.lanes_hbm), custom_call_target="tpu_custom_call" | custom-call | tf_op jit(solution)/shard_map/pallas_call | solution.py:280
  112.0 5.2 %all-to-all-start.1 = ((f32[8,2,128,256]{3,2,1,0:T(8,128)}), f32[8,2,128,256]{3,2,1,0:T(8,128)S(1)}, u32[]{:S(2)}, u32[]{:S(2)}) async-start(f32[8,2,128,256]{3,2,1,0:T(8,128)} %bitcast.41), calls=%async_computation.1 | async-start | bytes 4194304 | tf_op jit(solution)/shard_map/all_to_all | solution.py:256
  117.2 1.8 %reduce_sum.18 = f32[2,128,256]{2,1,0:T(8,128)S(1)} reduce(f32[8,2,128,256]{3,2,1,0:T(8,128)} %all-to-all-done, f32[]{:T(128)} %constant.10.clone.1), dimensions={0}, to_apply=%region_0.1 | reduce | flops 458752 | bytes 2359300 | tf_op jit(solution)/shard_map/reduce_sum | solution.py:256
  118.9 25.6 %all-to-all-done.1 = f32[8,2,128,256]{3,2,1,0:T(8,128)S(1)} async-done(((f32[8,2,128,256]{3,2,1,0:T(8,128)}), f32[8,2,128,256]{3,2,1,0:T(8,128)S(1)}, u32[]{:S(2)}, u32[]{:S(2)}) %all-to-all-start.1) | async-done | bytes 2097184 | tf_op jit(solution)/shard_map/all_to_all | solution.py:256
  144.7 0.8 pad_maximum_fusion.1
  (19 shorter events, 1.4 us)
Async XLA Ops:
  2.5 17.0 %collective-permute-start = (f32[2,32,4,256]{3,2,1,0:T(4,128)S(1)}, f32[2,32,4,256]{3,2,1,0:T(4,128)S(1)}, u32[]{:S(2)}, u32[]{:S(2)}) collective-permute-start(f32[2,32,4,256]{3,2,1,0:T(4,128)S(1)} %pad_maximum_fusion.2), channel_id=1, source_target_pairs={{0,4},{4,8},{8,12},{1,5},{5,9},{9,13},{2,6},{6,10},{10,14},{3,7},{... | collective-permute-start | bytes 786440 | tf_op jit(solution)/shard_map/ppermute | solution.py:65
  8.6 7.0 %copy-start = (f32[1,32,256,256]{3,2,1,0:T(8,128)S(1)}, f32[1,32,256,256]{3,2,1,0:T(8,128)}, u32[]{:S(2)}) copy-start(f32[1,32,256,256]{3,2,1,0:T(8,128)} %src_hbm.3) | copy-start | bytes 25165828
  8.6 7.0 %copy-start.1 = (s32[8]{0:T(128)S(1)}, s32[8]{0:T(128)}, u32[]{:S(2)}) copy-start(s32[8]{0:T(128)} %constant.34.clone) | copy-start | bytes 100
  8.6 11.6 %collective-permute-start.1 = (f32[2,32,4,256]{3,2,1,0:T(4,128)S(1)}, f32[2,32,4,256]{3,2,1,0:T(4,128)S(1)}, u32[]{:S(2)}, u32[]{:S(2)}) collective-permute-start(f32[2,32,4,256]{3,2,1,0:T(4,128)S(1)} %pad_maximum_fusion.3), channel_id=1, source_target_pairs={{4,0},{8,4},{12,8},{5,1},{9,5},{13,9},{6,2},{10,6},{14,10},{7,3},{... | collective-permute-start | bytes 786440 | tf_op jit(solution)/shard_map/ppermute | solution.py:66
  19.4 9.6 %copy-start.2 = (s32[8]{0:T(128)S(1)}, s32[8]{0:T(128)}, u32[]{:S(2)}) copy-start(s32[8]{0:T(128)} %constant.35.clone) | copy-start | bytes 100
  21.4 10.1 %collective-permute-start.2 = (f32[2,32,4,264]{3,2,1,0:T(4,128)S(1)}, f32[2,32,4,264]{3,2,1,0:T(4,128)S(1)}, u32[]{:S(2)}, u32[]{:S(2)}) collective-permute-start(f32[2,32,4,264]{3,2,1,0:T(4,128)S(1)} %get-tuple-element.12), channel_id=1, source_target_pairs={{1,0},{2,1},{3,2},{5,4},{6,5},{7,6},{9,8},{10,9},{11,10},{13,12},{... | collective-permute-start | bytes 811016 | tf_op jit(solution)/shard_map/ppermute | solution.py:77
  22.7 10.6 %collective-permute-start.3 = (f32[2,32,4,264]{3,2,1,0:T(4,128)S(1)}, f32[2,32,4,264]{3,2,1,0:T(4,128)S(1)}, u32[]{:S(2)}, u32[]{:S(2)}) collective-permute-start(f32[2,32,4,264]{3,2,1,0:T(4,128)S(1)} %get-tuple-element.13), channel_id=1, source_target_pairs={{0,1},{1,2},{2,3},{4,5},{5,6},{6,7},{8,9},{9,10},{10,11},{12,13},{... | collective-permute-start | bytes 811016 | tf_op jit(solution)/shard_map/ppermute | solution.py:76
  72.0 40.0 %all-to-all-start = ((f32[8,2,128,256]{3,2,1,0:T(8,128)}), f32[8,2,128,256]{3,2,1,0:T(8,128)}, u32[]{:S(2)}, u32[]{:S(2)}) async-start(f32[8,2,128,256]{3,2,1,0:T(8,128)} %bitcast.42), calls=%async_computation | async-start | bytes 4194304 | tf_op jit(solution)/shard_map/all_to_all | solution.py:256
  112.0 32.5 %all-to-all-start.1 = ((f32[8,2,128,256]{3,2,1,0:T(8,128)}), f32[8,2,128,256]{3,2,1,0:T(8,128)S(1)}, u32[]{:S(2)}, u32[]{:S(2)}) async-start(f32[8,2,128,256]{3,2,1,0:T(8,128)} %bitcast.41), calls=%async_computation.1 | async-start | bytes 4194304 | tf_op jit(solution)/shard_map/all_to_all | solution.py:256

commit v9 on v8

--- a/solution.py
+++ b/solution.py
@@ -88,8 +88,8 @@
     return r_lo, r_hi, lanes
 
 
-def make_kernel(nz, nx, ny, rz, half):
-    nh = nx // 2
+def make_kernel(nz, nx, ny, rz, xs, nh):
+    half = 0 if xs == 0 else 1
     rows = nh + 2 * PAD
     width = ny + EXTRA
     nblk = rows // RB
@@ -97,11 +97,11 @@
     b_last = nblk - 2
     acc_lo = PAD // RB
     acc_hi = (PAD + nh) // RB
-    nb = nh + PAD
-    s0 = 0 if half == 0 else nx - nb
-    b0 = PAD if half == 0 else 0
-    g0 = 0 if half == 0 else nb
-    lane0 = 0 if half == 0 else nh
+    s0 = max(0, xs - PAD)
+    nb = min(nx, xs + nh + PAD) - s0
+    b0 = s0 - (xs - PAD)
+    g0 = 0 if half == 0 else PAD + nh
+    lane0 = xs
 
     def kernel(coef, src_hbm, obs_hbm, ghost_hbm, lanes_hbm, out_ref,
                a_buf, b_buf, o_buf, obs_buf, sems, s_buf, n_buf):
@@ -238,11 +238,11 @@
             step(bufs[n % 2], bufs[(n + 1) % 2], n == 0)
 
         def leth(z, c):
-            for q in range(nh // 32):
-                load = out_ref[z, pl.ds(q * 32, 32), :]
+            for q in range(nh // 16):
+                load = out_ref[z, pl.ds(q * 16, 16), :]
                 probit = probit_a + probit_b * jnp.log(load + load_eps)
                 lethal = 0.5 * (1.0 + lax.erf((probit - 5.0) / math.sqrt(2.0)))
-                out_ref[z, pl.ds(q * 32, 32), :] = weight * lethal
+                out_ref[z, pl.ds(q * 16, 16), :] = weight * lethal
             return c
 
         lax.fori_loop(0, rz, leth, 0)
@@ -271,14 +271,15 @@
          weight, jnp.float32(0.0)]
     ).astype(jnp.float32)
     r_lo, r_hi, lanes = ghost_pieces(src, obstacle)
-    nh = nx // 2
-    rows = nh + 2 * PAD
+    first_rows = (nx // 2 + 16) // 16 * 16
     width = ny + EXTRA
     any_spec = pl.BlockSpec(memory_space=pl.ANY)
     halves = []
-    for half, ghost in ((0, r_lo), (1, r_hi)):
+    for half, ghost, xs, nh in ((0, r_lo, 0, first_rows), (1, r_hi, first_rows, nx - first_rows)):
+        rows = nh + 2 * PAD
+        nb = min(nx, xs + nh + PAD) - max(0, xs - PAD)
         halves.append(pl.pallas_call(
-            make_kernel(nz, nx, ny, RZ, half),
+            make_kernel(nz, nx, ny, RZ, xs, nh),
             out_shape=jax.ShapeDtypeStruct((RZ, nh, ny), jnp.float32),
             in_specs=[pl.BlockSpec(memory_space=pltpu.SMEM)] + [any_spec] * 4,
             out_specs=pl.BlockSpec(memory_space=pltpu.VMEM),
@@ -286,7 +287,7 @@
                 pltpu.VMEM((nz, rows, width), jnp.float32),
                 pltpu.VMEM((nz, rows, width), jnp.float32),
                 pltpu.VMEM((nz, rows, width), jnp.float32),
-                pltpu.VMEM((nz, nh + PAD, ny), jnp.int32),
+                pltpu.VMEM((nz, nb, ny), jnp.int32),
                 pltpu.SemaphoreType.DMA((8,)),
                 pltpu.VMEM((rows, width), jnp.float32),
                 pltpu.VMEM((rows, width), jnp.float32),

time: 146 us -> 156 us (1.068)
  waiting for transfers between devices: 28.7 us -> 34.9 us
  Pallas kernels: 67.3 us -> 70.1 us
  local copies, waits for them, and re-layouts: 4.13 us -> 6.38 us
    ppermute x1, waiting for transfers between devices: 1.33 us -> 4.12 us  [ghost_pieces(): ye = lax.ppermute(ext[:, :, :H], 'gy', by)]
    pallas_call x2, Pallas kernels: 67.3 us -> 70.1 us  [on_device(): pl.pallas_call(make_kernel(nz, nx, ny, RZ, xs, nh), out_shape=jax.ShapeDt...]
    all_to_all x2, waiting for transfers between devices: 25.6 us -> 28.2 us  [_reduce_sync(): return lax.all_to_all(parts, 'scen', 0, 0, tiled=True).sum(0)]
  transfers between devices with their start and end apart: 6 -> 6, of which waited for: 3 -> 3; matrix products, arithmetic and copies ran while one was open for 10% -> 10% of each run, Pallas kernels for 23% -> 24%
where the time goes in v9:
time: 156 us
  Pallas kernels  70.1 us (45%)
  waiting for transfers between devices  34.9 us (22%)
  starting transfers between devices  23.3 us (15%)
  matrix products  13 us (8%)
  local copies, waits for them, and re-layouts  6.38 us (4%)
  other arithmetic  6.34 us (4%)
  between operations  1.66 us (1%)
    pallas_call x2, Pallas kernels, on_device(): pl.pallas_call(make_kernel(nz, nx, ny, RZ, xs, nh), out_shape=jax.ShapeDt...  70.1 us
    all_to_all x2, waiting for transfers between devices, _reduce_sync(): return lax.all_to_all(parts, 'scen', 0, 0, tiled=True).sum(0)  28.2 us
    all_to_all x2, starting transfers between devices, _reduce_sync(): return lax.all_to_all(parts, 'scen', 0, 0, tiled=True).sum(0)  10.3 us
    ppermute x1, starting transfers between devices, ghost_pieces(): xlo = lax.ppermute(last_rows, 'gx', fx)  4.92 us
    dot_general x1, matrix products, ghost_pieces(): jnp.einsum('zxy,ky->zkx', (1 - obs).astype(jnp.bfloat16), pick.astype(jnp...  4.59 us
    dot_general x1, matrix products, ghost_pieces(): jnp.einsum('czkr,kj->czrj', jnp.concatenate(_split3(yt), 2), place, prefe...  4.54 us
    ppermute x1, waiting for transfers between devices, ghost_pieces(): ye = lax.ppermute(ext[:, :, :H], 'gy', by)  4.12 us
    dot_general x1, matrix products, ghost_pieces(): src_cols = jnp.einsum('zxy,ky->zkx', src, pick, precision=hi)  3.89 us
  transfers between devices with their start and end apart: 6, of which 3 were waited for; matrix products, arithmetic and copies ran while one was open for 10% of the time, Pallas kernels for 24%

profile of v9, /device:TPU:1, one launch (start us, length us, event | category | flops | bytes accessed | tf_op | source)
XLA Modules:
  0.0 155.8 jit_solution(2525418305420881559)
XLA Ops:
  0.0 1.1 convert_bitcast_fusion.1
  1.1 1.3 fusion.13
  2.5 3.3 %collective-permute-start.1 = (f32[2,32,4,256]{3,2,1,0:T(4,128)S(1)}, f32[2,32,4,256]{3,2,1,0:T(4,128)S(1)}, u32[]{:S(2)}, u32[]{:S(2)}) collective-permute-start(f32[2,32,4,256]{3,2,1,0:T(4,128)S(1)} %pad_maximum_fusion.3), channel_id=1, source_target_pairs={{4,0},{8,4},{12,8},{5,1},{9,5},{13,9},{6,2},{10,6},{14,10},{7,3},{... | collective-permute-start | bytes 786440 | tf_op jit(solution)/shard_map/ppermute | solution.py:66
  5.8 4.9 %collective-permute-start = (f32[2,32,4,256]{3,2,1,0:T(4,128)S(1)}, f32[2,32,4,256]{3,2,1,0:T(4,128)S(1)}, u32[]{:S(2)}, u32[]{:S(2)}) collective-permute-start(f32[2,32,4,256]{3,2,1,0:T(4,128)S(1)} %pad_maximum_fusion.2), channel_id=1, source_target_pairs={{0,4},{4,8},{8,12},{1,5},{5,9},{9,13},{2,6},{6,10},{10,14},{3,7},{... | collective-permute-start | bytes 786440 | tf_op jit(solution)/shard_map/ppermute | solution.py:65
  10.8 4.6 %fusion = f32[8,32,256]{2,0,1:T(8,128)S(1)} fusion(s32[32,256,256]{2,1,0:T(8,128)} %obs_hbm.3, s32[8]{0:T(128)} %constant.34.clone), kind=kOutput, calls=%fused_computation.1 | convolution fusion | flops 37754880 | bytes 8650784 | tf_op jit(solution)/shard_map/zxy,ky->zkx/dot_general | solution.py:69
  15.4 3.9 %fusion.9 = f32[1,32,8,256]{3,2,1,0:T(8,128)S(1)} fusion(f32[8,32,256]{2,0,1:T(8,128)S(1)} %fusion, s32[8]{0:T(128)S(1)} %copy-done.3, f32[1,32,256,256]{3,2,1,0:T(8,128)S(1)} %copy-done), kind=kOutput, calls=%fused_computation.13 | convolution fusion | flops 201394176 | bytes 8912928 | tf_op jit(solution)/shard_map/zxy,ky->zkx/dot_general | solution.py:68
  19.6 0.4 copy.16
  21.2 3.6 %collective-permute-start.3 = (f32[2,32,4,264]{3,2,1,0:T(4,128)S(1)}, f32[2,32,4,264]{3,2,1,0:T(4,128)S(1)}, u32[]{:S(2)}, u32[]{:S(2)}) collective-permute-start(f32[2,32,4,264]{3,2,1,0:T(4,128)S(1)} %get-tuple-element.13), channel_id=1, source_target_pairs={{0,1},{1,2},{2,3},{4,5},{5,6},{6,7},{8,9},{9,10},{10,11},{12,13},{... | collective-permute-start | bytes 811016 | tf_op jit(solution)/shard_map/ppermute | solution.py:76
  24.8 1.3 collective-permute-start.2
  27.6 0.7 stack.55.coef
  28.3 1.1 pad.14.ghost_hbm
  29.4 2.6 %collective-permute-done.3 = f32[2,32,4,264]{3,2,1,0:T(4,128)S(1)} collective-permute-done((f32[2,32,4,264]{3,2,1,0:T(4,128)S(1)}, f32[2,32,4,264]{3,2,1,0:T(4,128)S(1)}, u32[]{:S(2)}, u32[]{:S(2)}) %collective-permute-start.3) | collective-permute-done | bytes 270368 | tf_op jit(solution)/shard_map/ppermute | solution.py:76
  32.0 4.1 %collective-permute-done.2 = f32[2,32,4,264]{3,2,1,0:T(4,128)S(1)} collective-permute-done((f32[2,32,4,264]{3,2,1,0:T(4,128)S(1)}, f32[2,32,4,264]{3,2,1,0:T(4,128)S(1)}, u32[]{:S(2)}, u32[]{:S(2)}) %collective-permute-start.2) | collective-permute-done | bytes 270368 | tf_op jit(solution)/shard_map/ppermute | solution.py:77
  36.1 0.5 reduce-precision_convert_fusion.1
  36.7 4.5 %fusion.2.lanes_hbm = f32[2,32,288,128]{3,2,1,0:T(8,128)} fusion(bf16[2,32,8,288]{3,2,1,0:T(8,128)(2,1)S(1)} %get-tuple-element.10, bf16[2,32,8,288]{3,2,1,0:T(8,128)(2,1)S(1)} %get-tuple-element.11, bf16[2,32,8,288]{3,2,1,0:T(8,128)(2,1)S(1)} %get-tuple-element.9, pred[8,128]{1,0:T(8,128)(4,1)S(1)} %iota_compare_fusion.3), kind=kOutput, calls=%fused_computation.5 | convolution fusion | flops 115912704 | bytes 10322944 | tf_op jit(solution)/shard_map/czkr,kj->czrj/dot_general | solution.py:83
  41.2 32.5 %shard_map.65 = f32[16,112,256]{2,1,0:T(8,128)} custom-call(f32[8]{0:T(128)} %stack.55.coef, f32[1,32,256,256]{3,2,1,0:T(8,128)} %src_hbm.3, s32[32,256,256]{2,1,0:T(8,128)} %obs_hbm.3, f32[2,32,16,256]{3,2,1,0:T(8,128)} %pad.14.ghost_hbm, f32[2,32,288,128]{3,2,1,0:T(8,128)} %fusion.2.lanes_hbm), custom_call_target="tpu_custom_call" | custom-call | tf_op jit(solution)/shard_map/pallas_call | solution.py:281
  73.7 5.1 %all-to-all-start.1 = ((f32[8,2,112,256]{3,2,1,0:T(8,128)}), f32[8,2,112,256]{3,2,1,0:T(8,128)S(1)}, u32[]{:S(2)}, u32[]{:S(2)}) async-start(f32[8,2,112,256]{3,2,1,0:T(8,128)} %bitcast.42), calls=%async_computation.1 | async-start | bytes 3670016 | tf_op jit(solution)/shard_map/all_to_all | solution.py:256
  78.9 2.1 %pad.12.ghost_hbm = f32[2,32,16,256]{3,2,1,0:T(8,128)} pad(f32[2,32,4,256]{3,2,1,0:T(4,128)} %copy-done.2, f32[]{:T(128)} %constant.10.clone.1), padding=0_0x0_0x12_0x0_0 | pad | bytes 1310724 | tf_op jit(solution)/shard_map/jit(_pad)/pad | solution.py:86
  80.9 37.6 %shard_map.64 = f32[16,144,256]{2,1,0:T(8,128)} custom-call(f32[8]{0:T(128)} %stack.55.coef, f32[1,32,256,256]{3,2,1,0:T(8,128)} %src_hbm.3, s32[32,256,256]{2,1,0:T(8,128)} %obs_hbm.3, f32[2,32,16,256]{3,2,1,0:T(8,128)} %pad.12.ghost_hbm, f32[2,32,288,128]{3,2,1,0:T(8,128)} %fusion.2.lanes_hbm), custom_call_target="tpu_custom_call" | custom-call | tf_op jit(solution)/shard_map/pallas_call | solution.py:281
  118.5 1.3 copy-done.1
  119.8 5.1 %all-to-all-start = ((f32[8,2,144,256]{3,2,1,0:T(8,128)}), f32[8,2,144,256]{3,2,1,0:T(8,128)S(1)}, u32[]{:S(2)}, u32[]{:S(2)}) async-start(f32[8,2,144,256]{3,2,1,0:T(8,128)} %bitcast.41), calls=%async_computation | async-start | bytes 4718592 | tf_op jit(solution)/shard_map/all_to_all | solution.py:256
  124.9 1.6 %reduce_sum.19 = f32[2,112,256]{2,1,0:T(8,128)S(1)} reduce(f32[8,2,112,256]{3,2,1,0:T(8,128)} %copy-done.1, f32[]{:T(128)} %constant.10.clone.1), dimensions={0}, to_apply=%region_1.2 | reduce | flops 401408 | bytes 2064388 | tf_op jit(solution)/shard_map/reduce_sum | solution.py:256
  126.6 28.2 %all-to-all-done = f32[8,2,144,256]{3,2,1,0:T(8,128)S(1)} async-done(((f32[8,2,144,256]{3,2,1,0:T(8,128)}), f32[8,2,144,256]{3,2,1,0:T(8,128)S(1)}, u32[]{:S(2)}, u32[]{:S(2)}) %all-to-all-start) | async-done | bytes 2359328 | tf_op jit(solution)/shard_map/all_to_all | solution.py:256
  154.9 0.8 pad_maximum_fusion.1
  (23 shorter events, 1.8 us)
Async XLA Ops:
  2.5 16.8 %collective-permute-start.1 = (f32[2,32,4,256]{3,2,1,0:T(4,128)S(1)}, f32[2,32,4,256]{3,2,1,0:T(4,128)S(1)}, u32[]{:S(2)}, u32[]{:S(2)}) collective-permute-start(f32[2,32,4,256]{3,2,1,0:T(4,128)S(1)} %pad_maximum_fusion.3), channel_id=1, source_target_pairs={{4,0},{8,4},{12,8},{5,1},{9,5},{13,9},{6,2},{10,6},{14,10},{7,3},{... | collective-permute-start | bytes 786440 | tf_op jit(solution)/shard_map/ppermute | solution.py:66
  5.8 9.5 %copy-start = (f32[1,32,256,256]{3,2,1,0:T(8,128)S(1)}, f32[1,32,256,256]{3,2,1,0:T(8,128)}, u32[]{:S(2)}) copy-start(f32[1,32,256,256]{3,2,1,0:T(8,128)} %src_hbm.3) | copy-start | bytes 25165828
  5.8 9.5 %copy-start.3 = (s32[8]{0:T(128)S(1)}, s32[8]{0:T(128)}, u32[]{:S(2)}) copy-start(s32[8]{0:T(128)} %constant.34.clone) | copy-start | bytes 100
  5.8 14.2 %collective-permute-start = (f32[2,32,4,256]{3,2,1,0:T(4,128)S(1)}, f32[2,32,4,256]{3,2,1,0:T(4,128)S(1)}, u32[]{:S(2)}, u32[]{:S(2)}) collective-permute-start(f32[2,32,4,256]{3,2,1,0:T(4,128)S(1)} %pad_maximum_fusion.2), channel_id=1, source_target_pairs={{0,4},{4,8},{8,12},{1,5},{5,9},{9,13},{2,6},{6,10},{10,14},{3,7},{... | collective-permute-start | bytes 786440 | tf_op jit(solution)/shard_map/ppermute | solution.py:65
  19.3 9.0 %copy-start.4 = (s32[8]{0:T(128)S(1)}, s32[8]{0:T(128)}, u32[]{:S(2)}) copy-start(s32[8]{0:T(128)} %constant.35.clone) | copy-start | bytes 100
  20.0 12.0 %copy-start.2 = (f32[2,32,4,256]{3,2,1,0:T(4,128)}, f32[2,32,4,256]{3,2,1,0:T(4,128)S(1)}, u32[]{:S(2)}) copy-start(f32[2,32,4,256]{3,2,1,0:T(4,128)S(1)} %collective-permute-done) | copy-start | bytes 786436
  21.2 10.8 %collective-permute-start.3 = (f32[2,32,4,264]{3,2,1,0:T(4,128)S(1)}, f32[2,32,4,264]{3,2,1,0:T(4,128)S(1)}, u32[]{:S(2)}, u32[]{:S(2)}) collective-permute-start(f32[2,32,4,264]{3,2,1,0:T(4,128)S(1)} %get-tuple-element.13), channel_id=1, source_target_pairs={{0,1},{1,2},{2,3},{4,5},{5,6},{6,7},{8,9},{9,10},{10,11},{12,13},{... | collective-permute-start | bytes 811016 | tf_op jit(solution)/shard_map/ppermute | solution.py:76
  24.8 11.4 %collective-permute-start.2 = (f32[2,32,4,264]{3,2,1,0:T(4,128)S(1)}, f32[2,32,4,264]{3,2,1,0:T(4,128)S(1)}, u32[]{:S(2)}, u32[]{:S(2)}) collective-permute-start(f32[2,32,4,264]{3,2,1,0:T(4,128)S(1)} %get-tuple-element.12), channel_id=1, source_target_pairs={{1,0},{2,1},{3,2},{5,4},{6,5},{7,6},{9,8},{10,9},{11,10},{13,12},{... | collective-permute-start | bytes 811016 | tf_op jit(solution)/shard_map/ppermute | solution.py:77
  73.7 44.8 %all-to-all-start.1 = ((f32[8,2,112,256]{3,2,1,0:T(8,128)}), f32[8,2,112,256]{3,2,1,0:T(8,128)S(1)}, u32[]{:S(2)}, u32[]{:S(2)}) async-start(f32[8,2,112,256]{3,2,1,0:T(8,128)} %bitcast.42), calls=%async_computation.1 | async-start | bytes 3670016 | tf_op jit(solution)/shard_map/all_to_all | solution.py:256
  118.5 1.3 copy-start.1
  119.8 35.0 %all-to-all-start = ((f32[8,2,144,256]{3,2,1,0:T(8,128)}), f32[8,2,144,256]{3,2,1,0:T(8,128)S(1)}, u32[]{:S(2)}, u32[]{:S(2)}) async-start(f32[8,2,144,256]{3,2,1,0:T(8,128)} %bitcast.41), calls=%async_computation | async-start | bytes 4718592 | tf_op jit(solution)/shard_map/all_to_all | solution.py:256

commit v10 on v8

--- a/solution.py
+++ b/solution.py
@@ -83,9 +83,7 @@
     lanes = jnp.einsum(
         "czkr,kj->czrj", jnp.concatenate(_split3(yt), 2), place,
         preferred_element_type=jnp.float32)
-    r_lo = jnp.pad(xlo, ((0, 0), (0, 0), (PAD - H, 0), (0, 0)))
-    r_hi = jnp.pad(xhi, ((0, 0), (0, 0), (0, PAD - H), (0, 0)))
-    return r_lo, r_hi, lanes
+    return xlo, xhi, lanes
 
 
 def make_kernel(nz, nx, ny, rz, half):
@@ -100,17 +98,17 @@
     nb = nh + PAD
     s0 = 0 if half == 0 else nx - nb
     b0 = PAD if half == 0 else 0
-    g0 = 0 if half == 0 else nb
+    g0 = PAD - H if half == 0 else nb
     lane0 = 0 if half == 0 else nh
 
     def kernel(coef, src_hbm, obs_hbm, ghost_hbm, lanes_hbm, out_ref,
                a_buf, b_buf, o_buf, obs_buf, sems, s_buf, n_buf):
         copies = [
             pltpu.make_async_copy(obs_hbm.at[:, pl.ds(s0, nb), :], obs_buf, sems.at[0]),
-            pltpu.make_async_copy(ghost_hbm.at[1], o_buf.at[:, pl.ds(g0, PAD), pl.ds(0, ny)], sems.at[1]),
+            pltpu.make_async_copy(ghost_hbm.at[1], o_buf.at[:, pl.ds(g0, H), pl.ds(0, ny)], sems.at[1]),
             pltpu.make_async_copy(lanes_hbm.at[1, :, pl.ds(lane0, rows)], o_buf.at[:, :, pl.ds(ny, EXTRA)], sems.at[3]),
             pltpu.make_async_copy(src_hbm.at[0, :, pl.ds(s0, nb), :], a_buf.at[:, pl.ds(b0, nb), pl.ds(0, ny)], sems.at[4]),
-            pltpu.make_async_copy(ghost_hbm.at[0], a_buf.at[:, pl.ds(g0, PAD), pl.ds(0, ny)], sems.at[5]),
+            pltpu.make_async_copy(ghost_hbm.at[0], a_buf.at[:, pl.ds(g0, H), pl.ds(0, ny)], sems.at[5]),
             pltpu.make_async_copy(lanes_hbm.at[0, :, pl.ds(lane0, rows)], a_buf.at[:, :, pl.ds(ny, EXTRA)], sems.at[7]),
         ]
         for cp in copies:

time: 146 us -> 145 us (level)
  local copies, waits for them, and re-layouts: 4.13 us -> 1.91 us
  waiting for transfers between devices: 28.7 us -> 30.6 us
    pad x2 -> x0, local copies, waits for them, and re-layouts: 2.24 us -> none  [the longest x1 1.14 us: ghost_pieces(): r_lo = jnp.pad(xlo, ((0, 0), (0, 0), (PAD - H, 0), (0, 0)))]
    ppermute x1, waiting for transfers between devices: 1.33 us -> 3.29 us  [ghost_pieces(): ye = lax.ppermute(ext[:, :, :H], 'gy', by)]
  transfers between devices with their start and end apart: 6 -> 6, of which waited for: 3 -> 3; matrix products, arithmetic and copies ran while one was open for 10% -> 8% of each run, Pallas kernels for 23% -> 23%
where the time goes in v10:
time: 145 us
  Pallas kernels  67 us (46%)
  waiting for transfers between devices  30.6 us (21%)
  starting transfers between devices  24.1 us (17%)
  matrix products  13 us (9%)
  other arithmetic  6.44 us (4%)
  local copies, waits for them, and re-layouts  1.91 us (1%)
  between operations  1.66 us (1%)
    pallas_call x2, Pallas kernels, on_device(): pl.pallas_call(make_kernel(nz, nx, ny, RZ, half), out_shape=jax.ShapeDtyp...  67 us
    all_to_all x2, waiting for transfers between devices, _reduce_sync(): return lax.all_to_all(parts, 'scen', 0, 0, tiled=True).sum(0)  25.6 us
    all_to_all x2, starting transfers between devices, _reduce_sync(): return lax.all_to_all(parts, 'scen', 0, 0, tiled=True).sum(0)  10.4 us
    ppermute x1, starting transfers between devices, ghost_pieces(): xlo = lax.ppermute(last_rows, 'gx', fx)  4.92 us
    dot_general x1, matrix products, ghost_pieces(): jnp.einsum('zxy,ky->zkx', (1 - obs).astype(jnp.bfloat16), pick.astype(jnp...  4.59 us
    dot_general x1, matrix products, ghost_pieces(): jnp.einsum('czkr,kj->czrj', jnp.concatenate(_split3(yt), 2), place, prefe...  4.56 us
    ppermute x1, starting transfers between devices, ghost_pieces(): yw = lax.ppermute(ext[:, :, H:], 'gy', fy)  4.19 us
    dot_general x1, matrix products, ghost_pieces(): src_cols = jnp.einsum('zxy,ky->zkx', src, pick, precision=hi)  3.89 us
  transfers between devices with their start and end apart: 6, of which 3 were waited for; matrix products, arithmetic and copies ran while one was open for 8% of the time, Pallas kernels for 23%

profile of v10, /device:TPU:1, one launch (start us, length us, event | category | flops | bytes accessed | tf_op | source)
XLA Modules:
  0.0 144.8 jit_solution(16894996097113939932)
XLA Ops:
  0.0 1.1 convert_bitcast_fusion.1
  1.1 1.3 fusion.13
  2.5 3.3 %collective-permute-start.1 = (f32[2,32,4,256]{3,2,1,0:T(4,128)S(1)}, f32[2,32,4,256]{3,2,1,0:T(4,128)S(1)}, u32[]{:S(2)}, u32[]{:S(2)}) collective-permute-start(f32[2,32,4,256]{3,2,1,0:T(4,128)S(1)} %pad_maximum_fusion.3), channel_id=1, source_target_pairs={{4,0},{8,4},{12,8},{5,1},{9,5},{13,9},{6,2},{10,6},{14,10},{7,3},{... | collective-permute-start | bytes 786440 | tf_op jit(solution)/shard_map/ppermute | solution.py:66
  5.8 4.9 %collective-permute-start = (f32[2,32,4,256]{3,2,1,0:T(4,128)S(1)}, f32[2,32,4,256]{3,2,1,0:T(4,128)S(1)}, u32[]{:S(2)}, u32[]{:S(2)}) collective-permute-start(f32[2,32,4,256]{3,2,1,0:T(4,128)S(1)} %pad_maximum_fusion.2), channel_id=1, source_target_pairs={{0,4},{4,8},{8,12},{1,5},{5,9},{9,13},{2,6},{6,10},{10,14},{3,7},{... | collective-permute-start | bytes 786440 | tf_op jit(solution)/shard_map/ppermute | solution.py:65
  10.8 4.6 %fusion = f32[8,32,256]{2,0,1:T(8,128)S(1)} fusion(s32[32,256,256]{2,1,0:T(8,128)} %obs_hbm.3, s32[8]{0:T(128)} %constant.34.clone), kind=kOutput, calls=%fused_computation.1 | convolution fusion | flops 37754880 | bytes 8650784 | tf_op jit(solution)/shard_map/zxy,ky->zkx/dot_general | solution.py:69
  15.4 3.9 %fusion.9 = f32[1,32,8,256]{3,2,1,0:T(8,128)S(1)} fusion(f32[8,32,256]{2,0,1:T(8,128)S(1)} %fusion, s32[8]{0:T(128)S(1)} %copy-done.3, f32[1,32,256,256]{3,2,1,0:T(8,128)S(1)} %copy-done), kind=kOutput, calls=%fused_computation.13 | convolution fusion | flops 201394176 | bytes 8912928 | tf_op jit(solution)/shard_map/zxy,ky->zkx/dot_general | solution.py:68
  19.6 0.4 copy.16
  20.3 0.4 copy.15
  20.8 0.3 pad_maximum_fusion
  21.2 1.3 collective-permute-start.2
  22.5 4.2 %collective-permute-start.3 = (f32[2,32,4,264]{3,2,1,0:T(4,128)S(1)}, f32[2,32,4,264]{3,2,1,0:T(4,128)S(1)}, u32[]{:S(2)}, u32[]{:S(2)}) collective-permute-start(f32[2,32,4,264]{3,2,1,0:T(4,128)S(1)} %get-tuple-element.13), channel_id=1, source_target_pairs={{0,1},{1,2},{2,3},{4,5},{5,6},{6,7},{8,9},{9,10},{10,11},{12,13},{... | collective-permute-start | bytes 811016 | tf_op jit(solution)/shard_map/ppermute | solution.py:76
  28.2 0.6 stack.55.coef
  28.9 3.3 %collective-permute-done.2 = f32[2,32,4,264]{3,2,1,0:T(4,128)S(1)} collective-permute-done((f32[2,32,4,264]{3,2,1,0:T(4,128)S(1)}, f32[2,32,4,264]{3,2,1,0:T(4,128)S(1)}, u32[]{:S(2)}, u32[]{:S(2)}) %collective-permute-start.2) | collective-permute-done | bytes 270368 | tf_op jit(solution)/shard_map/ppermute | solution.py:77
  32.2 1.8 %collective-permute-done.3 = f32[2,32,4,264]{3,2,1,0:T(4,128)S(1)} collective-permute-done((f32[2,32,4,264]{3,2,1,0:T(4,128)S(1)}, f32[2,32,4,264]{3,2,1,0:T(4,128)S(1)}, u32[]{:S(2)}, u32[]{:S(2)}) %collective-permute-start.3) | collective-permute-done | bytes 270368 | tf_op jit(solution)/shard_map/ppermute | solution.py:76
  34.0 0.5 reduce-precision_convert_fusion.1
  34.5 4.6 %fusion.2.lanes_hbm = f32[2,32,288,128]{3,2,1,0:T(8,128)} fusion(bf16[2,32,8,288]{3,2,1,0:T(8,128)(2,1)S(1)} %get-tuple-element.10, bf16[2,32,8,288]{3,2,1,0:T(8,128)(2,1)S(1)} %get-tuple-element.11, bf16[2,32,8,288]{3,2,1,0:T(8,128)(2,1)S(1)} %get-tuple-element.9, pred[8,128]{1,0:T(8,128)(4,1)S(1)} %iota_compare_fusion.3), kind=kOutput, calls=%fused_computation.5 | convolution fusion | flops 115912704 | bytes 10322944 | tf_op jit(solution)/shard_map/czkr,kj->czrj/dot_general | solution.py:83
  39.0 33.6 %shard_map.65 = f32[16,128,256]{2,1,0:T(8,128)} custom-call(f32[8]{0:T(128)} %stack.55.coef, f32[1,32,256,256]{3,2,1,0:T(8,128)} %src_hbm.3, s32[32,256,256]{2,1,0:T(8,128)} %obs_hbm.3, f32[2,32,4,256]{3,2,1,0:T(4,128)} %copy-done.1, f32[2,32,288,128]{3,2,1,0:T(8,128)} %fusion.2.lanes_hbm), custom_call_target="tpu_custom_call" | custom-call | tf_op jit(solution)/shard_map/pallas_call | solution.py:278
  72.6 5.2 %all-to-all-start.1 = ((f32[8,2,128,256]{3,2,1,0:T(8,128)}), f32[8,2,128,256]{3,2,1,0:T(8,128)}, u32[]{:S(2)}, u32[]{:S(2)}) async-start(f32[8,2,128,256]{3,2,1,0:T(8,128)} %bitcast.42), calls=%async_computation.1 | async-start | bytes 4194304 | tf_op jit(solution)/shard_map/all_to_all | solution.py:254
  77.8 33.4 %shard_map.64 = f32[16,128,256]{2,1,0:T(8,128)} custom-call(f32[8]{0:T(128)} %stack.55.coef, f32[1,32,256,256]{3,2,1,0:T(8,128)} %src_hbm.3, s32[32,256,256]{2,1,0:T(8,128)} %obs_hbm.3, f32[2,32,4,256]{3,2,1,0:T(4,128)} %copy-done.2, f32[2,32,288,128]{3,2,1,0:T(8,128)} %fusion.2.lanes_hbm), custom_call_target="tpu_custom_call" | custom-call | tf_op jit(solution)/shard_map/pallas_call | solution.py:278
  111.3 5.2 %all-to-all-start = ((f32[8,2,128,256]{3,2,1,0:T(8,128)}), f32[8,2,128,256]{3,2,1,0:T(8,128)S(1)}, u32[]{:S(2)}, u32[]{:S(2)}) async-start(f32[8,2,128,256]{3,2,1,0:T(8,128)} %bitcast.41), calls=%async_computation | async-start | bytes 4194304 | tf_op jit(solution)/shard_map/all_to_all | solution.py:254
  116.5 1.8 %reduce_sum.19 = f32[2,128,256]{2,1,0:T(8,128)S(1)} reduce(f32[8,2,128,256]{3,2,1,0:T(8,128)} %all-to-all-done.1, f32[]{:T(128)} %constant.10.clone.1), dimensions={0}, to_apply=%region_1.2 | reduce | flops 458752 | bytes 2359300 | tf_op jit(solution)/shard_map/reduce_sum | solution.py:254
  118.2 25.6 %all-to-all-done = f32[8,2,128,256]{3,2,1,0:T(8,128)S(1)} async-done(((f32[8,2,128,256]{3,2,1,0:T(8,128)}), f32[8,2,128,256]{3,2,1,0:T(8,128)S(1)}, u32[]{:S(2)}, u32[]{:S(2)}) %all-to-all-start) | async-done | bytes 2097184 | tf_op jit(solution)/shard_map/all_to_all | solution.py:254
  143.8 0.1 reduce_sum.18
  143.9 0.8 pad_maximum_fusion.1
  (21 shorter events, 0.9 us)
Async XLA Ops:
  2.5 16.8 %collective-permute-start.1 = (f32[2,32,4,256]{3,2,1,0:T(4,128)S(1)}, f32[2,32,4,256]{3,2,1,0:T(4,128)S(1)}, u32[]{:S(2)}, u32[]{:S(2)}) collective-permute-start(f32[2,32,4,256]{3,2,1,0:T(4,128)S(1)} %pad_maximum_fusion.3), channel_id=1, source_target_pairs={{4,0},{8,4},{12,8},{5,1},{9,5},{13,9},{6,2},{10,6},{14,10},{7,3},{... | collective-permute-start | bytes 786440 | tf_op jit(solution)/shard_map/ppermute | solution.py:66
  5.8 9.5 %copy-start = (f32[1,32,256,256]{3,2,1,0:T(8,128)S(1)}, f32[1,32,256,256]{3,2,1,0:T(8,128)}, u32[]{:S(2)}) copy-start(f32[1,32,256,256]{3,2,1,0:T(8,128)} %src_hbm.3) | copy-start | bytes 25165828
  5.8 9.5 %copy-start.3 = (s32[8]{0:T(128)S(1)}, s32[8]{0:T(128)}, u32[]{:S(2)}) copy-start(s32[8]{0:T(128)} %constant.34.clone) | copy-start | bytes 100
  5.8 14.2 %collective-permute-start = (f32[2,32,4,256]{3,2,1,0:T(4,128)S(1)}, f32[2,32,4,256]{3,2,1,0:T(4,128)S(1)}, u32[]{:S(2)}, u32[]{:S(2)}) collective-permute-start(f32[2,32,4,256]{3,2,1,0:T(4,128)S(1)} %pad_maximum_fusion.2), channel_id=1, source_target_pairs={{0,4},{4,8},{8,12},{1,5},{5,9},{9,13},{2,6},{6,10},{10,14},{3,7},{... | collective-permute-start | bytes 786440 | tf_op jit(solution)/shard_map/ppermute | solution.py:65
  19.3 9.6 %copy-start.4 = (s32[8]{0:T(128)S(1)}, s32[8]{0:T(128)}, u32[]{:S(2)}) copy-start(s32[8]{0:T(128)} %constant.35.clone) | copy-start | bytes 100
  19.3 19.8 %copy-start.1 = (f32[2,32,4,256]{3,2,1,0:T(4,128)}, f32[2,32,4,256]{3,2,1,0:T(4,128)S(1)}, u32[]{:S(2)}) copy-start(f32[2,32,4,256]{3,2,1,0:T(4,128)S(1)} %collective-permute-done.1.ghost_hbm) | copy-start | bytes 786436
  20.0 19.0 %copy-start.2 = (f32[2,32,4,256]{3,2,1,0:T(4,128)}, f32[2,32,4,256]{3,2,1,0:T(4,128)S(1)}, u32[]{:S(2)}) copy-start(f32[2,32,4,256]{3,2,1,0:T(4,128)S(1)} %collective-permute-done.ghost_hbm) | copy-start | bytes 786436
  21.2 11.0 %collective-permute-start.2 = (f32[2,32,4,264]{3,2,1,0:T(4,128)S(1)}, f32[2,32,4,264]{3,2,1,0:T(4,128)S(1)}, u32[]{:S(2)}, u32[]{:S(2)}) collective-permute-start(f32[2,32,4,264]{3,2,1,0:T(4,128)S(1)} %get-tuple-element.12), channel_id=1, source_target_pairs={{1,0},{2,1},{3,2},{5,4},{6,5},{7,6},{9,8},{10,9},{11,10},{13,12},{... | collective-permute-start | bytes 811016 | tf_op jit(solution)/shard_map/ppermute | solution.py:77
  22.5 11.4 %collective-permute-start.3 = (f32[2,32,4,264]{3,2,1,0:T(4,128)S(1)}, f32[2,32,4,264]{3,2,1,0:T(4,128)S(1)}, u32[]{:S(2)}, u32[]{:S(2)}) collective-permute-start(f32[2,32,4,264]{3,2,1,0:T(4,128)S(1)} %get-tuple-element.13), channel_id=1, source_target_pairs={{0,1},{1,2},{2,3},{4,5},{5,6},{6,7},{8,9},{9,10},{10,11},{12,13},{... | collective-permute-start | bytes 811016 | tf_op jit(solution)/shard_map/ppermute | solution.py:76
  72.6 38.7 %all-to-all-start.1 = ((f32[8,2,128,256]{3,2,1,0:T(8,128)}), f32[8,2,128,256]{3,2,1,0:T(8,128)}, u32[]{:S(2)}, u32[]{:S(2)}) async-start(f32[8,2,128,256]{3,2,1,0:T(8,128)} %bitcast.42), calls=%async_computation.1 | async-start | bytes 4194304 | tf_op jit(solution)/shard_map/all_to_all | solution.py:254
  111.3 32.5 %all-to-all-start = ((f32[8,2,128,256]{3,2,1,0:T(8,128)}), f32[8,2,128,256]{3,2,1,0:T(8,128)S(1)}, u32[]{:S(2)}, u32[]{:S(2)}) async-start(f32[8,2,128,256]{3,2,1,0:T(8,128)} %bitcast.41), calls=%async_computation | async-start | bytes 4194304 | tf_op jit(solution)/shard_map/all_to_all | solution.py:254

commit v11 on v10

--- a/solution.py
+++ b/solution.py
@@ -103,15 +103,30 @@
 
     def kernel(coef, src_hbm, obs_hbm, ghost_hbm, lanes_hbm, out_ref,
                a_buf, b_buf, o_buf, obs_buf, sems, s_buf, n_buf):
-        copies = [
-            pltpu.make_async_copy(obs_hbm.at[:, pl.ds(s0, nb), :], obs_buf, sems.at[0]),
-            pltpu.make_async_copy(ghost_hbm.at[1], o_buf.at[:, pl.ds(g0, H), pl.ds(0, ny)], sems.at[1]),
-            pltpu.make_async_copy(lanes_hbm.at[1, :, pl.ds(lane0, rows)], o_buf.at[:, :, pl.ds(ny, EXTRA)], sems.at[3]),
-            pltpu.make_async_copy(src_hbm.at[0, :, pl.ds(s0, nb), :], a_buf.at[:, pl.ds(b0, nb), pl.ds(0, ny)], sems.at[4]),
-            pltpu.make_async_copy(ghost_hbm.at[0], a_buf.at[:, pl.ds(g0, H), pl.ds(0, ny)], sems.at[5]),
-            pltpu.make_async_copy(lanes_hbm.at[0, :, pl.ds(lane0, rows)], a_buf.at[:, :, pl.ds(ny, EXTRA)], sems.at[7]),
+        groups = 4
+        per = nz // groups
+        obs_cp = [
+            pltpu.make_async_copy(
+                obs_hbm.at[pl.ds(g * per, per), pl.ds(s0, nb), :],
+                obs_buf.at[pl.ds(g * per, per)], sems.at[g])
+            for g in range(groups)
         ]
-        for cp in copies:
+        src_cp = [
+            pltpu.make_async_copy(
+                src_hbm.at[0, pl.ds(g * per, per), pl.ds(s0, nb), :],
+                a_buf.at[pl.ds(g * per, per), pl.ds(b0, nb), pl.ds(0, ny)], sems.at[groups + g])
+            for g in range(groups)
+        ]
+        rest = [
+            pltpu.make_async_copy(ghost_hbm.at[1], o_buf.at[:, pl.ds(g0, H), pl.ds(0, ny)], sems.at[2 * groups]),
+            pltpu.make_async_copy(ghost_hbm.at[0], a_buf.at[:, pl.ds(g0, H), pl.ds(0, ny)], sems.at[2 * groups + 1]),
+            pltpu.make_async_copy(lanes_hbm.at[1, :, pl.ds(lane0, rows)], o_buf.at[:, :, pl.ds(ny, EXTRA)], sems.at[2 * groups + 2]),
+            pltpu.make_async_copy(lanes_hbm.at[0, :, pl.ds(lane0, rows)], a_buf.at[:, :, pl.ds(ny, EXTRA)], sems.at[2 * groups + 3]),
+        ]
+        for g in range(groups):
+            obs_cp[g].start()
+            src_cp[g].start()
+        for cp in rest:
             cp.start()
 
         zeros = jnp.zeros((RB, width), jnp.float32)
@@ -123,14 +138,9 @@
 
         lax.fori_loop(0, nz, clear, 0)
 
-        copies[0].wait()
-
         def to_open(z, c):
             o_buf[z, pl.ds(b0, nb), pl.ds(0, ny)] = (1 - obs_buf[z]).astype(jnp.float32)
             return c
-
-        lax.fori_loop(0, nz, to_open, 0)
-        copies[3].wait()
 
         def to_c0(z, c):
             a_buf[z, pl.ds(b0, nb), pl.ds(0, ny)] = (
@@ -138,8 +148,12 @@
             )
             return c
 
-        lax.fori_loop(0, nz, to_c0, 0)
-        for cp in copies[1:3] + copies[4:]:
+        for g in range(groups):
+            obs_cp[g].wait()
+            lax.fori_loop(g * per, (g + 1) * per, to_open, 0)
+            src_cp[g].wait()
+            lax.fori_loop(g * per, (g + 1) * per, to_c0, 0)
+        for cp in rest:
             cp.wait()
 
         k_w = coef[0]
@@ -285,7 +299,7 @@
                 pltpu.VMEM((nz, rows, width), jnp.float32),
                 pltpu.VMEM((nz, rows, width), jnp.float32),
                 pltpu.VMEM((nz, nh + PAD, ny), jnp.int32),
-                pltpu.SemaphoreType.DMA((8,)),
+                pltpu.SemaphoreType.DMA((12,)),
                 pltpu.VMEM((rows, width), jnp.float32),
                 pltpu.VMEM((rows, width), jnp.float32),
             ],

time: 145 us -> 145 us (level)
  no operation moved by 1% of the time
where the time goes in v11:
time: 145 us
  Pallas kernels  67.1 us (46%)
  waiting for transfers between devices  30.6 us (21%)
  starting transfers between devices  24.1 us (17%)
  matrix products  13 us (9%)
  other arithmetic  6.44 us (4%)
  local copies, waits for them, and re-layouts  1.91 us (1%)
  between operations  1.66 us (1%)
    pallas_call x2, Pallas kernels, on_device(): pl.pallas_call(make_kernel(nz, nx, ny, RZ, half), out_shape=jax.ShapeDtyp...  67.1 us
    all_to_all x2, waiting for transfers between devices, _reduce_sync(): return lax.all_to_all(parts, 'scen', 0, 0, tiled=True).sum(0)  25.6 us
    all_to_all x2, starting transfers between devices, _reduce_sync(): return lax.all_to_all(parts, 'scen', 0, 0, tiled=True).sum(0)  10.4 us
    ppermute x1, starting transfers between devices, ghost_pieces(): xlo = lax.ppermute(last_rows, 'gx', fx)  4.92 us
    dot_general x1, matrix products, ghost_pieces(): jnp.einsum('zxy,ky->zkx', (1 - obs).astype(jnp.bfloat16), pick.astype(jnp...  4.59 us
    dot_general x1, matrix products, ghost_pieces(): jnp.einsum('czkr,kj->czrj', jnp.concatenate(_split3(yt), 2), place, prefe...  4.56 us
    ppermute x1, starting transfers between devices, ghost_pieces(): yw = lax.ppermute(ext[:, :, H:], 'gy', fy)  4.19 us
    dot_general x1, matrix products, ghost_pieces(): src_cols = jnp.einsum('zxy,ky->zkx', src, pick, precision=hi)  3.89 us
  transfers between devices with their start and end apart: 6, of which 3 were waited for; matrix products, arithmetic and copies ran while one was open for 8% of the time, Pallas kernels for 23%

profile of v11, /device:TPU:1, one launch (start us, length us, event | category | flops | bytes accessed | tf_op | source)
XLA Modules:
  0.0 144.9 jit_solution(11749053532816194823)
XLA Ops:
  0.0 1.1 convert_bitcast_fusion.1
  1.1 1.3 fusion.13
  2.5 3.3 %collective-permute-start.1 = (f32[2,32,4,256]{3,2,1,0:T(4,128)S(1)}, f32[2,32,4,256]{3,2,1,0:T(4,128)S(1)}, u32[]{:S(2)}, u32[]{:S(2)}) collective-permute-start(f32[2,32,4,256]{3,2,1,0:T(4,128)S(1)} %pad_maximum_fusion.3), channel_id=1, source_target_pairs={{4,0},{8,4},{12,8},{5,1},{9,5},{13,9},{6,2},{10,6},{14,10},{7,3},{... | collective-permute-start | bytes 786440 | tf_op jit(solution)/shard_map/ppermute | solution.py:66
  5.8 4.9 %collective-permute-start = (f32[2,32,4,256]{3,2,1,0:T(4,128)S(1)}, f32[2,32,4,256]{3,2,1,0:T(4,128)S(1)}, u32[]{:S(2)}, u32[]{:S(2)}) collective-permute-start(f32[2,32,4,256]{3,2,1,0:T(4,128)S(1)} %pad_maximum_fusion.2), channel_id=1, source_target_pairs={{0,4},{4,8},{8,12},{1,5},{5,9},{9,13},{2,6},{6,10},{10,14},{3,7},{... | collective-permute-start | bytes 786440 | tf_op jit(solution)/shard_map/ppermute | solution.py:65
  10.8 4.6 %fusion = f32[8,32,256]{2,0,1:T(8,128)S(1)} fusion(s32[32,256,256]{2,1,0:T(8,128)} %obs_hbm.3, s32[8]{0:T(128)} %constant.34.clone), kind=kOutput, calls=%fused_computation.1 | convolution fusion | flops 37754880 | bytes 8650784 | tf_op jit(solution)/shard_map/zxy,ky->zkx/dot_general | solution.py:69
  15.4 3.9 %fusion.9 = f32[1,32,8,256]{3,2,1,0:T(8,128)S(1)} fusion(f32[8,32,256]{2,0,1:T(8,128)S(1)} %fusion, s32[8]{0:T(128)S(1)} %copy-done.3, f32[1,32,256,256]{3,2,1,0:T(8,128)S(1)} %copy-done), kind=kOutput, calls=%fused_computation.13 | convolution fusion | flops 201394176 | bytes 8912928 | tf_op jit(solution)/shard_map/zxy,ky->zkx/dot_general | solution.py:68
  19.6 0.4 copy.16
  20.3 0.4 copy.15
  20.8 0.3 pad_maximum_fusion
  21.2 1.3 collective-permute-start.2
  22.5 4.2 %collective-permute-start.3 = (f32[2,32,4,264]{3,2,1,0:T(4,128)S(1)}, f32[2,32,4,264]{3,2,1,0:T(4,128)S(1)}, u32[]{:S(2)}, u32[]{:S(2)}) collective-permute-start(f32[2,32,4,264]{3,2,1,0:T(4,128)S(1)} %get-tuple-element.13), channel_id=1, source_target_pairs={{0,1},{1,2},{2,3},{4,5},{5,6},{6,7},{8,9},{9,10},{10,11},{12,13},{... | collective-permute-start | bytes 811016 | tf_op jit(solution)/shard_map/ppermute | solution.py:76
  28.2 0.6 stack.55.coef
  28.9 3.3 %collective-permute-done.2 = f32[2,32,4,264]{3,2,1,0:T(4,128)S(1)} collective-permute-done((f32[2,32,4,264]{3,2,1,0:T(4,128)S(1)}, f32[2,32,4,264]{3,2,1,0:T(4,128)S(1)}, u32[]{:S(2)}, u32[]{:S(2)}) %collective-permute-start.2) | collective-permute-done | bytes 270368 | tf_op jit(solution)/shard_map/ppermute | solution.py:77
  32.2 1.8 %collective-permute-done.3 = f32[2,32,4,264]{3,2,1,0:T(4,128)S(1)} collective-permute-done((f32[2,32,4,264]{3,2,1,0:T(4,128)S(1)}, f32[2,32,4,264]{3,2,1,0:T(4,128)S(1)}, u32[]{:S(2)}, u32[]{:S(2)}) %collective-permute-start.3) | collective-permute-done | bytes 270368 | tf_op jit(solution)/shard_map/ppermute | solution.py:76
  34.0 0.5 reduce-precision_convert_fusion.1
  34.5 4.6 %fusion.2.lanes_hbm = f32[2,32,288,128]{3,2,1,0:T(8,128)} fusion(bf16[2,32,8,288]{3,2,1,0:T(8,128)(2,1)S(1)} %get-tuple-element.10, bf16[2,32,8,288]{3,2,1,0:T(8,128)(2,1)S(1)} %get-tuple-element.11, bf16[2,32,8,288]{3,2,1,0:T(8,128)(2,1)S(1)} %get-tuple-element.9, pred[8,128]{1,0:T(8,128)(4,1)S(1)} %iota_compare_fusion.3), kind=kOutput, calls=%fused_computation.5 | convolution fusion | flops 115912704 | bytes 10322944 | tf_op jit(solution)/shard_map/czkr,kj->czrj/dot_general | solution.py:83
  39.0 33.6 %shard_map.65 = f32[16,128,256]{2,1,0:T(8,128)} custom-call(f32[8]{0:T(128)} %stack.55.coef, f32[1,32,256,256]{3,2,1,0:T(8,128)} %src_hbm.3, s32[32,256,256]{2,1,0:T(8,128)} %obs_hbm.3, f32[2,32,4,256]{3,2,1,0:T(4,128)} %copy-done.1, f32[2,32,288,128]{3,2,1,0:T(8,128)} %fusion.2.lanes_hbm), custom_call_target="tpu_custom_call" | custom-call | tf_op jit(solution)/shard_map/pallas_call | solution.py:292
  72.7 5.2 %all-to-all-start.1 = ((f32[8,2,128,256]{3,2,1,0:T(8,128)}), f32[8,2,128,256]{3,2,1,0:T(8,128)}, u32[]{:S(2)}, u32[]{:S(2)}) async-start(f32[8,2,128,256]{3,2,1,0:T(8,128)} %bitcast.42), calls=%async_computation.1 | async-start | bytes 4194304 | tf_op jit(solution)/shard_map/all_to_all | solution.py:268
  77.9 33.5 %shard_map.64 = f32[16,128,256]{2,1,0:T(8,128)} custom-call(f32[8]{0:T(128)} %stack.55.coef, f32[1,32,256,256]{3,2,1,0:T(8,128)} %src_hbm.3, s32[32,256,256]{2,1,0:T(8,128)} %obs_hbm.3, f32[2,32,4,256]{3,2,1,0:T(4,128)} %copy-done.2, f32[2,32,288,128]{3,2,1,0:T(8,128)} %fusion.2.lanes_hbm), custom_call_target="tpu_custom_call" | custom-call | tf_op jit(solution)/shard_map/pallas_call | solution.py:292
  111.4 5.2 %all-to-all-start = ((f32[8,2,128,256]{3,2,1,0:T(8,128)}), f32[8,2,128,256]{3,2,1,0:T(8,128)S(1)}, u32[]{:S(2)}, u32[]{:S(2)}) async-start(f32[8,2,128,256]{3,2,1,0:T(8,128)} %bitcast.41), calls=%async_computation | async-start | bytes 4194304 | tf_op jit(solution)/shard_map/all_to_all | solution.py:268
  116.5 1.8 %reduce_sum.19 = f32[2,128,256]{2,1,0:T(8,128)S(1)} reduce(f32[8,2,128,256]{3,2,1,0:T(8,128)} %all-to-all-done.1, f32[]{:T(128)} %constant.10.clone.1), dimensions={0}, to_apply=%region_1.2 | reduce | flops 458752 | bytes 2359300 | tf_op jit(solution)/shard_map/reduce_sum | solution.py:268
  118.3 25.6 %all-to-all-done = f32[8,2,128,256]{3,2,1,0:T(8,128)S(1)} async-done(((f32[8,2,128,256]{3,2,1,0:T(8,128)}), f32[8,2,128,256]{3,2,1,0:T(8,128)S(1)}, u32[]{:S(2)}, u32[]{:S(2)}) %all-to-all-start) | async-done | bytes 2097184 | tf_op jit(solution)/shard_map/all_to_all | solution.py:268
  143.9 0.1 reduce_sum.18
  144.0 0.8 pad_maximum_fusion.1
  (21 shorter events, 0.9 us)
Async XLA Ops:
  2.5 16.8 %collective-permute-start.1 = (f32[2,32,4,256]{3,2,1,0:T(4,128)S(1)}, f32[2,32,4,256]{3,2,1,0:T(4,128)S(1)}, u32[]{:S(2)}, u32[]{:S(2)}) collective-permute-start(f32[2,32,4,256]{3,2,1,0:T(4,128)S(1)} %pad_maximum_fusion.3), channel_id=1, source_target_pairs={{4,0},{8,4},{12,8},{5,1},{9,5},{13,9},{6,2},{10,6},{14,10},{7,3},{... | collective-permute-start | bytes 786440 | tf_op jit(solution)/shard_map/ppermute | solution.py:66
  5.8 9.5 %copy-start = (f32[1,32,256,256]{3,2,1,0:T(8,128)S(1)}, f32[1,32,256,256]{3,2,1,0:T(8,128)}, u32[]{:S(2)}) copy-start(f32[1,32,256,256]{3,2,1,0:T(8,128)} %src_hbm.3) | copy-start | bytes 25165828
  5.8 9.5 %copy-start.3 = (s32[8]{0:T(128)S(1)}, s32[8]{0:T(128)}, u32[]{:S(2)}) copy-start(s32[8]{0:T(128)} %constant.34.clone) | copy-start | bytes 100
  5.8 14.2 %collective-permute-start = (f32[2,32,4,256]{3,2,1,0:T(4,128)S(1)}, f32[2,32,4,256]{3,2,1,0:T(4,128)S(1)}, u32[]{:S(2)}, u32[]{:S(2)}) collective-permute-start(f32[2,32,4,256]{3,2,1,0:T(4,128)S(1)} %pad_maximum_fusion.2), channel_id=1, source_target_pairs={{0,4},{4,8},{8,12},{1,5},{5,9},{9,13},{2,6},{6,10},{10,14},{3,7},{... | collective-permute-start | bytes 786440 | tf_op jit(solution)/shard_map/ppermute | solution.py:65
  19.3 9.6 %copy-start.4 = (s32[8]{0:T(128)S(1)}, s32[8]{0:T(128)}, u32[]{:S(2)}) copy-start(s32[8]{0:T(128)} %constant.35.clone) | copy-start | bytes 100
  19.3 19.8 %copy-start.1 = (f32[2,32,4,256]{3,2,1,0:T(4,128)}, f32[2,32,4,256]{3,2,1,0:T(4,128)S(1)}, u32[]{:S(2)}) copy-start(f32[2,32,4,256]{3,2,1,0:T(4,128)S(1)} %collective-permute-done.1.ghost_hbm) | copy-start | bytes 786436
  20.0 19.0 %copy-start.2 = (f32[2,32,4,256]{3,2,1,0:T(4,128)}, f32[2,32,4,256]{3,2,1,0:T(4,128)S(1)}, u32[]{:S(2)}) copy-start(f32[2,32,4,256]{3,2,1,0:T(4,128)S(1)} %collective-permute-done.ghost_hbm) | copy-start | bytes 786436
  21.2 11.0 %collective-permute-start.2 = (f32[2,32,4,264]{3,2,1,0:T(4,128)S(1)}, f32[2,32,4,264]{3,2,1,0:T(4,128)S(1)}, u32[]{:S(2)}, u32[]{:S(2)}) collective-permute-start(f32[2,32,4,264]{3,2,1,0:T(4,128)S(1)} %get-tuple-element.12), channel_id=1, source_target_pairs={{1,0},{2,1},{3,2},{5,4},{6,5},{7,6},{9,8},{10,9},{11,10},{13,12},{... | collective-permute-start | bytes 811016 | tf_op jit(solution)/shard_map/ppermute | solution.py:77
  22.5 11.4 %collective-permute-start.3 = (f32[2,32,4,264]{3,2,1,0:T(4,128)S(1)}, f32[2,32,4,264]{3,2,1,0:T(4,128)S(1)}, u32[]{:S(2)}, u32[]{:S(2)}) collective-permute-start(f32[2,32,4,264]{3,2,1,0:T(4,128)S(1)} %get-tuple-element.13), channel_id=1, source_target_pairs={{0,1},{1,2},{2,3},{4,5},{5,6},{6,7},{8,9},{9,10},{10,11},{12,13},{... | collective-permute-start | bytes 811016 | tf_op jit(solution)/shard_map/ppermute | solution.py:76
  72.7 38.7 %all-to-all-start.1 = ((f32[8,2,128,256]{3,2,1,0:T(8,128)}), f32[8,2,128,256]{3,2,1,0:T(8,128)}, u32[]{:S(2)}, u32[]{:S(2)}) async-start(f32[8,2,128,256]{3,2,1,0:T(8,128)} %bitcast.42), calls=%async_computation.1 | async-start | bytes 4194304 | tf_op jit(solution)/shard_map/all_to_all | solution.py:268
  111.4 32.5 %all-to-all-start = ((f32[8,2,128,256]{3,2,1,0:T(8,128)}), f32[8,2,128,256]{3,2,1,0:T(8,128)S(1)}, u32[]{:S(2)}, u32[]{:S(2)}) async-start(f32[8,2,128,256]{3,2,1,0:T(8,128)} %bitcast.41), calls=%async_computation | async-start | bytes 4194304 | tf_op jit(solution)/shard_map/all_to_all | solution.py:268

commit v12 on v10

--- a/solution.py
+++ b/solution.py
@@ -158,10 +158,13 @@
         first_lane = lane_id == 0
         last_lane = lane_id == 127
 
-        def pieces(ref, z, r):
-            return tuple(ref[z, pl.ds(r, RB), pl.ds(128 * k, 128)] for k in range(npc))
-
-        def step(src, dst, first):
+        def pieces(ref, z, r, count=npc):
+            return tuple(ref[z, pl.ds(r, RB), pl.ds(128 * k, 128)] for k in range(count))
+
+        def step(src, dst, first, last):
+            nk = nacc if last else npc
+            lo_b = acc_lo if last else b_first
+            hi_b = acc_hi - 1 if last else b_last
             def level(z, accumulate):
                 zu = jnp.minimum(z + 1, nz - 1)
                 zl = jnp.maximum(z - 1, 0)
@@ -173,24 +176,24 @@
                     cur = pieces(src, z, r)
                     right = tuple(pltpu.roll(v, 1, 1) for v in cur)
                     left = tuple(pltpu.roll(v, 127, 1) for v in cur)
-                    for k in range(npc):
+                    for k in range(nk):
                         s_buf[pl.ds(r, RB), pl.ds(128 * k, 128)] = jnp.where(
                             first_lane, right[(k - 1) % npc], right[k])
                         n_buf[pl.ds(r, RB), pl.ds(128 * k, 128)] = jnp.where(
                             last_lane, left[(k + 1) % npc], left[k])
                     return c
 
-                lax.fori_loop(b_first, b_last + 1, rot, 0, unroll=True)
+                lax.fori_loop(lo_b, hi_b + 1, rot, 0, unroll=True)
 
                 def blk(b, carry, acc):
                     prev, cur = carry
                     r = pl.multiple_of(b * RB, RB)
-                    nxt = pieces(src, z, r + RB)
-                    up = pieces(src, zu, r)
-                    low = pieces(src, zl, r)
-                    o = pieces(o_buf, z, r)
+                    nxt = pieces(src, z, r + RB, nk)
+                    up = pieces(src, zu, r, nk)
+                    low = pieces(src, zl, r, nk)
+                    o = pieces(o_buf, z, r, nk)
                     ro = pl.multiple_of(r - PAD, RB)
-                    for k in range(npc):
+                    for k in range(nk):
                         c = cur[k]
                         west = jnp.where(first_row, pltpu.roll(prev[k], 1, 0), pltpu.roll(c, 1, 0))
                         east = jnp.where(last_row, pltpu.roll(nxt[k], RB - 1, 0), pltpu.roll(c, RB - 1, 0))
@@ -201,7 +204,8 @@
                             + (k_e * east + k_s * south)
                             + ((k_n * north + ku * up[k]) + diffusion * low[k])
                         )
-                        dst[z, pl.ds(r, RB), pl.ds(128 * k, 128)] = new
+                        if not last:
+                            dst[z, pl.ds(r, RB), pl.ds(128 * k, 128)] = new
                         if acc and k < nacc:
                             sq = new * new
                             if first:
@@ -212,8 +216,10 @@
                                 )
                     return (cur, nxt)
 
-                carry = (pieces(src, z, 0), pieces(src, z, RB))
-                if accumulate:
+                carry = (pieces(src, z, (lo_b - 1) * RB, nk), pieces(src, z, lo_b * RB, nk))
+                if last:
+                    lax.fori_loop(acc_lo, acc_hi, lambda b, c: blk(b, c, accumulate), carry, unroll=True)
+                elif accumulate:
                     carry = lax.fori_loop(b_first, acc_lo, lambda b, c: blk(b, c, False), carry)
                     carry = lax.fori_loop(acc_lo, acc_hi, lambda b, c: blk(b, c, True), carry, unroll=True)
                     carry = lax.fori_loop(acc_hi, b_last + 1, lambda b, c: blk(b, c, False), carry)
@@ -233,7 +239,7 @@
 
         bufs = (a_buf, b_buf)
         for n in range(STEPS):
-            step(bufs[n % 2], bufs[(n + 1) % 2], n == 0)
+            step(bufs[n % 2], bufs[(n + 1) % 2], n == 0, n == STEPS - 1)
 
         def leth(z, c):
             for q in range(nh // 32):

time: 145 us -> 144 us (level)
  Pallas kernels: 67 us -> 65.4 us
    pallas_call x2, Pallas kernels: 67 us -> 65.4 us  [on_device(): pl.pallas_call(make_kernel(nz, nx, ny, RZ, half), out_shape=jax.ShapeDtyp...]
where the time goes in v12:
time: 144 us; the launch traced here: 143 us
  Pallas kernels  65.4 us (45%)
  waiting for transfers between devices  30.6 us (21%)
  starting transfers between devices  24.1 us (17%)
  matrix products  13 us (9%)
  other arithmetic  6.44 us (4%)
  local copies, waits for them, and re-layouts  1.91 us (1%)
  between operations  1.66 us (1%)
    pallas_call x2, Pallas kernels, on_device(): pl.pallas_call(make_kernel(nz, nx, ny, RZ, half), out_shape=jax.ShapeDtyp...  65.4 us
    all_to_all x2, waiting for transfers between devices, _reduce_sync(): return lax.all_to_all(parts, 'scen', 0, 0, tiled=True).sum(0)  25.6 us
    all_to_all x2, starting transfers between devices, _reduce_sync(): return lax.all_to_all(parts, 'scen', 0, 0, tiled=True).sum(0)  10.4 us
    ppermute x1, starting transfers between devices, ghost_pieces(): xlo = lax.ppermute(last_rows, 'gx', fx)  4.92 us
    dot_general x1, matrix products, ghost_pieces(): jnp.einsum('zxy,ky->zkx', (1 - obs).astype(jnp.bfloat16), pick.astype(jnp...  4.59 us
    dot_general x1, matrix products, ghost_pieces(): jnp.einsum('czkr,kj->czrj', jnp.concatenate(_split3(yt), 2), place, prefe...  4.56 us
    ppermute x1, starting transfers between devices, ghost_pieces(): yw = lax.ppermute(ext[:, :, H:], 'gy', fy)  4.19 us
    dot_general x1, matrix products, ghost_pieces(): src_cols = jnp.einsum('zxy,ky->zkx', src, pick, precision=hi)  3.89 us
  transfers between devices with their start and end apart: 6, of which 3 were waited for; matrix products, arithmetic and copies ran while one was open for 8% of the time, Pallas kernels for 23%

profile of v12, /device:TPU:1, one launch (start us, length us, event | category | flops | bytes accessed | tf_op | source)
XLA Modules:
  0.0 143.1 jit_solution(18386905888831823703)
XLA Ops:
  0.0 1.1 convert_bitcast_fusion.1
  1.1 1.3 fusion.13
  2.5 3.3 %collective-permute-start.1 = (f32[2,32,4,256]{3,2,1,0:T(4,128)S(1)}, f32[2,32,4,256]{3,2,1,0:T(4,128)S(1)}, u32[]{:S(2)}, u32[]{:S(2)}) collective-permute-start(f32[2,32,4,256]{3,2,1,0:T(4,128)S(1)} %pad_maximum_fusion.3), channel_id=1, source_target_pairs={{4,0},{8,4},{12,8},{5,1},{9,5},{13,9},{6,2},{10,6},{14,10},{7,3},{... | collective-permute-start | bytes 786440 | tf_op jit(solution)/shard_map/ppermute | solution.py:66
  5.8 4.9 %collective-permute-start = (f32[2,32,4,256]{3,2,1,0:T(4,128)S(1)}, f32[2,32,4,256]{3,2,1,0:T(4,128)S(1)}, u32[]{:S(2)}, u32[]{:S(2)}) collective-permute-start(f32[2,32,4,256]{3,2,1,0:T(4,128)S(1)} %pad_maximum_fusion.2), channel_id=1, source_target_pairs={{0,4},{4,8},{8,12},{1,5},{5,9},{9,13},{2,6},{6,10},{10,14},{3,7},{... | collective-permute-start | bytes 786440 | tf_op jit(solution)/shard_map/ppermute | solution.py:65
  10.8 4.6 %fusion = f32[8,32,256]{2,0,1:T(8,128)S(1)} fusion(s32[32,256,256]{2,1,0:T(8,128)} %obs_hbm.3, s32[8]{0:T(128)} %constant.34.clone), kind=kOutput, calls=%fused_computation.1 | convolution fusion | flops 37754880 | bytes 8650784 | tf_op jit(solution)/shard_map/zxy,ky->zkx/dot_general | solution.py:69
  15.4 3.9 %fusion.9 = f32[1,32,8,256]{3,2,1,0:T(8,128)S(1)} fusion(f32[8,32,256]{2,0,1:T(8,128)S(1)} %fusion, s32[8]{0:T(128)S(1)} %copy-done.3, f32[1,32,256,256]{3,2,1,0:T(8,128)S(1)} %copy-done), kind=kOutput, calls=%fused_computation.13 | convolution fusion | flops 201394176 | bytes 8912928 | tf_op jit(solution)/shard_map/zxy,ky->zkx/dot_general | solution.py:68
  19.6 0.4 copy.16
  20.3 0.4 copy.15
  20.8 0.3 pad_maximum_fusion
  21.2 1.3 collective-permute-start.2
  22.5 4.2 %collective-permute-start.3 = (f32[2,32,4,264]{3,2,1,0:T(4,128)S(1)}, f32[2,32,4,264]{3,2,1,0:T(4,128)S(1)}, u32[]{:S(2)}, u32[]{:S(2)}) collective-permute-start(f32[2,32,4,264]{3,2,1,0:T(4,128)S(1)} %get-tuple-element.13), channel_id=1, source_target_pairs={{0,1},{1,2},{2,3},{4,5},{5,6},{6,7},{8,9},{9,10},{10,11},{12,13},{... | collective-permute-start | bytes 811016 | tf_op jit(solution)/shard_map/ppermute | solution.py:76
  28.2 0.6 stack.55.coef
  28.9 3.3 %collective-permute-done.2 = f32[2,32,4,264]{3,2,1,0:T(4,128)S(1)} collective-permute-done((f32[2,32,4,264]{3,2,1,0:T(4,128)S(1)}, f32[2,32,4,264]{3,2,1,0:T(4,128)S(1)}, u32[]{:S(2)}, u32[]{:S(2)}) %collective-permute-start.2) | collective-permute-done | bytes 270368 | tf_op jit(solution)/shard_map/ppermute | solution.py:77
  32.2 1.8 %collective-permute-done.3 = f32[2,32,4,264]{3,2,1,0:T(4,128)S(1)} collective-permute-done((f32[2,32,4,264]{3,2,1,0:T(4,128)S(1)}, f32[2,32,4,264]{3,2,1,0:T(4,128)S(1)}, u32[]{:S(2)}, u32[]{:S(2)}) %collective-permute-start.3) | collective-permute-done | bytes 270368 | tf_op jit(solution)/shard_map/ppermute | solution.py:76
  34.0 0.5 reduce-precision_convert_fusion.1
  34.5 4.6 %fusion.2.lanes_hbm = f32[2,32,288,128]{3,2,1,0:T(8,128)} fusion(bf16[2,32,8,288]{3,2,1,0:T(8,128)(2,1)S(1)} %get-tuple-element.10, bf16[2,32,8,288]{3,2,1,0:T(8,128)(2,1)S(1)} %get-tuple-element.11, bf16[2,32,8,288]{3,2,1,0:T(8,128)(2,1)S(1)} %get-tuple-element.9, pred[8,128]{1,0:T(8,128)(4,1)S(1)} %iota_compare_fusion.3), kind=kOutput, calls=%fused_computation.5 | convolution fusion | flops 115912704 | bytes 10322944 | tf_op jit(solution)/shard_map/czkr,kj->czrj/dot_general | solution.py:83
  39.0 32.8 %shard_map.65 = f32[16,128,256]{2,1,0:T(8,128)} custom-call(f32[8]{0:T(128)} %stack.55.coef, f32[1,32,256,256]{3,2,1,0:T(8,128)} %src_hbm.3, s32[32,256,256]{2,1,0:T(8,128)} %obs_hbm.3, f32[2,32,4,256]{3,2,1,0:T(4,128)} %copy-done.1, f32[2,32,288,128]{3,2,1,0:T(8,128)} %fusion.2.lanes_hbm), custom_call_target="tpu_custom_call" | custom-call | tf_op jit(solution)/shard_map/pallas_call | solution.py:284
  71.8 5.2 %all-to-all-start.1 = ((f32[8,2,128,256]{3,2,1,0:T(8,128)}), f32[8,2,128,256]{3,2,1,0:T(8,128)}, u32[]{:S(2)}, u32[]{:S(2)}) async-start(f32[8,2,128,256]{3,2,1,0:T(8,128)} %bitcast.42), calls=%async_computation.1 | async-start | bytes 4194304 | tf_op jit(solution)/shard_map/all_to_all | solution.py:260
  77.0 32.6 %shard_map.64 = f32[16,128,256]{2,1,0:T(8,128)} custom-call(f32[8]{0:T(128)} %stack.55.coef, f32[1,32,256,256]{3,2,1,0:T(8,128)} %src_hbm.3, s32[32,256,256]{2,1,0:T(8,128)} %obs_hbm.3, f32[2,32,4,256]{3,2,1,0:T(4,128)} %copy-done.2, f32[2,32,288,128]{3,2,1,0:T(8,128)} %fusion.2.lanes_hbm), custom_call_target="tpu_custom_call" | custom-call | tf_op jit(solution)/shard_map/pallas_call | solution.py:284
  109.7 5.2 %all-to-all-start = ((f32[8,2,128,256]{3,2,1,0:T(8,128)}), f32[8,2,128,256]{3,2,1,0:T(8,128)S(1)}, u32[]{:S(2)}, u32[]{:S(2)}) async-start(f32[8,2,128,256]{3,2,1,0:T(8,128)} %bitcast.41), calls=%async_computation | async-start | bytes 4194304 | tf_op jit(solution)/shard_map/all_to_all | solution.py:260
  114.8 1.8 %reduce_sum.19 = f32[2,128,256]{2,1,0:T(8,128)S(1)} reduce(f32[8,2,128,256]{3,2,1,0:T(8,128)} %all-to-all-done.1, f32[]{:T(128)} %constant.10.clone.1), dimensions={0}, to_apply=%region_1.2 | reduce | flops 458752 | bytes 2359300 | tf_op jit(solution)/shard_map/reduce_sum | solution.py:260
  116.6 25.6 %all-to-all-done = f32[8,2,128,256]{3,2,1,0:T(8,128)S(1)} async-done(((f32[8,2,128,256]{3,2,1,0:T(8,128)}), f32[8,2,128,256]{3,2,1,0:T(8,128)S(1)}, u32[]{:S(2)}, u32[]{:S(2)}) %all-to-all-start) | async-done | bytes 2097184 | tf_op jit(solution)/shard_map/all_to_all | solution.py:260
  142.2 0.1 reduce_sum.18
  142.3 0.8 pad_maximum_fusion.1
  (21 shorter events, 0.9 us)
Async XLA Ops:
  2.5 16.8 %collective-permute-start.1 = (f32[2,32,4,256]{3,2,1,0:T(4,128)S(1)}, f32[2,32,4,256]{3,2,1,0:T(4,128)S(1)}, u32[]{:S(2)}, u32[]{:S(2)}) collective-permute-start(f32[2,32,4,256]{3,2,1,0:T(4,128)S(1)} %pad_maximum_fusion.3), channel_id=1, source_target_pairs={{4,0},{8,4},{12,8},{5,1},{9,5},{13,9},{6,2},{10,6},{14,10},{7,3},{... | collective-permute-start | bytes 786440 | tf_op jit(solution)/shard_map/ppermute | solution.py:66
  5.8 9.5 %copy-start = (f32[1,32,256,256]{3,2,1,0:T(8,128)S(1)}, f32[1,32,256,256]{3,2,1,0:T(8,128)}, u32[]{:S(2)}) copy-start(f32[1,32,256,256]{3,2,1,0:T(8,128)} %src_hbm.3) | copy-start | bytes 25165828
  5.8 9.5 %copy-start.3 = (s32[8]{0:T(128)S(1)}, s32[8]{0:T(128)}, u32[]{:S(2)}) copy-start(s32[8]{0:T(128)} %constant.34.clone) | copy-start | bytes 100
  5.8 14.2 %collective-permute-start = (f32[2,32,4,256]{3,2,1,0:T(4,128)S(1)}, f32[2,32,4,256]{3,2,1,0:T(4,128)S(1)}, u32[]{:S(2)}, u32[]{:S(2)}) collective-permute-start(f32[2,32,4,256]{3,2,1,0:T(4,128)S(1)} %pad_maximum_fusion.2), channel_id=1, source_target_pairs={{0,4},{4,8},{8,12},{1,5},{5,9},{9,13},{2,6},{6,10},{10,14},{3,7},{... | collective-permute-start | bytes 786440 | tf_op jit(solution)/shard_map/ppermute | solution.py:65
  19.3 9.6 %copy-start.4 = (s32[8]{0:T(128)S(1)}, s32[8]{0:T(128)}, u32[]{:S(2)}) copy-start(s32[8]{0:T(128)} %constant.35.clone) | copy-start | bytes 100
  19.3 19.8 %copy-start.1 = (f32[2,32,4,256]{3,2,1,0:T(4,128)}, f32[2,32,4,256]{3,2,1,0:T(4,128)S(1)}, u32[]{:S(2)}) copy-start(f32[2,32,4,256]{3,2,1,0:T(4,128)S(1)} %collective-permute-done.1.ghost_hbm) | copy-start | bytes 786436
  20.0 19.0 %copy-start.2 = (f32[2,32,4,256]{3,2,1,0:T(4,128)}, f32[2,32,4,256]{3,2,1,0:T(4,128)S(1)}, u32[]{:S(2)}) copy-start(f32[2,32,4,256]{3,2,1,0:T(4,128)S(1)} %collective-permute-done.ghost_hbm) | copy-start | bytes 786436
  21.2 11.0 %collective-permute-start.2 = (f32[2,32,4,264]{3,2,1,0:T(4,128)S(1)}, f32[2,32,4,264]{3,2,1,0:T(4,128)S(1)}, u32[]{:S(2)}, u32[]{:S(2)}) collective-permute-start(f32[2,32,4,264]{3,2,1,0:T(4,128)S(1)} %get-tuple-element.12), channel_id=1, source_target_pairs={{1,0},{2,1},{3,2},{5,4},{6,5},{7,6},{9,8},{10,9},{11,10},{13,12},{... | collective-permute-start | bytes 811016 | tf_op jit(solution)/shard_map/ppermute | solution.py:77
  22.5 11.4 %collective-permute-start.3 = (f32[2,32,4,264]{3,2,1,0:T(4,128)S(1)}, f32[2,32,4,264]{3,2,1,0:T(4,128)S(1)}, u32[]{:S(2)}, u32[]{:S(2)}) collective-permute-start(f32[2,32,4,264]{3,2,1,0:T(4,128)S(1)} %get-tuple-element.13), channel_id=1, source_target_pairs={{0,1},{1,2},{2,3},{4,5},{5,6},{6,7},{8,9},{9,10},{10,11},{12,13},{... | collective-permute-start | bytes 811016 | tf_op jit(solution)/shard_map/ppermute | solution.py:76
  71.8 37.8 %all-to-all-start.1 = ((f32[8,2,128,256]{3,2,1,0:T(8,128)}), f32[8,2,128,256]{3,2,1,0:T(8,128)}, u32[]{:S(2)}, u32[]{:S(2)}) async-start(f32[8,2,128,256]{3,2,1,0:T(8,128)} %bitcast.42), calls=%async_computation.1 | async-start | bytes 4194304 | tf_op jit(solution)/shard_map/all_to_all | solution.py:260
  109.7 32.5 %all-to-all-start = ((f32[8,2,128,256]{3,2,1,0:T(8,128)}), f32[8,2,128,256]{3,2,1,0:T(8,128)S(1)}, u32[]{:S(2)}, u32[]{:S(2)}) async-start(f32[8,2,128,256]{3,2,1,0:T(8,128)} %bitcast.41), calls=%async_computation | async-start | bytes 4194304 | tf_op jit(solution)/shard_map/all_to_all | solution.py:260

commit v13 on v12

--- a/solution.py
+++ b/solution.py
@@ -204,7 +204,7 @@
                             + (k_e * east + k_s * south)
                             + ((k_n * north + ku * up[k]) + diffusion * low[k])
                         )
-                        if not last:
+                        if not (last and acc):
                             dst[z, pl.ds(r, RB), pl.ds(128 * k, 128)] = new
                         if acc and k < nacc:
                             sq = new * new

time: 144 us -> 144 us (level)
  no operation moved by 1% of the time
where the time goes in v13:
time: 144 us; the launch traced here: 143 us
  Pallas kernels  65.6 us (46%)
  waiting for transfers between devices  30.6 us (21%)
  starting transfers between devices  24.1 us (17%)
  matrix products  13 us (9%)
  other arithmetic  6.44 us (4%)
  local copies, waits for them, and re-layouts  1.91 us (1%)
  between operations  1.66 us (1%)
    pallas_call x2, Pallas kernels, on_device(): pl.pallas_call(make_kernel(nz, nx, ny, RZ, half), out_shape=jax.ShapeDtyp...  65.6 us
    all_to_all x2, waiting for transfers between devices, _reduce_sync(): return lax.all_to_all(parts, 'scen', 0, 0, tiled=True).sum(0)  25.6 us
    all_to_all x2, starting transfers between devices, _reduce_sync(): return lax.all_to_all(parts, 'scen', 0, 0, tiled=True).sum(0)  10.4 us
    ppermute x1, starting transfers between devices, ghost_pieces(): xlo = lax.ppermute(last_rows, 'gx', fx)  4.92 us
    dot_general x1, matrix products, ghost_pieces(): jnp.einsum('zxy,ky->zkx', (1 - obs).astype(jnp.bfloat16), pick.astype(jnp...  4.59 us
    dot_general x1, matrix products, ghost_pieces(): jnp.einsum('czkr,kj->czrj', jnp.concatenate(_split3(yt), 2), place, prefe...  4.56 us
    ppermute x1, starting transfers between devices, ghost_pieces(): yw = lax.ppermute(ext[:, :, H:], 'gy', fy)  4.19 us
    dot_general x1, matrix products, ghost_pieces(): src_cols = jnp.einsum('zxy,ky->zkx', src, pick, precision=hi)  3.89 us
  transfers between devices with their start and end apart: 6, of which 3 were waited for; matrix products, arithmetic and copies ran while one was open for 8% of the time, Pallas kernels for 23%

profile of v13, /device:TPU:1, one launch (start us, length us, event | category | flops | bytes accessed | tf_op | source)
XLA Modules:
  0.0 143.3 jit_solution(772883927104835595)
XLA Ops:
  0.0 1.1 convert_bitcast_fusion.1
  1.1 1.3 fusion.13
  2.5 3.3 %collective-permute-start.1 = (f32[2,32,4,256]{3,2,1,0:T(4,128)S(1)}, f32[2,32,4,256]{3,2,1,0:T(4,128)S(1)}, u32[]{:S(2)}, u32[]{:S(2)}) collective-permute-start(f32[2,32,4,256]{3,2,1,0:T(4,128)S(1)} %pad_maximum_fusion.3), channel_id=1, source_target_pairs={{4,0},{8,4},{12,8},{5,1},{9,5},{13,9},{6,2},{10,6},{14,10},{7,3},{... | collective-permute-start | bytes 786440 | tf_op jit(solution)/shard_map/ppermute | solution.py:66
  5.8 4.9 %collective-permute-start = (f32[2,32,4,256]{3,2,1,0:T(4,128)S(1)}, f32[2,32,4,256]{3,2,1,0:T(4,128)S(1)}, u32[]{:S(2)}, u32[]{:S(2)}) collective-permute-start(f32[2,32,4,256]{3,2,1,0:T(4,128)S(1)} %pad_maximum_fusion.2), channel_id=1, source_target_pairs={{0,4},{4,8},{8,12},{1,5},{5,9},{9,13},{2,6},{6,10},{10,14},{3,7},{... | collective-permute-start | bytes 786440 | tf_op jit(solution)/shard_map/ppermute | solution.py:65
  10.8 4.6 %fusion = f32[8,32,256]{2,0,1:T(8,128)S(1)} fusion(s32[32,256,256]{2,1,0:T(8,128)} %obs_hbm.3, s32[8]{0:T(128)} %constant.34.clone), kind=kOutput, calls=%fused_computation.1 | convolution fusion | flops 37754880 | bytes 8650784 | tf_op jit(solution)/shard_map/zxy,ky->zkx/dot_general | solution.py:69
  15.4 3.9 %fusion.9 = f32[1,32,8,256]{3,2,1,0:T(8,128)S(1)} fusion(f32[8,32,256]{2,0,1:T(8,128)S(1)} %fusion, s32[8]{0:T(128)S(1)} %copy-done.3, f32[1,32,256,256]{3,2,1,0:T(8,128)S(1)} %copy-done), kind=kOutput, calls=%fused_computation.13 | convolution fusion | flops 201394176 | bytes 8912928 | tf_op jit(solution)/shard_map/zxy,ky->zkx/dot_general | solution.py:68
  19.6 0.4 copy.16
  20.3 0.4 copy.15
  20.8 0.3 pad_maximum_fusion
  21.2 1.3 collective-permute-start.2
  22.5 4.2 %collective-permute-start.3 = (f32[2,32,4,264]{3,2,1,0:T(4,128)S(1)}, f32[2,32,4,264]{3,2,1,0:T(4,128)S(1)}, u32[]{:S(2)}, u32[]{:S(2)}) collective-permute-start(f32[2,32,4,264]{3,2,1,0:T(4,128)S(1)} %get-tuple-element.13), channel_id=1, source_target_pairs={{0,1},{1,2},{2,3},{4,5},{5,6},{6,7},{8,9},{9,10},{10,11},{12,13},{... | collective-permute-start | bytes 811016 | tf_op jit(solution)/shard_map/ppermute | solution.py:76
  28.2 0.6 stack.55.coef
  28.9 3.3 %collective-permute-done.2 = f32[2,32,4,264]{3,2,1,0:T(4,128)S(1)} collective-permute-done((f32[2,32,4,264]{3,2,1,0:T(4,128)S(1)}, f32[2,32,4,264]{3,2,1,0:T(4,128)S(1)}, u32[]{:S(2)}, u32[]{:S(2)}) %collective-permute-start.2) | collective-permute-done | bytes 270368 | tf_op jit(solution)/shard_map/ppermute | solution.py:77
  32.2 1.8 %collective-permute-done.3 = f32[2,32,4,264]{3,2,1,0:T(4,128)S(1)} collective-permute-done((f32[2,32,4,264]{3,2,1,0:T(4,128)S(1)}, f32[2,32,4,264]{3,2,1,0:T(4,128)S(1)}, u32[]{:S(2)}, u32[]{:S(2)}) %collective-permute-start.3) | collective-permute-done | bytes 270368 | tf_op jit(solution)/shard_map/ppermute | solution.py:76
  34.0 0.5 reduce-precision_convert_fusion.1
  34.5 4.6 %fusion.2.lanes_hbm = f32[2,32,288,128]{3,2,1,0:T(8,128)} fusion(bf16[2,32,8,288]{3,2,1,0:T(8,128)(2,1)S(1)} %get-tuple-element.10, bf16[2,32,8,288]{3,2,1,0:T(8,128)(2,1)S(1)} %get-tuple-element.11, bf16[2,32,8,288]{3,2,1,0:T(8,128)(2,1)S(1)} %get-tuple-element.9, pred[8,128]{1,0:T(8,128)(4,1)S(1)} %iota_compare_fusion.3), kind=kOutput, calls=%fused_computation.5 | convolution fusion | flops 115912704 | bytes 10322944 | tf_op jit(solution)/shard_map/czkr,kj->czrj/dot_general | solution.py:83
  39.0 32.9 %shard_map.65 = f32[16,128,256]{2,1,0:T(8,128)} custom-call(f32[8]{0:T(128)} %stack.55.coef, f32[1,32,256,256]{3,2,1,0:T(8,128)} %src_hbm.3, s32[32,256,256]{2,1,0:T(8,128)} %obs_hbm.3, f32[2,32,4,256]{3,2,1,0:T(4,128)} %copy-done.1, f32[2,32,288,128]{3,2,1,0:T(8,128)} %fusion.2.lanes_hbm), custom_call_target="tpu_custom_call" | custom-call | tf_op jit(solution)/shard_map/pallas_call | solution.py:284
  71.9 5.2 %all-to-all-start.1 = ((f32[8,2,128,256]{3,2,1,0:T(8,128)}), f32[8,2,128,256]{3,2,1,0:T(8,128)}, u32[]{:S(2)}, u32[]{:S(2)}) async-start(f32[8,2,128,256]{3,2,1,0:T(8,128)} %bitcast.42), calls=%async_computation.1 | async-start | bytes 4194304 | tf_op jit(solution)/shard_map/all_to_all | solution.py:260
  77.1 32.7 %shard_map.64 = f32[16,128,256]{2,1,0:T(8,128)} custom-call(f32[8]{0:T(128)} %stack.55.coef, f32[1,32,256,256]{3,2,1,0:T(8,128)} %src_hbm.3, s32[32,256,256]{2,1,0:T(8,128)} %obs_hbm.3, f32[2,32,4,256]{3,2,1,0:T(4,128)} %copy-done.2, f32[2,32,288,128]{3,2,1,0:T(8,128)} %fusion.2.lanes_hbm), custom_call_target="tpu_custom_call" | custom-call | tf_op jit(solution)/shard_map/pallas_call | solution.py:284
  109.9 5.2 %all-to-all-start = ((f32[8,2,128,256]{3,2,1,0:T(8,128)}), f32[8,2,128,256]{3,2,1,0:T(8,128)S(1)}, u32[]{:S(2)}, u32[]{:S(2)}) async-start(f32[8,2,128,256]{3,2,1,0:T(8,128)} %bitcast.41), calls=%async_computation | async-start | bytes 4194304 | tf_op jit(solution)/shard_map/all_to_all | solution.py:260
  115.0 1.8 %reduce_sum.19 = f32[2,128,256]{2,1,0:T(8,128)S(1)} reduce(f32[8,2,128,256]{3,2,1,0:T(8,128)} %all-to-all-done.1, f32[]{:T(128)} %constant.10.clone.1), dimensions={0}, to_apply=%region_1.2 | reduce | flops 458752 | bytes 2359300 | tf_op jit(solution)/shard_map/reduce_sum | solution.py:260
  116.8 25.6 %all-to-all-done = f32[8,2,128,256]{3,2,1,0:T(8,128)S(1)} async-done(((f32[8,2,128,256]{3,2,1,0:T(8,128)}), f32[8,2,128,256]{3,2,1,0:T(8,128)S(1)}, u32[]{:S(2)}, u32[]{:S(2)}) %all-to-all-start) | async-done | bytes 2097184 | tf_op jit(solution)/shard_map/all_to_all | solution.py:260
  142.4 0.1 reduce_sum.18
  142.5 0.8 pad_maximum_fusion.1
  (21 shorter events, 0.9 us)
Async XLA Ops:
  2.5 16.8 %collective-permute-start.1 = (f32[2,32,4,256]{3,2,1,0:T(4,128)S(1)}, f32[2,32,4,256]{3,2,1,0:T(4,128)S(1)}, u32[]{:S(2)}, u32[]{:S(2)}) collective-permute-start(f32[2,32,4,256]{3,2,1,0:T(4,128)S(1)} %pad_maximum_fusion.3), channel_id=1, source_target_pairs={{4,0},{8,4},{12,8},{5,1},{9,5},{13,9},{6,2},{10,6},{14,10},{7,3},{... | collective-permute-start | bytes 786440 | tf_op jit(solution)/shard_map/ppermute | solution.py:66
  5.8 9.5 %copy-start = (f32[1,32,256,256]{3,2,1,0:T(8,128)S(1)}, f32[1,32,256,256]{3,2,1,0:T(8,128)}, u32[]{:S(2)}) copy-start(f32[1,32,256,256]{3,2,1,0:T(8,128)} %src_hbm.3) | copy-start | bytes 25165828
  5.8 9.5 %copy-start.3 = (s32[8]{0:T(128)S(1)}, s32[8]{0:T(128)}, u32[]{:S(2)}) copy-start(s32[8]{0:T(128)} %constant.34.clone) | copy-start | bytes 100
  5.8 14.2 %collective-permute-start = (f32[2,32,4,256]{3,2,1,0:T(4,128)S(1)}, f32[2,32,4,256]{3,2,1,0:T(4,128)S(1)}, u32[]{:S(2)}, u32[]{:S(2)}) collective-permute-start(f32[2,32,4,256]{3,2,1,0:T(4,128)S(1)} %pad_maximum_fusion.2), channel_id=1, source_target_pairs={{0,4},{4,8},{8,12},{1,5},{5,9},{9,13},{2,6},{6,10},{10,14},{3,7},{... | collective-permute-start | bytes 786440 | tf_op jit(solution)/shard_map/ppermute | solution.py:65
  19.3 9.6 %copy-start.4 = (s32[8]{0:T(128)S(1)}, s32[8]{0:T(128)}, u32[]{:S(2)}) copy-start(s32[8]{0:T(128)} %constant.35.clone) | copy-start | bytes 100
  19.3 19.8 %copy-start.1 = (f32[2,32,4,256]{3,2,1,0:T(4,128)}, f32[2,32,4,256]{3,2,1,0:T(4,128)S(1)}, u32[]{:S(2)}) copy-start(f32[2,32,4,256]{3,2,1,0:T(4,128)S(1)} %collective-permute-done.1.ghost_hbm) | copy-start | bytes 786436
  20.0 19.0 %copy-start.2 = (f32[2,32,4,256]{3,2,1,0:T(4,128)}, f32[2,32,4,256]{3,2,1,0:T(4,128)S(1)}, u32[]{:S(2)}) copy-start(f32[2,32,4,256]{3,2,1,0:T(4,128)S(1)} %collective-permute-done.ghost_hbm) | copy-start | bytes 786436
  21.2 11.0 %collective-permute-start.2 = (f32[2,32,4,264]{3,2,1,0:T(4,128)S(1)}, f32[2,32,4,264]{3,2,1,0:T(4,128)S(1)}, u32[]{:S(2)}, u32[]{:S(2)}) collective-permute-start(f32[2,32,4,264]{3,2,1,0:T(4,128)S(1)} %get-tuple-element.12), channel_id=1, source_target_pairs={{1,0},{2,1},{3,2},{5,4},{6,5},{7,6},{9,8},{10,9},{11,10},{13,12},{... | collective-permute-start | bytes 811016 | tf_op jit(solution)/shard_map/ppermute | solution.py:77
  22.5 11.4 %collective-permute-start.3 = (f32[2,32,4,264]{3,2,1,0:T(4,128)S(1)}, f32[2,32,4,264]{3,2,1,0:T(4,128)S(1)}, u32[]{:S(2)}, u32[]{:S(2)}) collective-permute-start(f32[2,32,4,264]{3,2,1,0:T(4,128)S(1)} %get-tuple-element.13), channel_id=1, source_target_pairs={{0,1},{1,2},{2,3},{4,5},{5,6},{6,7},{8,9},{9,10},{10,11},{12,13},{... | collective-permute-start | bytes 811016 | tf_op jit(solution)/shard_map/ppermute | solution.py:76
  71.9 37.9 %all-to-all-start.1 = ((f32[8,2,128,256]{3,2,1,0:T(8,128)}), f32[8,2,128,256]{3,2,1,0:T(8,128)}, u32[]{:S(2)}, u32[]{:S(2)}) async-start(f32[8,2,128,256]{3,2,1,0:T(8,128)} %bitcast.42), calls=%async_computation.1 | async-start | bytes 4194304 | tf_op jit(solution)/shard_map/all_to_all | solution.py:260
  109.9 32.5 %all-to-all-start = ((f32[8,2,128,256]{3,2,1,0:T(8,128)}), f32[8,2,128,256]{3,2,1,0:T(8,128)S(1)}, u32[]{:S(2)}, u32[]{:S(2)}) async-start(f32[8,2,128,256]{3,2,1,0:T(8,128)} %bitcast.41), calls=%async_computation | async-start | bytes 4194304 | tf_op jit(solution)/shard_map/all_to_all | solution.py:260
